TPU v7x, 128 devices: a whole 4x4x4 slice. The times are simulated.
128 devices in a mesh: tm: 32 (over x, z, core), sub: 4 (over y).
Axes of the slice: x: 4, y: 4, z: 4, core: 2. Of those that a mesh axis runs over, the one named last changes fastest.
Arguments:
- vis_coords: float32 [16384, 2, 1024], P(('tm', 'sub')), may hold values from 0 to 31
- vis_values: float32 [16384, 2, 1024], P(('tm', 'sub')), may hold values from -1.6 to 1.6
- block_dest: int32 [16384, 1], P(('tm', 'sub')), may hold values from 0 to 127; in each aligned block of 128 rows (0 to 127, 128 to 255, ...) at most 2 rows name the same one
- block_local: int32 [16384], P(('tm', 'sub')), may hold values from 0 to 15
- block_tile: int32 [16384], P(('tm', 'sub')), may hold values from 0 to 63
- block_counts: int32 [128], P(('tm', 'sub')), may hold values from 64 to 128, as said below
- facet_offsets: int32 [32, 2], replicated, may hold values from 0 to 384
- correction: float32 [32, 128, 128], P('tm', 'sub'), may hold values from 0.2 to 2
Outputs:
- facets: float32 [32, 128, 2, 128], P('tm', 'sub')
Inputs may be any that keep to these rules, and one draw needn't show every extreme that they name: `block_dest`: among the 128 blocks of one device at most 2 name the same destination, a bound that some device reaches. `block_counts`: some device's count is 128.
All inputs are finite; a program needn't handle non-finite values.
Results may differ from a plain program's by a relative error of at most 0.000096.
Values sent between devices are 32-bit elements; how exact they have to be, the bound alone decides.
No kernel may reach another device: no remote copies, remote signals or barrier semaphores. Data moves between devices by JAX's collectives and lax.ppermute only.
A program may use at most 128 MiB of HBM per device.

v0:
```python
import math

import jax
import jax.numpy as jnp
from jax import lax
from jax.experimental import pallas as pl
from jax.sharding import PartitionSpec as P

SG = 512
PATCH = 32
FS = 128
VIS = 1024
SG_PER = 16


kernel_width = 0.7


def patch_kernel(coords_ref, values_ref, phase_ref, out_ref):
    cells = lax.broadcasted_iota(jnp.int32, (PATCH, 1), 0).astype(jnp.float32)

    def one_block(i, carry):
        x = coords_ref[i, 0:1, :]
        y = coords_ref[i, 1:2, :]
        rows_kernel = jnp.exp(-0.5 * ((x - cells) / kernel_width) ** 2)
        cols_kernel = jnp.exp(-0.5 * ((y - cells) / kernel_width) ** 2)
        v_re = values_ref[i, 0:1, :]
        v_im = values_ref[i, 1:2, :]
        cos_b = phase_ref[i, 0]
        sin_b = phase_ref[i, 1]
        w_re = cols_kernel * (v_re * cos_b + v_im * sin_b)
        w_im = cols_kernel * (v_im * cos_b - v_re * sin_b)
        weighted = jnp.concatenate([w_re, w_im], axis=0)
        out_ref[i] = lax.dot_general(
            rows_kernel,
            weighted,
            (((1,), (1,)), ((), ())),
            precision=lax.Precision.HIGHEST,
            preferred_element_type=jnp.float32,
        )
        return carry

    lax.fori_loop(0, out_ref.shape[0], one_block, 0)


def make_phased_patches(vis_coords, vis_values, live, local):
    count = vis_coords.shape[0]
    step = 8
    phase = (jnp.arange(PATCH, dtype=jnp.int32)[None, :] * local[:, None]) % SG_PER
    angle = phase.astype(jnp.float32) * (2.0 * math.pi / SG_PER)
    keep = live.astype(jnp.float32)[:, None]
    phases = jnp.stack([jnp.cos(angle) * keep, jnp.sin(angle) * keep], axis=1)[..., None]
    spec = pl.BlockSpec((step, 2, VIS), lambda i: (i, 0, 0))
    patch = pl.pallas_call(
        patch_kernel,
        grid=(count // step,),
        in_specs=[spec, spec, pl.BlockSpec((step, 2, PATCH, 1), lambda i: (i, 0, 0, 0))],
        out_specs=pl.BlockSpec((step, PATCH, 2 * PATCH), lambda i: (i, 0, 0)),
        out_shape=jax.ShapeDtypeStruct((count, PATCH, 2 * PATCH), jnp.float32),
        cost_estimate=pl.CostEstimate(
            flops=count * PATCH * 2 * PATCH * VIS * 2,
            transcendentals=count * 2 * PATCH * VIS,
            bytes_accessed=count * (4 * VIS + 2 * PATCH * PATCH) * 4,
        ),
    )(vis_coords, vis_values, phases)
    return patch.reshape(count, 2 * PATCH * PATCH)


def column_table():
    index = jnp.arange(SG, dtype=jnp.int32)
    phase = index[:, None] * index[None, :] % SG
    angle = phase.astype(jnp.float32) * (2.0 * math.pi / SG)
    scale = 1.0 / math.sqrt(SG)
    cosine = jnp.cos(angle) * scale
    sine = jnp.sin(angle) * scale
    return jnp.concatenate(
        [jnp.concatenate([cosine, -sine], 1), jnp.concatenate([sine, cosine], 1)], 0
    )


def body(
    vis_coords,
    vis_values,
    block_dest,
    block_local,
    block_tile,
    block_counts,
    facet_offsets,
    correction,
):
    n_tm = lax.axis_size("tm")
    n_sub = lax.axis_size("sub")
    devices = n_tm * n_sub
    blocks = vis_coords.shape[0]
    band_rows = SG // n_sub
    band_tiles = band_rows // PATCH
    col_tiles = SG // PATCH
    tiles_all = col_tiles * col_tiles
    chunk = SG // devices
    facet_rows = FS // n_sub

    live = jnp.arange(blocks, dtype=jnp.int32) < block_counts[0]
    patches = make_phased_patches(vis_coords, vis_values, live, block_local)

    target = block_dest[:, 0]
    row_tile = (target % n_sub) * band_tiles + block_tile // col_tiles
    tile_id = row_tile * col_tiles + block_tile % col_tiles
    placer = (
        tile_id[None, :] == jnp.arange(tiles_all, dtype=jnp.int32)[:, None]
    ).astype(jnp.float32)
    tiles = jnp.dot(placer, patches, precision=lax.Precision.HIGHEST)
    per_tile_row = PATCH // chunk
    outgoing = (
        tiles.reshape(col_tiles, col_tiles, per_tile_row, chunk, 2, PATCH)
        .transpose(0, 2, 3, 4, 1, 5)
        .reshape(devices, chunk, 2, SG)
    )
    arrived = lax.all_to_all(
        outgoing, ("tm", "sub"), split_axis=0, concat_axis=0, tiled=True
    )
    grid_rows = jnp.sum(arrived, axis=0).reshape(chunk, 2 * SG)
    spectrum = jnp.dot(grid_rows, column_table(), precision=lax.Precision.HIGHEST).reshape(
        chunk, 2, SG
    )

    offsets = jnp.clip(facet_offsets, 0, SG - FS)
    windows = jax.vmap(lambda start: lax.dynamic_slice_in_dim(spectrum, start, FS, 2))(
        offsets[:, 1]
    )
    windows = jnp.broadcast_to(
        windows[:, None], (n_tm, n_sub, chunk, 2, FS)
    ).reshape(devices, chunk, 2, FS)
    gathered = lax.all_to_all(
        windows, ("tm", "sub"), split_axis=0, concat_axis=0, tiled=True
    ).reshape(SG, 2, FS)

    facet = lax.axis_index("tm")
    band = lax.axis_index("sub")
    first_y = offsets[facet, 0] + band * facet_rows
    ys = first_y + jnp.arange(facet_rows, dtype=jnp.int32)
    rs = jnp.arange(SG, dtype=jnp.int32)
    angle = ((ys[:, None] * rs[None, :]) % SG).astype(jnp.float32) * (2.0 * math.pi / SG)
    scale = 1.0 / math.sqrt(SG)
    left = jnp.concatenate([jnp.cos(angle) * scale, jnp.sin(angle) * scale], 1)
    real_part = gathered[:, 0]
    imag_part = gathered[:, 1]
    right = jnp.concatenate(
        [
            jnp.concatenate([real_part, imag_part], 1),
            jnp.concatenate([imag_part, -real_part], 1),
        ],
        0,
    )
    summed = jnp.dot(left, right, precision=lax.Precision.HIGHEST).reshape(
        1, facet_rows, 2, FS
    )
    return summed * correction[:, :, None, :]


def solution(mesh):
    in_specs = (
        P(("tm", "sub"), None, None),
        P(("tm", "sub"), None, None),
        P(("tm", "sub"), None),
        P(("tm", "sub")),
        P(("tm", "sub")),
        P(("tm", "sub")),
        P(),
        P("tm", "sub", None),
    )
    out_specs = P("tm", "sub", None, None)
    return jax.shard_map(body, mesh=mesh, in_specs=in_specs, out_specs=out_specs, check_vma=False)
```

profile of v0, /device:TPU:1, one launch (start us, length us, event | category | flops | bytes accessed | tf_op | source)
XLA Modules:
  0.0 160.0 jit_solution(16142797065752575775)
XLA Ops:
  0.7 0.7 cosine_multiply_fusion.2
  1.4 4.4 %copy.13.phase_ref = f32[128,2,32,1]{3,2,1,0:T(8,128)} copy(f32[128,2,32,1]{0,2,3,1:T(8,128)S(1)} %maximum_bitcast_fusion) | data formatting | bytes 65536 | tf_op jit(solution)/shard_map/broadcast_in_dim | solution.py:52
  5.9 0.0 copy-start.2
  5.9 0.0 copy-start.3
  5.9 55.9 %shard_map.82 = f32[128,32,64]{2,1,0:T(8,128)} custom-call(f32[128,2,1024]{2,1,0:T(2,128)} %coords_ref.1, f32[128,2,1024]{2,1,0:T(2,128)} %values_ref.1, f32[128,2,32,1]{3,2,1,0:T(8,128)} %copy.13.phase_ref), custom_call_target="tpu_custom_call" | custom-call | flops 536870912 | bytes 3145728 | tf_op jit(solution)/shard_map/pallas_call | solution.py:54
  61.7 2.7 %copy.14 = f32[128,32,64]{0,2,1:T(8,128)S(1)} copy(f32[128,32,64]{2,1,0:T(8,128)} %shard_map.82) | data formatting | bytes 2097152 | tf_op jit(solution)/shard_map/pallas_call | solution.py:54
  64.4 0.0 copy-done.2
  64.4 0.0 copy-done.3
  64.4 5.7 %convolution_bitcast_fusion = f32[16,8,4,2,16,32]{5,4,3,2,1,0:T(8,128)} fusion(f32[8,4,2,32,128,1]{4,3,2,1,0,5:T(8,128)S(1)} %bitcast.41, s32[16,16]{1,0:T(8,128)S(1)} %multiply_add_fusion, s32[128]{0:T(128)S(1)} %fusion.34), kind=kOutput, calls=%fused_computation.2 | convolution fusion | flops 805339136 | bytes 3147264 | tf_op jit(solution)/shard_map/dot_general | solution.py:111
  70.1 7.8 %reshape.200 = f32[128,4,2,512]{3,2,1,0:T(2,128)} reshape(f32[16,8,4,2,16,32]{5,4,3,2,1,0:T(8,128)} %convolution_bitcast_fusion) | data formatting | bytes 4194304 | tf_op jit(solution)/shard_map/reshape | solution.py:116
  78.0 11.7 %all-to-all-start = ((f32[128,4,2,512]{3,2,1,0:T(2,128)}), f32[128,4,2,512]{3,2,1,0:T(2,128)S(1)}, u32[]{:S(2)}, u32[]{:S(2)}) async-start(f32[128,4,2,512]{3,2,1,0:T(2,128)} %reshape.200), calls=%async_computation | async-start | bytes 4194304 | tf_op jit(solution)/shard_map/all_to_all | solution.py:118
  89.6 3.9 %fusion.14 = f32[512,512]{0,1:T(8,128)S(1)} fusion(), kind=kLoop, calls=%fused_computation.22 | loop fusion | flops 4194304 | bytes 1048576 | tf_op jit(solution)/shard_map/neg | solution.py:77
  93.5 4.2 %sine_multiply_fusion = (f32[512,512]{0,1:T(8,128)S(1)}, f32[512,512]{0,1:T(8,128)S(1)}) fusion(), kind=kLoop, calls=%fused_computation.17 | loop fusion | flops 4194304 | bytes 2097152 | tf_op jit(solution)/shard_map/mul | solution.py:75
  97.7 0.0 copy-start.1
  97.7 2.3 %maximum_maximum_fusion = f32[1024,1024]{0,1:T(8,128)} fusion(f32[512,512]{0,1:T(8,128)S(1)} %get-tuple-element.12, f32[512,512]{0,1:T(8,128)S(1)} %get-tuple-element.11, f32[512,512]{0,1:T(8,128)S(1)} %fusion.14), kind=kLoop, calls=%fused_computation.1 | loop fusion | flops 3145728 | bytes 7340032 | tf_op jit(solution)/shard_map/concatenate | solution.py:76
  100.0 0.0 copy-done.1
  100.0 20.4 %all-to-all-done = f32[128,4,2,512]{3,2,1,0:T(2,128)S(1)} async-done(((f32[128,4,2,512]{3,2,1,0:T(2,128)}), f32[128,4,2,512]{3,2,1,0:T(2,128)S(1)}, u32[]{:S(2)}, u32[]{:S(2)}) %all-to-all-start) | async-done | bytes 2097184 | tf_op jit(solution)/shard_map/all_to_all | solution.py:118
  120.4 0.7 reduce_sum.9
  121.2 5.9 %fusion.43 = f32[4,2,512]{2,0,1:T(4,128)S(1)} fusion(f32[4,1024,1]{1,0,2:T(4,128)S(1)} %reshape.213, f32[2,512,1024]{2,1,0:T(8,128)} %bitcast.40), kind=kOutput, calls=%fused_computation.77 | convolution fusion | flops 50331648 | bytes 4227072 | tf_op jit(solution)/shard_map/dot_general | solution.py:122
  127.0 0.3 copy.15
  127.3 6.9 %gather_fusion = f32[32,4,2,128]{1,2,3,0:T(2,128)} fusion(f32[4,2,512]{0,1,2:T(2,128)S(1)} %copy.15, s32[32]{0:T(128)S(1)} %fusion.40), kind=kCustom, calls=%fused_computation | custom fusion | bytes 262528 | tf_op jit(solution)/shard_map/vmap()/gather | solution.py:127
  134.2 0.0 copy-start
  134.2 5.3 %copy.16 = f32[32,4,2,128]{3,2,1,0:T(2,128)S(1)} copy(f32[32,4,2,128]{1,2,3,0:T(2,128)} %gather_fusion) | data formatting | bytes 262144 | tf_op jit(solution)/shard_map/vmap()/gather | solution.py:127
  139.5 0.9 broadcast_in_dim.5
  140.4 3.6 %all-to-all-start.1 = ((f32[128,4,2,128]{3,2,1,0:T(2,128)}), f32[128,4,2,128]{3,2,1,0:T(2,128)S(1)}, u32[]{:S(2)}, u32[]{:S(2)}) async-start(f32[128,4,2,128]{3,2,1,0:T(2,128)} %bitcast.14), calls=%async_computation.1 | async-start | bytes 1048576 | tf_op jit(solution)/shard_map/all_to_all | solution.py:133
  144.1 0.6 constant_dynamic-slice_fusion
  145.3 0.3 cosine_multiply_fusion.1
  145.7 12.7 %all-to-all-done.1 = f32[128,4,2,128]{3,2,1,0:T(2,128)S(1)} async-done(((f32[128,4,2,128]{3,2,1,0:T(2,128)}), f32[128,4,2,128]{3,2,1,0:T(2,128)S(1)}, u32[]{:S(2)}, u32[]{:S(2)}) %all-to-all-start.1) | async-done | bytes 524320 | tf_op jit(solution)/shard_map/all_to_all | solution.py:133
  158.3 0.4 fusion.42
  158.8 0.6 fusion.3
  159.4 0.0 copy-done
  159.4 0.6 broadcast_multiply_fusion
  (10 shorter events, 0.1 us)
Async XLA Ops:
  5.9 58.5 %copy-start.2 = (s32[128,1]{0,1:T(1,128)S(1)}, s32[128,1]{0,1:T(1,128)}, u32[]{:S(2)}) copy-start(s32[128,1]{0,1:T(1,128)} %param.10) | copy-start | bytes 1540
  5.9 58.5 %copy-start.3 = (s32[128]{0:T(128)S(1)}, s32[128]{0:T(128)}, u32[]{:S(2)}) copy-start(s32[128]{0:T(128)} %param.12) | copy-start | bytes 1540
  78.0 42.5 %all-to-all-start = ((f32[128,4,2,512]{3,2,1,0:T(2,128)}), f32[128,4,2,512]{3,2,1,0:T(2,128)S(1)}, u32[]{:S(2)}, u32[]{:S(2)}) async-start(f32[128,4,2,512]{3,2,1,0:T(2,128)} %reshape.200), calls=%async_computation | async-start | bytes 4194304 | tf_op jit(solution)/shard_map/all_to_all | solution.py:118
  97.7 2.4 %copy-start.1 = (s32[32,2]{0,1:T(2,128)S(1)}, s32[32,2]{0,1:T(2,128)}, u32[]{:S(2)}) copy-start(s32[32,2]{0,1:T(2,128)} %param.14) | copy-start | bytes 772
  134.2 25.2 %copy-start = (f32[1,32,128]{2,1,0:T(8,128)S(1)}, f32[1,32,128]{2,1,0:T(8,128)}, u32[]{:S(2)}) copy-start(f32[1,32,128]{2,1,0:T(8,128)} %param.15) | copy-start | bytes 49156
  140.4 17.9 %all-to-all-start.1 = ((f32[128,4,2,128]{3,2,1,0:T(2,128)}), f32[128,4,2,128]{3,2,1,0:T(2,128)S(1)}, u32[]{:S(2)}, u32[]{:S(2)}) async-start(f32[128,4,2,128]{3,2,1,0:T(2,128)} %bitcast.14), calls=%async_computation.1 | async-start | bytes 1048576 | tf_op jit(solution)/shard_map/all_to_all | solution.py:133
where the time goes:
time: 161 us; the launch traced here: 160 us
  Pallas kernels  55.9 us (35%)
  waiting for transfers between devices  33.1 us (21%)
  local copies, waits for them, and re-layouts  29.4 us (18%)
  starting transfers between devices  15.3 us (10%)
  other arithmetic  12.9 us (8%)
  matrix products  12.1 us (8%)
    pallas_call x1, Pallas kernels, make_phased_patches(): pl.pallas_call(patch_kernel, grid=(count // step,), in_specs=[spec, spec,...  55.9 us
    all_to_all x1, waiting for transfers between devices, body(): lax.all_to_all(outgoing, ('tm', 'sub'), split_axis=0, concat_axis=0, tile...  20.4 us
    all_to_all x1, waiting for transfers between devices, body(): lax.all_to_all(windows, ('tm', 'sub'), split_axis=0, concat_axis=0, tiled...  12.7 us
    gather x2, local copies, waits for them, and re-layouts, body(): lax.dynamic_slice_in_dim(spectrum, start, FS, 2)  12.1 us
    all_to_all x1, starting transfers between devices, body(): lax.all_to_all(outgoing, ('tm', 'sub'), split_axis=0, concat_axis=0, tile...  11.7 us
    reshape x1, local copies, waits for them, and re-layouts, body(): outgoing = tiles.reshape(col_tiles, col_tiles, per_tile_row, chunk, 2, PA...  7.84 us
    dot_general x1, matrix products, body(): jnp.dot(grid_rows, column_table(), precision=lax.Precision.HIGHEST)  5.85 us
    dot_general x1, matrix products, body(): tiles = jnp.dot(placer, patches, precision=lax.Precision.HIGHEST)  5.67 us
  transfers between devices with their start and end apart: 2, of which 2 were waited for; matrix products, arithmetic and copies ran while one was open for 7% of the time, Pallas kernels for 0%

commit v1 on v0

--- a/solution.py
+++ b/solution.py
@@ -16,6 +16,12 @@
 kernel_width = 0.7
 
 
+def split_bf16(x):
+    high = x.astype(jnp.bfloat16)
+    low = (x - high.astype(jnp.float32)).astype(jnp.bfloat16)
+    return jnp.concatenate([high, low], axis=0)
+
+
 def patch_kernel(coords_ref, values_ref, phase_ref, out_ref):
     cells = lax.broadcasted_iota(jnp.int32, (PATCH, 1), 0).astype(jnp.float32)
 
@@ -24,19 +30,27 @@
         y = coords_ref[i, 1:2, :]
         rows_kernel = jnp.exp(-0.5 * ((x - cells) / kernel_width) ** 2)
         cols_kernel = jnp.exp(-0.5 * ((y - cells) / kernel_width) ** 2)
-        v_re = values_ref[i, 0:1, :]
-        v_im = values_ref[i, 1:2, :]
-        cos_b = phase_ref[i, 0]
-        sin_b = phase_ref[i, 1]
-        w_re = cols_kernel * (v_re * cos_b + v_im * sin_b)
-        w_im = cols_kernel * (v_im * cos_b - v_re * sin_b)
-        weighted = jnp.concatenate([w_re, w_im], axis=0)
-        out_ref[i] = lax.dot_general(
-            rows_kernel,
-            weighted,
+        weighted = jnp.concatenate(
+            [cols_kernel * values_ref[i, 0:1, :], cols_kernel * values_ref[i, 1:2, :]], axis=0
+        )
+        both = lax.dot_general(
+            split_bf16(rows_kernel),
+            split_bf16(weighted),
             (((1,), (1,)), ((), ())),
-            precision=lax.Precision.HIGHEST,
             preferred_element_type=jnp.float32,
+        )
+        width = 2 * PATCH
+        plain = (both[:PATCH, :width] + both[:PATCH, width:]) + (
+            both[PATCH:, :width] + both[PATCH:, width:]
+        )
+        real_part = plain[:, :PATCH]
+        imag_part = plain[:, PATCH:]
+        phase = phase_ref[pl.ds(i, 1), :]
+        cos_b = phase[:, :PATCH]
+        sin_b = phase[:, PATCH:]
+        out_ref[i] = jnp.concatenate(
+            [real_part * cos_b + imag_part * sin_b, imag_part * cos_b - real_part * sin_b],
+            axis=1,
         )
         return carry
 
@@ -49,16 +63,16 @@
     phase = (jnp.arange(PATCH, dtype=jnp.int32)[None, :] * local[:, None]) % SG_PER
     angle = phase.astype(jnp.float32) * (2.0 * math.pi / SG_PER)
     keep = live.astype(jnp.float32)[:, None]
-    phases = jnp.stack([jnp.cos(angle) * keep, jnp.sin(angle) * keep], axis=1)[..., None]
+    phases = jnp.concatenate([jnp.cos(angle) * keep, jnp.sin(angle) * keep], axis=1)
     spec = pl.BlockSpec((step, 2, VIS), lambda i: (i, 0, 0))
     patch = pl.pallas_call(
         patch_kernel,
         grid=(count // step,),
-        in_specs=[spec, spec, pl.BlockSpec((step, 2, PATCH, 1), lambda i: (i, 0, 0, 0))],
+        in_specs=[spec, spec, pl.BlockSpec((step, 2 * PATCH), lambda i: (i, 0))],
         out_specs=pl.BlockSpec((step, PATCH, 2 * PATCH), lambda i: (i, 0, 0)),
         out_shape=jax.ShapeDtypeStruct((count, PATCH, 2 * PATCH), jnp.float32),
         cost_estimate=pl.CostEstimate(
-            flops=count * PATCH * 2 * PATCH * VIS * 2,
+            flops=count * 4 * PATCH * 4 * PATCH * VIS * 2,
             transcendentals=count * 2 * PATCH * VIS,
             bytes_accessed=count * (4 * VIS + 2 * PATCH * PATCH) * 4,
         ),

time: 161 us -> 151 us (0.938)
  Pallas kernels: 55.9 us -> 50.1 us
  local copies, waits for them, and re-layouts: 29.4 us -> 25 us
    pallas_call x1, Pallas kernels: 55.9 us -> 50.1 us  [make_phased_patches(): pl.pallas_call(patch_kernel, grid=(count // step,), in_specs=[spec, spec,...]
    broadcast_in_dim x1 -> x0, local copies, waits for them, and re-layouts: 4.44 us -> none  [make_phased_patches(): jnp.stack([jnp.cos(angle) * keep, jnp.sin(angle) * keep], axis=1)[..., None]]
where the time goes in v1:
time: 151 us
  Pallas kernels  50.1 us (33%)
  waiting for transfers between devices  33.1 us (22%)
  local copies, waits for them, and re-layouts  25 us (17%)
  starting transfers between devices  15.3 us (10%)
  other arithmetic  13.8 us (9%)
  matrix products  12.1 us (8%)
    pallas_call x1, Pallas kernels, make_phased_patches(): pl.pallas_call(patch_kernel, grid=(count // step,), in_specs=[spec, spec,...  50.1 us
    all_to_all x1, waiting for transfers between devices, body(): lax.all_to_all(outgoing, ('tm', 'sub'), split_axis=0, concat_axis=0, tile...  20.4 us
    all_to_all x1, waiting for transfers between devices, body(): lax.all_to_all(windows, ('tm', 'sub'), split_axis=0, concat_axis=0, tiled...  12.7 us
    gather x2, local copies, waits for them, and re-layouts, body(): lax.dynamic_slice_in_dim(spectrum, start, FS, 2)  12.1 us
    all_to_all x1, starting transfers between devices, body(): lax.all_to_all(outgoing, ('tm', 'sub'), split_axis=0, concat_axis=0, tile...  11.7 us
    reshape x1, local copies, waits for them, and re-layouts, body(): outgoing = tiles.reshape(col_tiles, col_tiles, per_tile_row, chunk, 2, PA...  7.84 us
    dot_general x1, matrix products, body(): jnp.dot(grid_rows, column_table(), precision=lax.Precision.HIGHEST)  5.85 us
    dot_general x1, matrix products, body(): tiles = jnp.dot(placer, patches, precision=lax.Precision.HIGHEST)  5.66 us
  transfers between devices with their start and end apart: 2, of which 2 were waited for; matrix products, arithmetic and copies ran while one was open for 7% of the time, Pallas kernels for 0%

profile of v1, /device:TPU:1, one launch (start us, length us, event | category | flops | bytes accessed | tf_op | source)
XLA Modules:
  0.0 150.8 jit_solution(3166913386906408556)
XLA Ops:
  0.0 0.7 fusion.29
  0.7 0.1 copy.17
  1.4 0.2 cosine_multiply_fusion.1
  1.7 0.7 pad_maximum_fusion.phase_ref
  2.4 0.0 copy-start.2
  2.4 50.1 %shard_map.82 = f32[128,32,64]{2,1,0:T(8,128)} custom-call(f32[128,2,1024]{2,1,0:T(2,128)} %coords_ref.1, f32[128,2,1024]{2,1,0:T(2,128)} %values_ref.1, f32[128,64]{1,0:T(8,128)} %pad_maximum_fusion.phase_ref), custom_call_target="tpu_custom_call" | custom-call | flops 4294967296 | bytes 3145728 | tf_op jit(solution)/shard_map/pallas_call | solution.py:68
  52.5 2.7 %copy.18 = f32[128,32,64]{0,2,1:T(8,128)S(1)} copy(f32[128,32,64]{2,1,0:T(8,128)} %shard_map.82) | data formatting | bytes 2097152 | tf_op jit(solution)/shard_map/pallas_call | solution.py:68
  55.2 0.0 copy-done.2
  55.2 0.0 copy-done.3
  55.2 5.7 %convolution_bitcast_fusion = f32[16,8,4,2,16,32]{5,4,3,2,1,0:T(8,128)} fusion(f32[8,4,2,32,128,1]{4,3,2,1,0,5:T(8,128)S(1)} %bitcast.39, s32[16,16]{1,0:T(8,128)S(1)} %multiply_add_fusion, s32[128]{0:T(128)S(1)} %fusion.33), kind=kOutput, calls=%fused_computation.2 | convolution fusion | flops 805339136 | bytes 3147264 | tf_op jit(solution)/shard_map/dot_general | solution.py:125
  60.9 7.8 %reshape.68 = f32[128,4,2,512]{3,2,1,0:T(2,128)} reshape(f32[16,8,4,2,16,32]{5,4,3,2,1,0:T(8,128)} %convolution_bitcast_fusion) | data formatting | bytes 4194304 | tf_op jit(solution)/shard_map/reshape | solution.py:130
  68.7 11.7 %all-to-all-start = ((f32[128,4,2,512]{3,2,1,0:T(2,128)}), f32[128,4,2,512]{3,2,1,0:T(2,128)S(1)}, u32[]{:S(2)}, u32[]{:S(2)}) async-start(f32[128,4,2,512]{3,2,1,0:T(2,128)} %reshape.68), calls=%async_computation | async-start | bytes 4194304 | tf_op jit(solution)/shard_map/all_to_all | solution.py:132
  80.4 3.9 %fusion.14 = f32[512,512]{0,1:T(8,128)S(1)} fusion(), kind=kLoop, calls=%fused_computation.22 | loop fusion | flops 4194304 | bytes 1048576 | tf_op jit(solution)/shard_map/neg | solution.py:91
  84.3 4.2 %sine_multiply_fusion = (f32[512,512]{0,1:T(8,128)S(1)}, f32[512,512]{0,1:T(8,128)S(1)}) fusion(), kind=kLoop, calls=%fused_computation.17 | loop fusion | flops 4194304 | bytes 2097152 | tf_op jit(solution)/shard_map/mul | solution.py:89
  88.4 0.0 copy-start.1
  88.5 2.3 %maximum_maximum_fusion = f32[1024,1024]{0,1:T(8,128)} fusion(f32[512,512]{0,1:T(8,128)S(1)} %get-tuple-element.12, f32[512,512]{0,1:T(8,128)S(1)} %get-tuple-element.11, f32[512,512]{0,1:T(8,128)S(1)} %fusion.14), kind=kLoop, calls=%fused_computation.1 | loop fusion | flops 3145728 | bytes 7340032 | tf_op jit(solution)/shard_map/concatenate | solution.py:90
  90.8 0.0 copy-done.1
  90.8 20.4 %all-to-all-done = f32[128,4,2,512]{3,2,1,0:T(2,128)S(1)} async-done(((f32[128,4,2,512]{3,2,1,0:T(2,128)}), f32[128,4,2,512]{3,2,1,0:T(2,128)S(1)}, u32[]{:S(2)}, u32[]{:S(2)}) %all-to-all-start) | async-done | bytes 2097184 | tf_op jit(solution)/shard_map/all_to_all | solution.py:132
  111.2 0.7 reduce_sum.9
  112.0 5.9 %fusion.42 = f32[4,2,512]{2,0,1:T(4,128)S(1)} fusion(f32[4,1024,1]{1,0,2:T(4,128)S(1)} %reshape.81, f32[2,512,1024]{2,1,0:T(8,128)} %bitcast.38), kind=kOutput, calls=%fused_computation.76 | convolution fusion | flops 50331648 | bytes 4227072 | tf_op jit(solution)/shard_map/dot_general | solution.py:136
  117.8 0.3 copy.19
  118.1 6.9 %gather_fusion = f32[32,4,2,128]{1,2,3,0:T(2,128)} fusion(f32[4,2,512]{0,1,2:T(2,128)S(1)} %copy.19, s32[32]{0:T(128)S(1)} %fusion.39), kind=kCustom, calls=%fused_computation | custom fusion | bytes 262528 | tf_op jit(solution)/shard_map/vmap()/gather | solution.py:141
  125.0 5.3 %copy.20 = f32[32,4,2,128]{3,2,1,0:T(2,128)S(1)} copy(f32[32,4,2,128]{1,2,3,0:T(2,128)} %gather_fusion) | data formatting | bytes 262144 | tf_op jit(solution)/shard_map/vmap()/gather | solution.py:141
  130.3 0.9 broadcast_in_dim.2
  131.2 3.6 %all-to-all-start.1 = ((f32[128,4,2,128]{3,2,1,0:T(2,128)}), f32[128,4,2,128]{3,2,1,0:T(2,128)S(1)}, u32[]{:S(2)}, u32[]{:S(2)}) async-start(f32[128,4,2,128]{3,2,1,0:T(2,128)} %bitcast.13), calls=%async_computation.1 | async-start | bytes 1048576 | tf_op jit(solution)/shard_map/all_to_all | solution.py:147
  134.9 0.6 constant_dynamic-slice_fusion
  136.1 0.3 cosine_multiply_fusion.2
  136.4 12.7 %all-to-all-done.1 = f32[128,4,2,128]{3,2,1,0:T(2,128)S(1)} async-done(((f32[128,4,2,128]{3,2,1,0:T(2,128)}), f32[128,4,2,128]{3,2,1,0:T(2,128)S(1)}, u32[]{:S(2)}, u32[]{:S(2)}) %all-to-all-start.1) | async-done | bytes 524320 | tf_op jit(solution)/shard_map/all_to_all | solution.py:147
  149.1 0.4 fusion.41
  149.6 0.6 fusion.3
  150.2 0.0 copy-done
  150.2 0.6 broadcast_multiply_fusion
  (11 shorter events, 0.1 us)
Async XLA Ops:
  2.4 52.8 %copy-start.2 = (s32[128,1]{0,1:T(1,128)S(1)}, s32[128,1]{0,1:T(1,128)}, u32[]{:S(2)}) copy-start(s32[128,1]{0,1:T(1,128)} %param.10) | copy-start | bytes 1540
  2.4 52.8 %copy-start.3 = (s32[128]{0:T(128)S(1)}, s32[128]{0:T(128)}, u32[]{:S(2)}) copy-start(s32[128]{0:T(128)} %param.12) | copy-start | bytes 1540
  68.7 42.5 %all-to-all-start = ((f32[128,4,2,512]{3,2,1,0:T(2,128)}), f32[128,4,2,512]{3,2,1,0:T(2,128)S(1)}, u32[]{:S(2)}, u32[]{:S(2)}) async-start(f32[128,4,2,512]{3,2,1,0:T(2,128)} %reshape.68), calls=%async_computation | async-start | bytes 4194304 | tf_op jit(solution)/shard_map/all_to_all | solution.py:132
  88.4 2.4 %copy-start.1 = (s32[32,2]{0,1:T(2,128)S(1)}, s32[32,2]{0,1:T(2,128)}, u32[]{:S(2)}) copy-start(s32[32,2]{0,1:T(2,128)} %param.14) | copy-start | bytes 772
  125.0 25.2 %copy-start = (f32[1,32,128]{2,1,0:T(8,128)S(1)}, f32[1,32,128]{2,1,0:T(8,128)}, u32[]{:S(2)}) copy-start(f32[1,32,128]{2,1,0:T(8,128)} %param.15) | copy-start | bytes 49156
  131.2 17.9 %all-to-all-start.1 = ((f32[128,4,2,128]{3,2,1,0:T(2,128)}), f32[128,4,2,128]{3,2,1,0:T(2,128)S(1)}, u32[]{:S(2)}, u32[]{:S(2)}) async-start(f32[128,4,2,128]{3,2,1,0:T(2,128)} %bitcast.13), calls=%async_computation.1 | async-start | bytes 1048576 | tf_op jit(solution)/shard_map/all_to_all | solution.py:147

commit v2 on v1

--- a/solution.py
+++ b/solution.py
@@ -14,6 +14,7 @@
 
 
 kernel_width = 0.7
+gauss_scale = -0.5 / (kernel_width * kernel_width) / math.log(2.0)
 
 
 def split_bf16(x):
@@ -28,8 +29,8 @@
     def one_block(i, carry):
         x = coords_ref[i, 0:1, :]
         y = coords_ref[i, 1:2, :]
-        rows_kernel = jnp.exp(-0.5 * ((x - cells) / kernel_width) ** 2)
-        cols_kernel = jnp.exp(-0.5 * ((y - cells) / kernel_width) ** 2)
+        rows_kernel = jnp.exp2(((x - cells) ** 2) * gauss_scale)
+        cols_kernel = jnp.exp2(((y - cells) ** 2) * gauss_scale)
         weighted = jnp.concatenate(
             [cols_kernel * values_ref[i, 0:1, :], cols_kernel * values_ref[i, 1:2, :]], axis=0
         )

time: 151 us -> 149 us (0.987)
  Pallas kernels: 50.1 us -> 48.2 us
    pallas_call x1, Pallas kernels: 50.1 us -> 48.2 us  [make_phased_patches(): pl.pallas_call(patch_kernel, grid=(count // step,), in_specs=[spec, spec,...]
  transfers between devices with their start and end apart: 2 -> 2, of which waited for: 2 -> 2; matrix products, arithmetic and copies ran while one was open for 7% -> 8% of each run, Pallas kernels for 0% -> 0%
where the time goes in v2:
time: 149 us
  Pallas kernels  48.2 us (32%)
  waiting for transfers between devices  33.1 us (22%)
  local copies, waits for them, and re-layouts  25 us (17%)
  starting transfers between devices  15.3 us (10%)
  other arithmetic  13.8 us (9%)
  matrix products  12.1 us (8%)
    pallas_call x1, Pallas kernels, make_phased_patches(): pl.pallas_call(patch_kernel, grid=(count // step,), in_specs=[spec, spec,...  48.2 us
    all_to_all x1, waiting for transfers between devices, body(): lax.all_to_all(outgoing, ('tm', 'sub'), split_axis=0, concat_axis=0, tile...  20.4 us
    all_to_all x1, waiting for transfers between devices, body(): lax.all_to_all(windows, ('tm', 'sub'), split_axis=0, concat_axis=0, tiled...  12.7 us
    gather x2, local copies, waits for them, and re-layouts, body(): lax.dynamic_slice_in_dim(spectrum, start, FS, 2)  12.1 us
    all_to_all x1, starting transfers between devices, body(): lax.all_to_all(outgoing, ('tm', 'sub'), split_axis=0, concat_axis=0, tile...  11.7 us
    reshape x1, local copies, waits for them, and re-layouts, body(): outgoing = tiles.reshape(col_tiles, col_tiles, per_tile_row, chunk, 2, PA...  7.84 us
    dot_general x1, matrix products, body(): jnp.dot(grid_rows, column_table(), precision=lax.Precision.HIGHEST)  5.85 us
    dot_general x1, matrix products, body(): tiles = jnp.dot(placer, patches, precision=lax.Precision.HIGHEST)  5.66 us
  transfers between devices with their start and end apart: 2, of which 2 were waited for; matrix products, arithmetic and copies ran while one was open for 8% of the time, Pallas kernels for 0%

profile of v2, /device:TPU:1, one launch (start us, length us, event | category | flops | bytes accessed | tf_op | source)
XLA Modules:
  0.0 148.9 jit_solution(15198362361690743763)
XLA Ops:
  0.0 0.7 fusion.29
  0.7 0.1 copy.17
  1.4 0.2 cosine_multiply_fusion.1
  1.7 0.7 pad_maximum_fusion.phase_ref
  2.4 0.0 copy-start.2
  2.4 48.2 %shard_map.82 = f32[128,32,64]{2,1,0:T(8,128)} custom-call(f32[128,2,1024]{2,1,0:T(2,128)} %coords_ref.1, f32[128,2,1024]{2,1,0:T(2,128)} %values_ref.1, f32[128,64]{1,0:T(8,128)} %pad_maximum_fusion.phase_ref), custom_call_target="tpu_custom_call" | custom-call | flops 4294967296 | bytes 3145728 | tf_op jit(solution)/shard_map/pallas_call | solution.py:69
  50.6 2.7 %copy.18 = f32[128,32,64]{0,2,1:T(8,128)S(1)} copy(f32[128,32,64]{2,1,0:T(8,128)} %shard_map.82) | data formatting | bytes 2097152 | tf_op jit(solution)/shard_map/pallas_call | solution.py:69
  53.3 0.0 copy-done.2
  53.3 0.0 copy-done.3
  53.3 5.7 %convolution_bitcast_fusion = f32[16,8,4,2,16,32]{5,4,3,2,1,0:T(8,128)} fusion(f32[8,4,2,32,128,1]{4,3,2,1,0,5:T(8,128)S(1)} %bitcast.39, s32[16,16]{1,0:T(8,128)S(1)} %multiply_add_fusion, s32[128]{0:T(128)S(1)} %fusion.33), kind=kOutput, calls=%fused_computation.2 | convolution fusion | flops 805339136 | bytes 3147264 | tf_op jit(solution)/shard_map/dot_general | solution.py:126
  59.0 7.8 %reshape.68 = f32[128,4,2,512]{3,2,1,0:T(2,128)} reshape(f32[16,8,4,2,16,32]{5,4,3,2,1,0:T(8,128)} %convolution_bitcast_fusion) | data formatting | bytes 4194304 | tf_op jit(solution)/shard_map/reshape | solution.py:131
  66.8 11.7 %all-to-all-start = ((f32[128,4,2,512]{3,2,1,0:T(2,128)}), f32[128,4,2,512]{3,2,1,0:T(2,128)S(1)}, u32[]{:S(2)}, u32[]{:S(2)}) async-start(f32[128,4,2,512]{3,2,1,0:T(2,128)} %reshape.68), calls=%async_computation | async-start | bytes 4194304 | tf_op jit(solution)/shard_map/all_to_all | solution.py:133
  78.5 3.9 %fusion.14 = f32[512,512]{0,1:T(8,128)S(1)} fusion(), kind=kLoop, calls=%fused_computation.22 | loop fusion | flops 4194304 | bytes 1048576 | tf_op jit(solution)/shard_map/neg | solution.py:92
  82.4 4.2 %sine_multiply_fusion = (f32[512,512]{0,1:T(8,128)S(1)}, f32[512,512]{0,1:T(8,128)S(1)}) fusion(), kind=kLoop, calls=%fused_computation.17 | loop fusion | flops 4194304 | bytes 2097152 | tf_op jit(solution)/shard_map/mul | solution.py:90
  86.5 0.0 copy-start.1
  86.5 2.3 %maximum_maximum_fusion = f32[1024,1024]{0,1:T(8,128)} fusion(f32[512,512]{0,1:T(8,128)S(1)} %get-tuple-element.12, f32[512,512]{0,1:T(8,128)S(1)} %get-tuple-element.11, f32[512,512]{0,1:T(8,128)S(1)} %fusion.14), kind=kLoop, calls=%fused_computation.1 | loop fusion | flops 3145728 | bytes 7340032 | tf_op jit(solution)/shard_map/concatenate | solution.py:91
  88.9 0.0 copy-done.1
  88.9 20.4 %all-to-all-done = f32[128,4,2,512]{3,2,1,0:T(2,128)S(1)} async-done(((f32[128,4,2,512]{3,2,1,0:T(2,128)}), f32[128,4,2,512]{3,2,1,0:T(2,128)S(1)}, u32[]{:S(2)}, u32[]{:S(2)}) %all-to-all-start) | async-done | bytes 2097184 | tf_op jit(solution)/shard_map/all_to_all | solution.py:133
  109.3 0.7 reduce_sum.9
  110.1 5.9 %fusion.42 = f32[4,2,512]{2,0,1:T(4,128)S(1)} fusion(f32[4,1024,1]{1,0,2:T(4,128)S(1)} %reshape.81, f32[2,512,1024]{2,1,0:T(8,128)} %bitcast.38), kind=kOutput, calls=%fused_computation.76 | convolution fusion | flops 50331648 | bytes 4227072 | tf_op jit(solution)/shard_map/dot_general | solution.py:137
  115.9 0.3 copy.19
  116.2 6.9 %gather_fusion = f32[32,4,2,128]{1,2,3,0:T(2,128)} fusion(f32[4,2,512]{0,1,2:T(2,128)S(1)} %copy.19, s32[32]{0:T(128)S(1)} %fusion.39), kind=kCustom, calls=%fused_computation | custom fusion | bytes 262528 | tf_op jit(solution)/shard_map/vmap()/gather | solution.py:142
  123.1 5.3 %copy.20 = f32[32,4,2,128]{3,2,1,0:T(2,128)S(1)} copy(f32[32,4,2,128]{1,2,3,0:T(2,128)} %gather_fusion) | data formatting | bytes 262144 | tf_op jit(solution)/shard_map/vmap()/gather | solution.py:142
  128.3 0.9 broadcast_in_dim.2
  129.3 3.6 %all-to-all-start.1 = ((f32[128,4,2,128]{3,2,1,0:T(2,128)}), f32[128,4,2,128]{3,2,1,0:T(2,128)S(1)}, u32[]{:S(2)}, u32[]{:S(2)}) async-start(f32[128,4,2,128]{3,2,1,0:T(2,128)} %bitcast.13), calls=%async_computation.1 | async-start | bytes 1048576 | tf_op jit(solution)/shard_map/all_to_all | solution.py:148
  132.9 0.6 constant_dynamic-slice_fusion
  134.2 0.3 cosine_multiply_fusion.2
  134.5 12.7 %all-to-all-done.1 = f32[128,4,2,128]{3,2,1,0:T(2,128)S(1)} async-done(((f32[128,4,2,128]{3,2,1,0:T(2,128)}), f32[128,4,2,128]{3,2,1,0:T(2,128)S(1)}, u32[]{:S(2)}, u32[]{:S(2)}) %all-to-all-start.1) | async-done | bytes 524320 | tf_op jit(solution)/shard_map/all_to_all | solution.py:148
  147.2 0.4 fusion.41
  147.6 0.6 fusion.3
  148.3 0.0 copy-done
  148.3 0.6 broadcast_multiply_fusion
  (11 shorter events, 0.1 us)
Async XLA Ops:
  2.4 50.9 %copy-start.2 = (s32[128,1]{0,1:T(1,128)S(1)}, s32[128,1]{0,1:T(1,128)}, u32[]{:S(2)}) copy-start(s32[128,1]{0,1:T(1,128)} %param.10) | copy-start | bytes 1540
  2.4 50.9 %copy-start.3 = (s32[128]{0:T(128)S(1)}, s32[128]{0:T(128)}, u32[]{:S(2)}) copy-start(s32[128]{0:T(128)} %param.12) | copy-start | bytes 1540
  66.8 42.5 %all-to-all-start = ((f32[128,4,2,512]{3,2,1,0:T(2,128)}), f32[128,4,2,512]{3,2,1,0:T(2,128)S(1)}, u32[]{:S(2)}, u32[]{:S(2)}) async-start(f32[128,4,2,512]{3,2,1,0:T(2,128)} %reshape.68), calls=%async_computation | async-start | bytes 4194304 | tf_op jit(solution)/shard_map/all_to_all | solution.py:133
  86.5 2.4 %copy-start.1 = (s32[32,2]{0,1:T(2,128)S(1)}, s32[32,2]{0,1:T(2,128)}, u32[]{:S(2)}) copy-start(s32[32,2]{0,1:T(2,128)} %param.14) | copy-start | bytes 772
  123.1 25.2 %copy-start = (f32[1,32,128]{2,1,0:T(8,128)S(1)}, f32[1,32,128]{2,1,0:T(8,128)}, u32[]{:S(2)}) copy-start(f32[1,32,128]{2,1,0:T(8,128)} %param.15) | copy-start | bytes 49156
  129.3 17.9 %all-to-all-start.1 = ((f32[128,4,2,128]{3,2,1,0:T(2,128)}), f32[128,4,2,128]{3,2,1,0:T(2,128)S(1)}, u32[]{:S(2)}, u32[]{:S(2)}) async-start(f32[128,4,2,128]{3,2,1,0:T(2,128)} %bitcast.13), calls=%async_computation.1 | async-start | bytes 1048576 | tf_op jit(solution)/shard_map/all_to_all | solution.py:148

commit v3 on v2

--- a/solution.py
+++ b/solution.py
@@ -124,16 +124,27 @@
         tile_id[None, :] == jnp.arange(tiles_all, dtype=jnp.int32)[:, None]
     ).astype(jnp.float32)
     tiles = jnp.dot(placer, patches, precision=lax.Precision.HIGHEST)
-    per_tile_row = PATCH // chunk
-    outgoing = (
-        tiles.reshape(col_tiles, col_tiles, per_tile_row, chunk, 2, PATCH)
-        .transpose(0, 2, 3, 4, 1, 5)
-        .reshape(devices, chunk, 2, SG)
-    )
+    grid = (
+        tiles.reshape(col_tiles, col_tiles, PATCH, 2, PATCH)
+        .transpose(0, 2, 3, 1, 4)
+        .reshape(2, SG // 2, 2, SG)
+    )
+    core = lax.axis_index("tm") % 2
+    keep = jnp.where(core == 0, grid[0], grid[1])
+    give = jnp.where(core == 0, grid[1], grid[0])
+    pair = [(i, i ^ 1) for i in range(n_tm)]
+    chip_half = keep + lax.ppermute(give, "tm", pair)
+    half_chunk = chunk // 2
     arrived = lax.all_to_all(
-        outgoing, ("tm", "sub"), split_axis=0, concat_axis=0, tiled=True
-    )
-    grid_rows = jnp.sum(arrived, axis=0).reshape(chunk, 2 * SG)
+        chip_half.reshape(devices, half_chunk, 2, SG),
+        ("tm", "sub"),
+        split_axis=0,
+        concat_axis=0,
+        tiled=True,
+    )
+    grid_rows = jnp.sum(
+        arrived.reshape(n_tm // 2, 2, n_sub, half_chunk, 2, SG), axis=(0, 2)
+    ).reshape(chunk, 2 * SG)
     spectrum = jnp.dot(grid_rows, column_table(), precision=lax.Precision.HIGHEST).reshape(
         chunk, 2, SG
     )
@@ -153,7 +164,12 @@
     band = lax.axis_index("sub")
     first_y = offsets[facet, 0] + band * facet_rows
     ys = first_y + jnp.arange(facet_rows, dtype=jnp.int32)
-    rs = jnp.arange(SG, dtype=jnp.int32)
+    order = jnp.arange(SG, dtype=jnp.int32)
+    rs = (
+        ((order // half_chunk) % 2) * (SG // 2)
+        + (order // chunk) * half_chunk
+        + order % half_chunk
+    )
     angle = ((ys[:, None] * rs[None, :]) % SG).astype(jnp.float32) * (2.0 * math.pi / SG)
     scale = 1.0 / math.sqrt(SG)
     left = jnp.concatenate([jnp.cos(angle) * scale, jnp.sin(angle) * scale], 1)

time: 149 us -> 141 us (0.946)
  waiting for transfers between devices: 33.1 us -> 21.8 us
  other arithmetic: 13.8 us -> 19.2 us
  matrix products: 12.1 us -> 9.69 us
    all_to_all x1, waiting for transfers between devices: 20.4 us -> 9.17 us  [body(): lax.all_to_all(chip_half.reshape(devices, half_chunk, 2, SG), ('tm', 'sub...]
    reshape x2 -> x1, local copies, waits for them, and re-layouts: 7.87 us -> 0.03 us  [body(): grid_rows = jnp.sum(arrived.reshape(n_tm // 2, 2, n_sub, half_chunk, 2, S...]
    select_n x0 -> x2, local copies, waits for them, and re-layouts: none -> 7.68 us  [the longest x1 3.84 us: body(): give = jnp.where(core == 0, grid[1], grid[0])]
    select_n x0 -> x1, other arithmetic: none -> 4.26 us  [body(): give = jnp.where(core == 0, grid[1], grid[0])]
    dot_general x1, matrix products: 5.66 us -> 3.46 us  [body(): tiles = jnp.dot(placer, patches, precision=lax.Precision.HIGHEST)]
    add x0 -> x2, other arithmetic: none -> 1.52 us  [the longest x1 1.51 us: body(): chip_half = keep + lax.ppermute(give, 'tm', pair)]
    ppermute x0 -> x1, starting transfers between devices: none -> 1.5 us  [body(): chip_half = keep + lax.ppermute(give, 'tm', pair)]
  transfers between devices with their start and end apart: 2 -> 3, of which waited for: 2 -> 2; matrix products, arithmetic and copies ran while one was open for 8% -> 11% of each run, Pallas kernels for 0% -> 0%
where the time goes in v3:
time: 141 us
  Pallas kernels  48.2 us (34%)
  local copies, waits for them, and re-layouts  25.1 us (18%)
  waiting for transfers between devices  21.8 us (15%)
  other arithmetic  19.2 us (14%)
  starting transfers between devices  15.5 us (11%)
  matrix products  9.69 us (7%)
  between operations  1.49 us (1%)
    pallas_call x1, Pallas kernels, make_phased_patches(): pl.pallas_call(patch_kernel, grid=(count // step,), in_specs=[spec, spec,...  48.2 us
    all_to_all x1, waiting for transfers between devices, body(): lax.all_to_all(windows, ('tm', 'sub'), split_axis=0, concat_axis=0, tiled...  12.7 us
    gather x2, local copies, waits for them, and re-layouts, body(): lax.dynamic_slice_in_dim(spectrum, start, FS, 2)  12.1 us
    all_to_all x1, starting transfers between devices, body(): lax.all_to_all(chip_half.reshape(devices, half_chunk, 2, SG), ('tm', 'sub...  10.4 us
    all_to_all x1, waiting for transfers between devices, body(): lax.all_to_all(chip_half.reshape(devices, half_chunk, 2, SG), ('tm', 'sub...  9.17 us
    dot_general x1, matrix products, body(): jnp.dot(grid_rows, column_table(), precision=lax.Precision.HIGHEST)  5.65 us
    select_n x1, other arithmetic, body(): give = jnp.where(core == 0, grid[1], grid[0])  4.26 us
    mul x1, other arithmetic, column_table(): sine = jnp.sin(angle) * scale  4.16 us
  transfers between devices with their start and end apart: 3, of which 2 were waited for; matrix products, arithmetic and copies ran while one was open for 11% of the time, Pallas kernels for 0%

profile of v3, /device:TPU:1, one launch (start us, length us, event | category | flops | bytes accessed | tf_op | source)
XLA Modules:
  0.0 140.9 jit_solution(17007771498960174260)
XLA Ops:
  0.0 0.7 fusion.26
  0.7 0.1 copy.17
  1.4 0.2 cosine_multiply_fusion.1
  1.7 0.7 pad_maximum_fusion.phase_ref
  2.4 48.2 %shard_map.82 = f32[128,32,64]{2,1,0:T(8,128)} custom-call(f32[128,2,1024]{2,1,0:T(2,128)} %coords_ref.1, f32[128,2,1024]{2,1,0:T(2,128)} %values_ref.1, f32[128,64]{1,0:T(8,128)} %pad_maximum_fusion.phase_ref), custom_call_target="tpu_custom_call" | custom-call | flops 4294967296 | bytes 3145728 | tf_op jit(solution)/shard_map/pallas_call | solution.py:69
  50.6 2.7 %copy.18 = f32[128,32,64]{0,2,1:T(8,128)S(1)} copy(f32[128,32,64]{2,1,0:T(8,128)} %shard_map.82) | data formatting | bytes 2097152 | tf_op jit(solution)/shard_map/pallas_call | solution.py:69
  53.3 3.5 %convolution_bitcast_fusion = f32[16,32,2,16,32]{4,3,2,1,0:T(8,128)S(1)} fusion(f32[32,2,32,128,1]{3,2,1,0,4:T(8,128)S(1)} %bitcast.44, s32[16,16]{1,0:T(8,128)S(1)} %multiply_add_fusion, s32[128]{0:T(128)S(1)} %fusion.43), kind=kOutput, calls=%fused_computation.4 | convolution fusion | flops 805339136 | bytes 3147264 | tf_op jit(solution)/shard_map/dot_general | solution.py:126
  56.7 4.3 %slice_select_fusion = (f32[8,32,2,16,32]{4,3,2,1,0:T(8,128)}, f32[8,32,2,16,32]{4,3,2,1,0:T(8,128)}) fusion(f32[16,32,2,16,32]{4,3,2,1,0:T(8,128)S(1)} %convolution_bitcast_fusion, pred[]{:T(512)S(6)} %eq.42), kind=kLoop, calls=%fused_computation.2 | loop fusion | flops 524288 | bytes 4194305 | tf_op jit(solution)/shard_map/jit(_where)/select_n | solution.py:134
  61.0 3.8 %select_n.120 = f32[256,2,512]{2,1,0:T(2,128)S(1)} reshape(f32[8,32,2,16,32]{4,3,2,1,0:T(8,128)} %get-tuple-element.5) | data formatting | bytes 2097152 | tf_op jit(solution)/shard_map/jit(_where)/select_n | solution.py:134
  64.9 1.5 %collective-permute-start = (f32[256,2,512]{2,1,0:T(2,128)S(1)}, f32[256,2,512]{2,1,0:T(2,128)S(1)}, u32[]{:S(2)}, u32[]{:S(2)}) collective-permute-start(f32[256,2,512]{2,1,0:T(2,128)S(1)} %select_n.120), channel_id=1, source_target_pairs={{0,4},{4,0},{8,12},{12,8},{16,20},{20,16},{24,28},{28,24},{32,36},... | collective-permute-start | bytes 3145736 | tf_op jit(solution)/shard_map/ppermute | solution.py:136
  66.4 3.8 %select_n.118 = f32[256,2,512]{2,1,0:T(2,128)S(1)} reshape(f32[8,32,2,16,32]{4,3,2,1,0:T(8,128)} %get-tuple-element.6) | data formatting | bytes 2097152 | tf_op jit(solution)/shard_map/jit(_where)/select_n | solution.py:133
  70.2 0.0 collective-permute-done
  70.2 1.5 %add.134 = f32[256,2,512]{2,1,0:T(2,128)} add(f32[256,2,512]{2,1,0:T(2,128)S(1)} %select_n.118, f32[256,2,512]{2,1,0:T(2,128)S(1)} %collective-permute-done) | non-fusion elementwise | flops 262144 | bytes 3145728 | tf_op jit(solution)/shard_map/add | solution.py:136
  71.7 10.4 %all-to-all-start = ((f32[128,2,2,512]{3,2,1,0:T(2,128)}), f32[128,2,2,512]{3,2,1,0:T(2,128)S(1)}, u32[]{:S(2)}, u32[]{:S(2)}) async-start(f32[128,2,2,512]{3,2,1,0:T(2,128)} %bitcast.10), calls=%async_computation | async-start | bytes 2097152 | tf_op jit(solution)/shard_map/all_to_all | solution.py:138
  82.1 3.9 %fusion.14 = f32[512,512]{0,1:T(8,128)S(1)} fusion(), kind=kLoop, calls=%fused_computation.24 | loop fusion | flops 4194304 | bytes 1048576 | tf_op jit(solution)/shard_map/neg | solution.py:92
  86.0 4.2 %sine_multiply_fusion = (f32[512,512]{0,1:T(8,128)S(1)}, f32[512,512]{0,1:T(8,128)S(1)}) fusion(), kind=kLoop, calls=%fused_computation.19 | loop fusion | flops 4194304 | bytes 2097152 | tf_op jit(solution)/shard_map/mul | solution.py:90
  90.1 0.0 copy-start.1
  90.1 2.4 %maximum_maximum_fusion = f32[1024,1024]{0,1:T(8,128)} fusion(f32[512,512]{0,1:T(8,128)S(1)} %get-tuple-element.14, f32[512,512]{0,1:T(8,128)S(1)} %get-tuple-element.13, f32[512,512]{0,1:T(8,128)S(1)} %fusion.14), kind=kLoop, calls=%fused_computation.1 | loop fusion | flops 3145728 | bytes 7340032 | tf_op jit(solution)/shard_map/concatenate | solution.py:91
  92.5 9.2 %all-to-all-done = f32[128,2,2,512]{3,2,1,0:T(2,128)S(1)} async-done(((f32[128,2,2,512]{3,2,1,0:T(2,128)}), f32[128,2,2,512]{3,2,1,0:T(2,128)S(1)}, u32[]{:S(2)}, u32[]{:S(2)}) %all-to-all-start) | async-done | bytes 1048608 | tf_op jit(solution)/shard_map/all_to_all | solution.py:138
  101.7 0.4 reduce_sum.9
  102.1 5.6 %fusion.52 = f32[4,2,512]{2,0,1:T(4,128)S(1)} fusion(f32[4,1024,1]{1,0,2:T(4,128)S(1)} %reshape.137, f32[2,512,1024]{2,1,0:T(8,128)} %bitcast.42), kind=kOutput, calls=%fused_computation.100 | convolution fusion | flops 50331648 | bytes 4227072 | tf_op jit(solution)/shard_map/dot_general | solution.py:148
  107.7 0.5 copy.19
  108.2 6.9 %gather_fusion = f32[32,4,2,128]{1,2,3,0:T(2,128)} fusion(f32[4,2,512]{0,1,2:T(2,128)S(1)} %copy.19, s32[32]{0:T(128)S(1)} %fusion.49), kind=kCustom, calls=%fused_computation | custom fusion | bytes 262528 | tf_op jit(solution)/shard_map/vmap()/gather | solution.py:153
  115.1 5.3 %copy.20 = f32[32,4,2,128]{3,2,1,0:T(2,128)S(1)} copy(f32[32,4,2,128]{1,2,3,0:T(2,128)} %gather_fusion) | data formatting | bytes 262144 | tf_op jit(solution)/shard_map/vmap()/gather | solution.py:153
  120.4 0.9 broadcast_in_dim.2
  121.3 3.6 %all-to-all-start.1 = ((f32[128,4,2,128]{3,2,1,0:T(2,128)}), f32[128,4,2,128]{3,2,1,0:T(2,128)S(1)}, u32[]{:S(2)}, u32[]{:S(2)}) async-start(f32[128,4,2,128]{3,2,1,0:T(2,128)} %bitcast.15), calls=%async_computation.1 | async-start | bytes 1048576 | tf_op jit(solution)/shard_map/all_to_all | solution.py:159
  124.9 0.6 constant_dynamic-slice_fusion
  126.2 0.3 cosine_multiply_fusion.2
  126.5 12.7 %all-to-all-done.1 = f32[128,4,2,128]{3,2,1,0:T(2,128)S(1)} async-done(((f32[128,4,2,128]{3,2,1,0:T(2,128)}), f32[128,4,2,128]{3,2,1,0:T(2,128)S(1)}, u32[]{:S(2)}, u32[]{:S(2)}) %all-to-all-start.1) | async-done | bytes 524320 | tf_op jit(solution)/shard_map/all_to_all | solution.py:159
  139.2 0.4 fusion.51
  139.6 0.6 fusion.3
  140.3 0.6 broadcast_multiply_fusion
  (17 shorter events, 0.1 us)
Async XLA Ops:
  2.4 50.8 %copy-start.2 = (s32[128,1]{0,1:T(1,128)S(1)}, s32[128,1]{0,1:T(1,128)}, u32[]{:S(2)}) copy-start(s32[128,1]{0,1:T(1,128)} %param.10) | copy-start | bytes 1540
  2.4 50.8 %copy-start.3 = (s32[128]{0:T(128)S(1)}, s32[128]{0:T(128)}, u32[]{:S(2)}) copy-start(s32[128]{0:T(128)} %param.12) | copy-start | bytes 1540
  64.9 5.4 %collective-permute-start = (f32[256,2,512]{2,1,0:T(2,128)S(1)}, f32[256,2,512]{2,1,0:T(2,128)S(1)}, u32[]{:S(2)}, u32[]{:S(2)}) collective-permute-start(f32[256,2,512]{2,1,0:T(2,128)S(1)} %select_n.120), channel_id=1, source_target_pairs={{0,4},{4,0},{8,12},{12,8},{16,20},{20,16},{24,28},{28,24},{32,36},... | collective-permute-start | bytes 3145736 | tf_op jit(solution)/shard_map/ppermute | solution.py:136
  71.7 29.9 %all-to-all-start = ((f32[128,2,2,512]{3,2,1,0:T(2,128)}), f32[128,2,2,512]{3,2,1,0:T(2,128)S(1)}, u32[]{:S(2)}, u32[]{:S(2)}) async-start(f32[128,2,2,512]{3,2,1,0:T(2,128)} %bitcast.10), calls=%async_computation | async-start | bytes 2097152 | tf_op jit(solution)/shard_map/all_to_all | solution.py:138
  90.1 2.4 %copy-start.1 = (s32[32,2]{0,1:T(2,128)S(1)}, s32[32,2]{0,1:T(2,128)}, u32[]{:S(2)}) copy-start(s32[32,2]{0,1:T(2,128)} %param.14) | copy-start | bytes 772
  115.1 25.2 %copy-start = (f32[1,32,128]{2,1,0:T(8,128)S(1)}, f32[1,32,128]{2,1,0:T(8,128)}, u32[]{:S(2)}) copy-start(f32[1,32,128]{2,1,0:T(8,128)} %param.15) | copy-start | bytes 49156
  121.3 17.9 %all-to-all-start.1 = ((f32[128,4,2,128]{3,2,1,0:T(2,128)}), f32[128,4,2,128]{3,2,1,0:T(2,128)S(1)}, u32[]{:S(2)}, u32[]{:S(2)}) async-start(f32[128,4,2,128]{3,2,1,0:T(2,128)} %bitcast.15), calls=%async_computation.1 | async-start | bytes 1048576 | tf_op jit(solution)/shard_map/all_to_all | solution.py:159

commit v4 on v3

--- a/solution.py
+++ b/solution.py
@@ -119,6 +119,8 @@
 
     target = block_dest[:, 0]
     row_tile = (target % n_sub) * band_tiles + block_tile // col_tiles
+    core = lax.axis_index("tm") % 2
+    row_tile = (row_tile + core * (col_tiles // 2)) % col_tiles
     tile_id = row_tile * col_tiles + block_tile % col_tiles
     placer = (
         tile_id[None, :] == jnp.arange(tiles_all, dtype=jnp.int32)[:, None]
@@ -129,11 +131,8 @@
         .transpose(0, 2, 3, 1, 4)
         .reshape(2, SG // 2, 2, SG)
     )
-    core = lax.axis_index("tm") % 2
-    keep = jnp.where(core == 0, grid[0], grid[1])
-    give = jnp.where(core == 0, grid[1], grid[0])
     pair = [(i, i ^ 1) for i in range(n_tm)]
-    chip_half = keep + lax.ppermute(give, "tm", pair)
+    chip_half = grid[0] + lax.ppermute(grid[1], "tm", pair)
     half_chunk = chunk // 2
     arrived = lax.all_to_all(
         chip_half.reshape(devices, half_chunk, 2, SG),
@@ -150,8 +149,8 @@
     )
 
     offsets = jnp.clip(facet_offsets, 0, SG - FS)
-    windows = jax.vmap(lambda start: lax.dynamic_slice_in_dim(spectrum, start, FS, 2))(
-        offsets[:, 1]
+    windows = jnp.stack(
+        [lax.dynamic_slice_in_dim(spectrum, offsets[f, 1], FS, 2) for f in range(n_tm)]
     )
     windows = jnp.broadcast_to(
         windows[:, None], (n_tm, n_sub, chunk, 2, FS)

time: 141 us -> 189 us (1.34)
  between operations: 1.49 us -> 61.8 us
  waiting for transfers between devices: 21.8 us -> 13.2 us
  local copies, waits for them, and re-layouts: 25.1 us -> 18.2 us
  starting transfers between devices: 15.5 us -> 21.6 us
  other arithmetic: 19.2 us -> 14.9 us
    gather x2 -> x0, local copies, waits for them, and re-layouts: 12.1 us -> none  [body(): lax.dynamic_slice_in_dim(spectrum, start, FS, 2)]
    all_to_all x1, waiting for transfers between devices: 9.17 us -> 0.01 us  [body(): lax.all_to_all(chip_half.reshape(devices, half_chunk, 2, SG), ('tm', 'sub...]
    squeeze x0 -> x2, local copies, waits for them, and re-layouts: none -> 7.7 us  [body(): chip_half = grid[0] + lax.ppermute(grid[1], 'tm', pair)]
    select_n x2 -> x0, local copies, waits for them, and re-layouts: 7.68 us -> none  [the longest x1 3.84 us: body(): give = jnp.where(core == 0, grid[1], grid[0])]
    all_to_all x1, starting transfers between devices: 3.64 us -> 9.76 us  [body(): lax.all_to_all(windows, ('tm', 'sub'), split_axis=0, concat_axis=0, tiled...]
    slice x0 -> x2, local copies, waits for them, and re-layouts: none -> 4.92 us  [the longest x1 4.21 us: body(): chip_half = grid[0] + lax.ppermute(grid[1], 'tm', pair)]
    select_n x1 -> x0, other arithmetic: 4.26 us -> none  [body(): give = jnp.where(core == 0, grid[1], grid[0])]
  transfers between devices with their start and end apart: 3 -> 3, of which waited for: 2 -> 1; matrix products, arithmetic and copies ran while one was open for 11% -> 9% of each run, Pallas kernels for 0% -> 0%
where the time goes in v4:
time: 189 us; the launch traced here: 188 us
  between operations  61.8 us (33%)
  Pallas kernels  48.2 us (26%)
  starting transfers between devices  21.6 us (11%)
  local copies, waits for them, and re-layouts  18.2 us (10%)
  other arithmetic  14.9 us (8%)
  waiting for transfers between devices  13.2 us (7%)
  matrix products  9.91 us (5%)
    pallas_call x1, Pallas kernels, make_phased_patches(): pl.pallas_call(patch_kernel, grid=(count // step,), in_specs=[spec, spec,...  48.2 us
    all_to_all x1, waiting for transfers between devices, body(): lax.all_to_all(windows, ('tm', 'sub'), split_axis=0, concat_axis=0, tiled...  13.2 us
    all_to_all x1, starting transfers between devices, body(): lax.all_to_all(chip_half.reshape(devices, half_chunk, 2, SG), ('tm', 'sub...  10.4 us
    all_to_all x1, starting transfers between devices, body(): lax.all_to_all(windows, ('tm', 'sub'), split_axis=0, concat_axis=0, tiled...  9.76 us
    squeeze x2, local copies, waits for them, and re-layouts, body(): chip_half = grid[0] + lax.ppermute(grid[1], 'tm', pair)  7.7 us
    dot_general x1, matrix products, body(): jnp.dot(grid_rows, column_table(), precision=lax.Precision.HIGHEST)  5.87 us
    slice x1, local copies, waits for them, and re-layouts, body(): chip_half = grid[0] + lax.ppermute(grid[1], 'tm', pair)  4.21 us
    mul x1, other arithmetic, column_table(): sine = jnp.sin(angle) * scale  4.16 us
  transfers between devices with their start and end apart: 3, of which 1 were waited for; matrix products, arithmetic and copies ran while one was open for 9% of the time, Pallas kernels for 0%

profile of v4, /device:TPU:1, one launch (start us, length us, event | category | flops | bytes accessed | tf_op | source)
XLA Modules:
  0.0 187.8 jit_solution(2305974797928620166)
XLA Ops:
  0.0 0.7 fusion.26
  0.7 0.1 copy.45
  1.4 0.2 cosine_multiply_fusion.1
  1.7 0.7 pad_maximum_fusion.phase_ref
  2.4 48.2 %shard_map.82 = f32[128,32,64]{2,1,0:T(8,128)} custom-call(f32[128,2,1024]{2,1,0:T(2,128)} %coords_ref.1, f32[128,2,1024]{2,1,0:T(2,128)} %values_ref.1, f32[128,64]{1,0:T(8,128)} %pad_maximum_fusion.phase_ref), custom_call_target="tpu_custom_call" | custom-call | flops 4294967296 | bytes 3145728 | tf_op jit(solution)/shard_map/pallas_call | solution.py:69
  50.6 2.7 %copy.46 = f32[128,32,64]{0,2,1:T(8,128)S(1)} copy(f32[128,32,64]{2,1,0:T(8,128)} %shard_map.82) | data formatting | bytes 2097152 | tf_op jit(solution)/shard_map/pallas_call | solution.py:69
  53.3 3.5 %convolution_bitcast_fusion = f32[16,32,2,16,32]{4,3,2,1,0:T(8,128)S(1)} fusion(f32[32,2,32,128,1]{3,2,1,0,4:T(8,128)S(1)} %bitcast.138, s32[16,16]{1,0:T(8,128)S(1)} %multiply_add_fusion, s32[128]{0:T(128)S(1)} %fusion.43), kind=kOutput, calls=%fused_computation.1 | convolution fusion | flops 805339136 | bytes 3147264 | tf_op jit(solution)/shard_map/dot_general | solution.py:128
  56.8 4.2 %fusion.50 = (f32[8,32,2,16,32]{4,3,2,1,0:T(8,128)}, f32[8,32,2,16,32]{4,3,2,1,0:T(8,128)}) fusion(f32[16,32,2,16,32]{4,3,2,1,0:T(8,128)S(1)} %convolution_bitcast_fusion), kind=kLoop, calls=%fused_computation.161 | loop fusion | bytes 4194304 | tf_op jit(solution)/shard_map/slice | solution.py:135
  61.0 3.8 %squeeze.121 = f32[256,2,512]{2,1,0:T(2,128)S(1)} reshape(f32[8,32,2,16,32]{4,3,2,1,0:T(8,128)} %get-tuple-element.5) | data formatting | bytes 2097152 | tf_op jit(solution)/shard_map/squeeze | solution.py:135
  64.8 1.5 collective-permute-start
  66.3 3.9 %squeeze.120 = f32[256,2,512]{2,1,0:T(2,128)S(1)} reshape(f32[8,32,2,16,32]{4,3,2,1,0:T(8,128)} %get-tuple-element.6) | data formatting | bytes 2097152 | tf_op jit(solution)/shard_map/squeeze | solution.py:135
  70.2 0.0 collective-permute-done
  70.2 1.5 add.234
  71.7 10.4 %all-to-all-start = ((f32[128,2,2,512]{3,2,1,0:T(2,128)}), f32[128,2,2,512]{3,2,1,0:T(2,128)S(1)}, u32[]{:S(2)}, u32[]{:S(2)}) async-start(f32[128,2,2,512]{3,2,1,0:T(2,128)} %bitcast.10), calls=%async_computation | async-start | bytes 2097152 | tf_op jit(solution)/shard_map/all_to_all | solution.py:137
  82.1 0.7 fusion.52
  100.5 0.7 constant_dynamic-slice_fusion.32
  143.8 3.9 %fusion.14 = f32[512,512]{0,1:T(8,128)S(1)} fusion(), kind=kLoop, calls=%fused_computation.21 | loop fusion | flops 4194304 | bytes 1048576 | tf_op jit(solution)/shard_map/neg | solution.py:92
  147.7 4.2 %sine_multiply_fusion = (f32[512,512]{0,1:T(8,128)S(1)}, f32[512,512]{0,1:T(8,128)S(1)}) fusion(), kind=kLoop, calls=%fused_computation.16 | loop fusion | flops 4194304 | bytes 2097152 | tf_op jit(solution)/shard_map/mul | solution.py:90
  151.9 2.4 %maximum_maximum_fusion = f32[1024,1024]{0,1:T(8,128)} fusion(f32[512,512]{0,1:T(8,128)S(1)} %get-tuple-element.79, f32[512,512]{0,1:T(8,128)S(1)} %get-tuple-element.78, f32[512,512]{0,1:T(8,128)S(1)} %fusion.14), kind=kLoop, calls=%fused_computation | loop fusion | flops 3145728 | bytes 7340032 | tf_op jit(solution)/shard_map/concatenate | solution.py:91
  154.2 0.0 all-to-all-done
  154.2 0.4 reduce_sum.9
  154.6 0.0 copy-start
  154.6 5.9 %fusion.53 = f32[4,2,512]{2,0,1:T(4,128)S(1)} fusion(f32[4,1024,1]{1,0,2:T(4,128)S(1)} %reshape.127, f32[2,512,1024]{2,1,0:T(8,128)} %bitcast.136), kind=kOutput, calls=%fused_computation.164 | convolution fusion | flops 50331648 | bytes 4227072 | tf_op jit(solution)/shard_map/dot_general | solution.py:147
  160.5 0.2 constant_dynamic-slice_fusion.18
  160.8 0.2 constant_dynamic-slice_fusion
  161.3 0.9 broadcast_in_dim.2
  162.2 9.8 %all-to-all-start.1 = ((f32[128,4,2,128]{3,2,1,0:T(2,128)}), f32[128,4,2,128]{3,2,1,0:T(2,128)S(1)}, u32[]{:S(2)}, u32[]{:S(2)}) async-start(f32[128,4,2,128]{3,2,1,0:T(2,128)} %bitcast.78), calls=%async_computation.1 | async-start | bytes 1048576 | tf_op jit(solution)/shard_map/all_to_all | solution.py:158
  172.5 0.3 cosine_multiply_fusion.2
  172.9 13.2 %all-to-all-done.1 = f32[128,4,2,128]{3,2,1,0:T(2,128)S(1)} async-done(((f32[128,4,2,128]{3,2,1,0:T(2,128)}), f32[128,4,2,128]{3,2,1,0:T(2,128)S(1)}, u32[]{:S(2)}, u32[]{:S(2)}) %all-to-all-start.1) | async-done | bytes 524320 | tf_op jit(solution)/shard_map/all_to_all | solution.py:158
  186.1 0.4 fusion.51
  186.5 0.6 fusion.3
  187.2 0.6 broadcast_multiply_fusion
  (48 shorter events, 0.4 us)
Async XLA Ops:
  2.4 50.8 %copy-start.2 = (s32[128,1]{0,1:T(1,128)S(1)}, s32[128,1]{0,1:T(1,128)}, u32[]{:S(2)}) copy-start(s32[128,1]{0,1:T(1,128)} %param.10) | copy-start | bytes 1540
  2.4 50.9 %copy-start.3 = (s32[128]{0:T(128)S(1)}, s32[128]{0:T(128)}, u32[]{:S(2)}) copy-start(s32[128]{0:T(128)} %param.12) | copy-start | bytes 1540
  64.8 5.4 %collective-permute-start = (f32[256,2,512]{2,1,0:T(2,128)S(1)}, f32[256,2,512]{2,1,0:T(2,128)S(1)}, u32[]{:S(2)}, u32[]{:S(2)}) collective-permute-start(f32[256,2,512]{2,1,0:T(2,128)S(1)} %squeeze.121), channel_id=1, source_target_pairs={{0,4},{4,0},{8,12},{12,8},{16,20},{20,16},{24,28},{28,24},{32,36},... | collective-permute-start | bytes 3145736 | tf_op jit(solution)/shard_map/ppermute | solution.py:135
  66.3 15.8 %copy-start.1 = (s32[32,2]{0,1:T(2,128)S(1)}, s32[32,2]{0,1:T(2,128)}, u32[]{:S(2)}) copy-start(s32[32,2]{0,1:T(2,128)} %param.14) | copy-start | bytes 772
  71.7 82.5 %all-to-all-start = ((f32[128,2,2,512]{3,2,1,0:T(2,128)}), f32[128,2,2,512]{3,2,1,0:T(2,128)S(1)}, u32[]{:S(2)}, u32[]{:S(2)}) async-start(f32[128,2,2,512]{3,2,1,0:T(2,128)} %bitcast.10), calls=%async_computation | async-start | bytes 2097152 | tf_op jit(solution)/shard_map/all_to_all | solution.py:137
  154.6 32.6 %copy-start = (f32[1,32,128]{2,1,0:T(8,128)S(1)}, f32[1,32,128]{2,1,0:T(8,128)}, u32[]{:S(2)}) copy-start(f32[1,32,128]{2,1,0:T(8,128)} %param.15) | copy-start | bytes 49156
  162.2 23.9 %all-to-all-start.1 = ((f32[128,4,2,128]{3,2,1,0:T(2,128)}), f32[128,4,2,128]{3,2,1,0:T(2,128)S(1)}, u32[]{:S(2)}, u32[]{:S(2)}) async-start(f32[128,4,2,128]{3,2,1,0:T(2,128)} %bitcast.78), calls=%async_computation.1 | async-start | bytes 1048576 | tf_op jit(solution)/shard_map/all_to_all | solution.py:158

commit v5 on v4

--- a/solution.py
+++ b/solution.py
@@ -81,10 +81,10 @@
     return patch.reshape(count, 2 * PATCH * PATCH)
 
 
-def column_table():
-    index = jnp.arange(SG, dtype=jnp.int32)
-    phase = index[:, None] * index[None, :] % SG
-    angle = phase.astype(jnp.float32) * (2.0 * math.pi / SG)
+def window_table():
+    cs = jnp.arange(SG, dtype=jnp.int32)
+    xs = jnp.arange(FS, dtype=jnp.int32)
+    angle = ((cs[:, None] * xs[None, :]) % SG).astype(jnp.float32) * (2.0 * math.pi / SG)
     scale = 1.0 / math.sqrt(SG)
     cosine = jnp.cos(angle) * scale
     sine = jnp.sin(angle) * scale
@@ -126,13 +126,19 @@
         tile_id[None, :] == jnp.arange(tiles_all, dtype=jnp.int32)[:, None]
     ).astype(jnp.float32)
     tiles = jnp.dot(placer, patches, precision=lax.Precision.HIGHEST)
-    grid = (
-        tiles.reshape(col_tiles, col_tiles, PATCH, 2, PATCH)
-        .transpose(0, 2, 3, 1, 4)
-        .reshape(2, SG // 2, 2, SG)
-    )
+    half_tiles = tiles_all // 2
+
+    def to_rows(part):
+        return (
+            part.reshape(col_tiles // 2, col_tiles, PATCH, 2, PATCH)
+            .transpose(0, 2, 3, 1, 4)
+            .reshape(SG // 2, 2, SG)
+        )
+
     pair = [(i, i ^ 1) for i in range(n_tm)]
-    chip_half = grid[0] + lax.ppermute(grid[1], "tm", pair)
+    chip_half = to_rows(tiles[:half_tiles]) + lax.ppermute(
+        to_rows(tiles[half_tiles:]), "tm", pair
+    )
     half_chunk = chunk // 2
     arrived = lax.all_to_all(
         chip_half.reshape(devices, half_chunk, 2, SG),
@@ -144,13 +150,20 @@
     grid_rows = jnp.sum(
         arrived.reshape(n_tm // 2, 2, n_sub, half_chunk, 2, SG), axis=(0, 2)
     ).reshape(chunk, 2 * SG)
-    spectrum = jnp.dot(grid_rows, column_table(), precision=lax.Precision.HIGHEST).reshape(
-        chunk, 2, SG
-    )
-
     offsets = jnp.clip(facet_offsets, 0, SG - FS)
-    windows = jnp.stack(
-        [lax.dynamic_slice_in_dim(spectrum, offsets[f, 1], FS, 2) for f in range(n_tm)]
+    cs = jnp.arange(SG, dtype=jnp.int32)
+    shift = ((offsets[:, 1][:, None] * cs[None, :]) % SG).astype(jnp.float32) * (
+        2.0 * math.pi / SG
+    )
+    cos_s = jnp.cos(shift)[:, None, :]
+    sin_s = jnp.sin(shift)[:, None, :]
+    g_re = grid_rows[None, :, :SG]
+    g_im = grid_rows[None, :, SG:]
+    shifted = jnp.concatenate(
+        [g_re * cos_s + g_im * sin_s, g_im * cos_s - g_re * sin_s], axis=2
+    ).reshape(n_tm * chunk, 2 * SG)
+    windows = jnp.dot(shifted, window_table(), precision=lax.Precision.HIGHEST).reshape(
+        n_tm, chunk, 2, FS
     )
     windows = jnp.broadcast_to(
         windows[:, None], (n_tm, n_sub, chunk, 2, FS)

time: 189 us -> 141 us (0.75)
  between operations: 61.8 us -> 1.58 us
  local copies, waits for them, and re-layouts: 18.2 us -> 37 us
  waiting for transfers between devices: 13.2 us -> 29.9 us
  other arithmetic: 14.9 us -> 5.79 us
  matrix products: 9.91 us -> 2.79 us
  starting transfers between devices: 21.6 us -> 15.5 us
    reshape x1 -> x8, local copies, waits for them, and re-layouts: 0.03 us -> 32 us  [the longest x4 22.9 us: to_rows(): part.reshape(col_tiles // 2, col_tiles, PATCH, 2, PATCH)]
    all_to_all x1, waiting for transfers between devices: 0.01 us -> 17.2 us  [body(): lax.all_to_all(chip_half.reshape(devices, half_chunk, 2, SG), ('tm', 'sub...]
    squeeze x2 -> x0, local copies, waits for them, and re-layouts: 7.7 us -> none  [body(): chip_half = grid[0] + lax.ppermute(grid[1], 'tm', pair)]
    all_to_all x1, starting transfers between devices: 9.76 us -> 3.64 us  [body(): lax.all_to_all(windows, ('tm', 'sub'), split_axis=0, concat_axis=0, tiled...]
    slice x2, local copies, waits for them, and re-layouts: 4.92 us -> 0.22 us  [the longest x1 0.22 us: body(): tiles[half_tiles:]]
    dot_general x1, matrix products: 5.87 us -> 1.18 us  [body(): jnp.dot(shifted, window_table(), precision=lax.Precision.HIGHEST)]
    mul x1, other arithmetic: 4.16 us -> 1.05 us  [window_table(): sine = jnp.sin(angle) * scale]
    neg x1, other arithmetic: 3.86 us -> 0.98 us  [window_table(): -sine]
  transfers between devices with their start and end apart: 3 -> 3, of which waited for: 1 -> 2; matrix products, arithmetic and copies ran while one was open for 9% -> 13% of each run, Pallas kernels for 0% -> 0%
where the time goes in v5:
time: 141 us
  Pallas kernels  48.2 us (34%)
  local copies, waits for them, and re-layouts  37 us (26%)
  waiting for transfers between devices  29.9 us (21%)
  starting transfers between devices  15.5 us (11%)
  other arithmetic  5.79 us (4%)
  matrix products  2.79 us (2%)
  between operations  1.58 us (1%)
    pallas_call x1, Pallas kernels, make_phased_patches(): pl.pallas_call(patch_kernel, grid=(count // step,), in_specs=[spec, spec,...  48.2 us
    reshape x4, local copies, waits for them, and re-layouts, to_rows(): part.reshape(col_tiles // 2, col_tiles, PATCH, 2, PATCH)  22.9 us
    all_to_all x1, waiting for transfers between devices, body(): lax.all_to_all(chip_half.reshape(devices, half_chunk, 2, SG), ('tm', 'sub...  17.2 us
    all_to_all x1, waiting for transfers between devices, body(): lax.all_to_all(windows, ('tm', 'sub'), split_axis=0, concat_axis=0, tiled...  12.7 us
    all_to_all x1, starting transfers between devices, body(): lax.all_to_all(chip_half.reshape(devices, half_chunk, 2, SG), ('tm', 'sub...  10.2 us
    reshape x2, local copies, waits for them, and re-layouts, to_rows(): return part.reshape(col_tiles // 2, col_tiles, PATCH, 2, PATCH).transpose...  7.09 us
    all_to_all x1, starting transfers between devices, body(): lax.all_to_all(windows, ('tm', 'sub'), split_axis=0, concat_axis=0, tiled...  3.64 us
  transfers between devices with their start and end apart: 3, of which 2 were waited for; matrix products, arithmetic and copies ran while one was open for 13% of the time, Pallas kernels for 0%

profile of v5, /device:TPU:1, one launch (start us, length us, event | category | flops | bytes accessed | tf_op | source)
XLA Modules:
  0.0 140.7 jit_solution(11162955843074061417)
XLA Ops:
  0.0 0.7 fusion.35
  1.4 0.2 cosine_multiply_fusion.1
  1.7 0.7 pad_maximum_fusion.phase_ref
  2.4 48.2 %shard_map.82 = f32[128,32,64]{2,1,0:T(8,128)} custom-call(f32[128,2,1024]{2,1,0:T(2,128)} %coords_ref.1, f32[128,2,1024]{2,1,0:T(2,128)} %values_ref.1, f32[128,64]{1,0:T(8,128)} %pad_maximum_fusion.phase_ref), custom_call_target="tpu_custom_call" | custom-call | flops 4294967296 | bytes 3145728 | tf_op jit(solution)/shard_map/pallas_call | solution.py:69
  50.6 2.7 %copy.32 = f32[128,32,64]{0,2,1:T(8,128)S(1)} copy(f32[128,32,64]{2,1,0:T(8,128)} %shard_map.82) | data formatting | bytes 2097152 | tf_op jit(solution)/shard_map/pallas_call | solution.py:69
  53.3 1.0 fusion.20
  54.3 0.2 fusion.60
  54.6 4.9 %reshape.202 = f32[8,16,32,2,32]{4,3,2,1,0:T(2,128)} reshape(f32[128,2048]{1,0:T(8,128)S(1)} %get-tuple-element.5) | data formatting | bytes 2097152 | tf_op jit(solution)/shard_map/reshape | solution.py:133
  59.4 6.6 %copy.47 = f32[8,16,32,2,32]{4,1,2,0,3:T(8,128)} copy(f32[8,16,32,2,32]{4,3,2,1,0:T(2,128)} %reshape.202) | data formatting | bytes 2097152 | tf_op jit(solution)/shard_map/reshape | solution.py:133
  66.0 3.5 %reshape.203 = f32[256,2,512]{2,0,1:T(8,128)S(1)} reshape(f32[8,32,2,16,32]{4,3,1,0,2:T(8,128)} %bitcast.50) | data formatting | bytes 2097152 | tf_op jit(solution)/shard_map/reshape | solution.py:135
  69.6 1.7 %collective-permute-start = (f32[256,2,512]{2,0,1:T(8,128)S(1)}, f32[256,2,512]{2,0,1:T(8,128)S(1)}, u32[]{:S(2)}, u32[]{:S(2)}) collective-permute-start(f32[256,2,512]{2,0,1:T(8,128)S(1)} %reshape.203), channel_id=1, source_target_pairs={{0,4},{4,0},{8,12},{12,8},{16,20},{20,16},{24,28},{28,24},{32,36},... | collective-permute-start | bytes 3145736 | tf_op jit(solution)/shard_map/ppermute | solution.py:139
  71.3 4.9 %reshape.200 = f32[8,16,32,2,32]{4,3,2,1,0:T(2,128)} reshape(f32[128,2048]{1,0:T(8,128)S(1)} %get-tuple-element.6) | data formatting | bytes 2097152 | tf_op jit(solution)/shard_map/reshape | solution.py:133
  76.1 6.6 %copy.48 = f32[8,16,32,2,32]{4,1,2,0,3:T(8,128)} copy(f32[8,16,32,2,32]{4,3,2,1,0:T(2,128)} %reshape.200) | data formatting | bytes 2097152 | tf_op jit(solution)/shard_map/reshape | solution.py:133
  82.7 3.5 %reshape.201 = f32[256,2,512]{2,0,1:T(8,128)S(1)} reshape(f32[8,32,2,16,32]{4,3,1,0,2:T(8,128)} %bitcast.51) | data formatting | bytes 2097152 | tf_op jit(solution)/shard_map/reshape | solution.py:135
  86.3 0.2 add.156
  86.5 0.6 reshape.204
  87.1 1.3 copy.35
  88.5 10.2 %all-to-all-start = ((f32[128,2,2,512]{3,1,2,0:T(2,128)}), f32[128,2,2,512]{3,1,2,0:T(2,128)S(1)}, u32[]{:S(2)}, u32[]{:S(2)}) async-start(f32[128,2,2,512]{3,1,2,0:T(2,128)} %copy.35), calls=%async_computation | async-start | bytes 2097152 | tf_op jit(solution)/shard_map/all_to_all | solution.py:143
  98.7 1.0 fusion.21
  99.6 1.1 sine_multiply_fusion
  100.8 0.3 fusion.33
  101.2 17.2 %all-to-all-done = f32[128,2,2,512]{3,1,2,0:T(2,128)S(1)} async-done(((f32[128,2,2,512]{3,1,2,0:T(2,128)}), f32[128,2,2,512]{3,1,2,0:T(2,128)S(1)}, u32[]{:S(2)}, u32[]{:S(2)}) %all-to-all-start) | async-done | bytes 1048608 | tf_op jit(solution)/shard_map/all_to_all | solution.py:143
  118.4 0.4 reduce_sum.9
  118.9 1.2 fusion.8
  120.2 0.9 broadcast_in_dim.2
  121.1 3.6 %all-to-all-start.1 = ((f32[128,4,2,128]{3,2,1,0:T(2,128)}), f32[128,4,2,128]{3,2,1,0:T(2,128)S(1)}, u32[]{:S(2)}, u32[]{:S(2)}) async-start(f32[128,4,2,128]{3,2,1,0:T(2,128)} %bitcast.14), calls=%async_computation.1 | async-start | bytes 1048576 | tf_op jit(solution)/shard_map/all_to_all | solution.py:171
  124.8 0.6 constant_dynamic-slice_fusion
  126.0 0.3 cosine_multiply_fusion.2
  126.4 12.7 %all-to-all-done.1 = f32[128,4,2,128]{3,2,1,0:T(2,128)S(1)} async-done(((f32[128,4,2,128]{3,2,1,0:T(2,128)}), f32[128,4,2,128]{3,2,1,0:T(2,128)S(1)}, u32[]{:S(2)}, u32[]{:S(2)}) %all-to-all-start.1) | async-done | bytes 524320 | tf_op jit(solution)/shard_map/all_to_all | solution.py:171
  139.0 0.4 fusion.61
  139.5 0.6 fusion
  140.1 0.6 broadcast_multiply_fusion
  (24 shorter events, 0.5 us)
Async XLA Ops:
  2.4 50.8 %copy-start.2 = (s32[128,1]{0,1:T(1,128)S(1)}, s32[128,1]{0,1:T(1,128)}, u32[]{:S(2)}) copy-start(s32[128,1]{0,1:T(1,128)} %param.10) | copy-start | bytes 1540
  2.4 50.9 %copy-start.3 = (s32[128]{0:T(128)S(1)}, s32[128]{0:T(128)}, u32[]{:S(2)}) copy-start(s32[128]{0:T(128)} %param.12) | copy-start | bytes 1540
  69.6 16.7 %collective-permute-start = (f32[256,2,512]{2,0,1:T(8,128)S(1)}, f32[256,2,512]{2,0,1:T(8,128)S(1)}, u32[]{:S(2)}, u32[]{:S(2)}) collective-permute-start(f32[256,2,512]{2,0,1:T(8,128)S(1)} %reshape.203), channel_id=1, source_target_pairs={{0,4},{4,0},{8,12},{12,8},{16,20},{20,16},{24,28},{28,24},{32,36},... | collective-permute-start | bytes 3145736 | tf_op jit(solution)/shard_map/ppermute | solution.py:139
  86.5 14.3 %copy-start.1 = (s32[32,2]{0,1:T(2,128)S(1)}, s32[32,2]{0,1:T(2,128)}, u32[]{:S(2)}) copy-start(s32[32,2]{0,1:T(2,128)} %param.14) | copy-start | bytes 772
  88.5 29.9 %all-to-all-start = ((f32[128,2,2,512]{3,1,2,0:T(2,128)}), f32[128,2,2,512]{3,1,2,0:T(2,128)S(1)}, u32[]{:S(2)}, u32[]{:S(2)}) async-start(f32[128,2,2,512]{3,1,2,0:T(2,128)} %copy.35), calls=%async_computation | async-start | bytes 2097152 | tf_op jit(solution)/shard_map/all_to_all | solution.py:143
  118.8 21.3 %copy-start = (f32[1,32,128]{2,1,0:T(8,128)S(1)}, f32[1,32,128]{2,1,0:T(8,128)}, u32[]{:S(2)}) copy-start(f32[1,32,128]{2,1,0:T(8,128)} %param.15) | copy-start | bytes 49156
  121.1 17.9 %all-to-all-start.1 = ((f32[128,4,2,128]{3,2,1,0:T(2,128)}), f32[128,4,2,128]{3,2,1,0:T(2,128)S(1)}, u32[]{:S(2)}, u32[]{:S(2)}) async-start(f32[128,4,2,128]{3,2,1,0:T(2,128)} %bitcast.14), calls=%async_computation.1 | async-start | bytes 1048576 | tf_op jit(solution)/shard_map/all_to_all | solution.py:171

commit v6 on v5

--- a/solution.py
+++ b/solution.py
@@ -4,6 +4,7 @@
 import jax.numpy as jnp
 from jax import lax
 from jax.experimental import pallas as pl
+from jax.experimental.pallas import tpu as pltpu
 from jax.sharding import PartitionSpec as P
 
 SG = 512
@@ -23,8 +24,16 @@
     return jnp.concatenate([high, low], axis=0)
 
 
-def patch_kernel(coords_ref, values_ref, phase_ref, out_ref):
+def patch_kernel(place_ref, coords_ref, values_ref, phase_ref, out_ref):
+    step = coords_ref.shape[0]
     cells = lax.broadcasted_iota(jnp.int32, (PATCH, 1), 0).astype(jnp.float32)
+    slot = lax.broadcasted_iota(jnp.int32, (PATCH, 128), 1) // PATCH
+    half = out_ref.shape[1] // 2
+    per_group = 128 // PATCH
+
+    @pl.when(pl.program_id(0) == 0)
+    def _():
+        out_ref[...] = jnp.zeros_like(out_ref)
 
     def one_block(i, carry):
         x = coords_ref[i, 0:1, :]
@@ -49,36 +58,51 @@
         phase = phase_ref[pl.ds(i, 1), :]
         cos_b = phase[:, :PATCH]
         sin_b = phase[:, PATCH:]
-        out_ref[i] = jnp.concatenate(
-            [real_part * cos_b + imag_part * sin_b, imag_part * cos_b - real_part * sin_b],
-            axis=1,
-        )
+        phased = (
+            real_part * cos_b + imag_part * sin_b,
+            imag_part * cos_b - real_part * sin_b,
+        )
+        tile = place_ref[pl.program_id(0) * step + i]
+        row_tile = tile // (SG // PATCH)
+        col_tile = tile % (SG // PATCH)
+        rows = pl.ds(pl.multiple_of(row_tile * PATCH, PATCH), PATCH)
+        keep = slot == col_tile % per_group
+        for part, values in enumerate(phased):
+            start = pl.multiple_of(part * half + (col_tile // per_group) * 128, 128)
+            spread = jnp.concatenate([values] * per_group, axis=1)
+            out_ref[rows, pl.ds(start, 128)] += jnp.where(keep, spread, 0.0)
         return carry
 
-    lax.fori_loop(0, out_ref.shape[0], one_block, 0)
-
-
-def make_phased_patches(vis_coords, vis_values, live, local):
+    lax.fori_loop(0, step, one_block, 0)
+
+
+def make_phased_grid(vis_coords, vis_values, live, local, tile_id):
     count = vis_coords.shape[0]
     step = 8
     phase = (jnp.arange(PATCH, dtype=jnp.int32)[None, :] * local[:, None]) % SG_PER
     angle = phase.astype(jnp.float32) * (2.0 * math.pi / SG_PER)
     keep = live.astype(jnp.float32)[:, None]
     phases = jnp.concatenate([jnp.cos(angle) * keep, jnp.sin(angle) * keep], axis=1)
-    spec = pl.BlockSpec((step, 2, VIS), lambda i: (i, 0, 0))
-    patch = pl.pallas_call(
+    spec = pl.BlockSpec((step, 2, VIS), lambda i, place: (i, 0, 0))
+    return pl.pallas_call(
         patch_kernel,
-        grid=(count // step,),
-        in_specs=[spec, spec, pl.BlockSpec((step, 2 * PATCH), lambda i: (i, 0))],
-        out_specs=pl.BlockSpec((step, PATCH, 2 * PATCH), lambda i: (i, 0, 0)),
-        out_shape=jax.ShapeDtypeStruct((count, PATCH, 2 * PATCH), jnp.float32),
+        grid_spec=pltpu.PrefetchScalarGridSpec(
+            num_scalar_prefetch=1,
+            grid=(count // step,),
+            in_specs=[
+                spec,
+                spec,
+                pl.BlockSpec((step, 2 * PATCH), lambda i, place: (i, 0)),
+            ],
+            out_specs=pl.BlockSpec((SG, 2 * SG), lambda i, place: (0, 0)),
+        ),
+        out_shape=jax.ShapeDtypeStruct((SG, 2 * SG), jnp.float32),
         cost_estimate=pl.CostEstimate(
             flops=count * 4 * PATCH * 4 * PATCH * VIS * 2,
             transcendentals=count * 2 * PATCH * VIS,
-            bytes_accessed=count * (4 * VIS + 2 * PATCH * PATCH) * 4,
+            bytes_accessed=count * 4 * VIS * 4 + SG * SG * 8,
         ),
-    )(vis_coords, vis_values, phases)
-    return patch.reshape(count, 2 * PATCH * PATCH)
+    )(tile_id, vis_coords, vis_values, phases)
 
 
 def window_table():
@@ -115,30 +139,15 @@
     facet_rows = FS // n_sub
 
     live = jnp.arange(blocks, dtype=jnp.int32) < block_counts[0]
-    patches = make_phased_patches(vis_coords, vis_values, live, block_local)
-
     target = block_dest[:, 0]
     row_tile = (target % n_sub) * band_tiles + block_tile // col_tiles
     core = lax.axis_index("tm") % 2
     row_tile = (row_tile + core * (col_tiles // 2)) % col_tiles
     tile_id = row_tile * col_tiles + block_tile % col_tiles
-    placer = (
-        tile_id[None, :] == jnp.arange(tiles_all, dtype=jnp.int32)[:, None]
-    ).astype(jnp.float32)
-    tiles = jnp.dot(placer, patches, precision=lax.Precision.HIGHEST)
-    half_tiles = tiles_all // 2
-
-    def to_rows(part):
-        return (
-            part.reshape(col_tiles // 2, col_tiles, PATCH, 2, PATCH)
-            .transpose(0, 2, 3, 1, 4)
-            .reshape(SG // 2, 2, SG)
-        )
+    grid = make_phased_grid(vis_coords, vis_values, live, block_local, tile_id)
 
     pair = [(i, i ^ 1) for i in range(n_tm)]
-    chip_half = to_rows(tiles[:half_tiles]) + lax.ppermute(
-        to_rows(tiles[half_tiles:]), "tm", pair
-    )
+    chip_half = grid[: SG // 2] + lax.ppermute(grid[SG // 2 :], "tm", pair)
     half_chunk = chunk // 2
     arrived = lax.all_to_all(
         chip_half.reshape(devices, half_chunk, 2, SG),

time: 141 us -> 125 us (0.89)
  local copies, waits for them, and re-layouts: 37 us -> 5.52 us
  Pallas kernels: 48.2 us -> 61 us
  waiting for transfers between devices: 29.9 us -> 32.2 us
    reshape x6 -> x0, local copies, waits for them, and re-layouts: 30 us -> none  [the longest x4 22.9 us: to_rows(): part.reshape(col_tiles // 2, col_tiles, PATCH, 2, PATCH)]
    pallas_call x1, Pallas kernels: 48.2 us -> 61 us  [make_phased_grid(): pl.pallas_call(patch_kernel, grid_spec=pltpu.PrefetchScalarGridSpec(num_s...]
    pallas_call x1 -> x0, local copies, waits for them, and re-layouts: 2.66 us -> none  [make_phased_patches(): pl.pallas_call(patch_kernel, grid=(count // step,), in_specs=[spec, spec,...]
    ppermute x1, waiting for transfers between devices: 0.01 us -> 2.29 us  [body(): chip_half = grid[:SG // 2] + lax.ppermute(grid[SG // 2:], 'tm', pair)]
  transfers between devices with their start and end apart: 3 -> 3, of which waited for: 2 -> 3; matrix products, arithmetic and copies ran while one was open for 13% -> 3% of each run, Pallas kernels for 0% -> 0%
where the time goes in v6:
time: 125 us; the launch traced here: 124 us
  Pallas kernels  61 us (49%)
  waiting for transfers between devices  32.2 us (26%)
  starting transfers between devices  15.6 us (12%)
  other arithmetic  6.93 us (6%)
  local copies, waits for them, and re-layouts  5.52 us (4%)
  matrix products  1.76 us (1%)
  between operations  1.5 us (1%)
    pallas_call x1, Pallas kernels, make_phased_grid(): pl.pallas_call(patch_kernel, grid_spec=pltpu.PrefetchScalarGridSpec(num_s...  61 us
    all_to_all x1, waiting for transfers between devices, body(): lax.all_to_all(chip_half.reshape(devices, half_chunk, 2, SG), ('tm', 'sub...  17.2 us
    all_to_all x1, waiting for transfers between devices, body(): lax.all_to_all(windows, ('tm', 'sub'), split_axis=0, concat_axis=0, tiled...  12.7 us
    all_to_all x1, starting transfers between devices, body(): lax.all_to_all(chip_half.reshape(devices, half_chunk, 2, SG), ('tm', 'sub...  10.4 us
    all_to_all x1, starting transfers between devices, body(): lax.all_to_all(windows, ('tm', 'sub'), split_axis=0, concat_axis=0, tiled...  3.64 us
  transfers between devices with their start and end apart: 3, of which 3 were waited for; matrix products, arithmetic and copies ran while one was open for 3% of the time, Pallas kernels for 0%

profile of v6, /device:TPU:1, one launch (start us, length us, event | category | flops | bytes accessed | tf_op | source)
XLA Modules:
  0.0 124.4 jit_solution(18151508118050906238)
XLA Ops:
  0.0 0.7 fusion.33
  0.7 0.1 copy.11
  1.4 0.2 cosine_multiply_fusion.1
  1.7 0.7 pad_maximum_fusion.phase_ref
  2.4 1.2 fusion.50.place_ref
  3.6 61.0 %shard_map.82 = f32[512,1024]{1,0:T(8,128)} custom-call(s32[128]{0:T(128)} %fusion.50.place_ref, f32[128,2,1024]{2,1,0:T(2,128)} %coords_ref.1, f32[128,2,1024]{2,1,0:T(2,128)} %values_ref.1, f32[128,64]{1,0:T(8,128)} %pad_maximum_fusion.phase_ref), custom_call_target="tpu_custom_call" | custom-call | flops 4294967296 | bytes 4194304 | tf_op jit(solution)/shard_map/pallas_call | solution.py:87
  64.6 1.5 %slice.29 = f32[256,1024]{1,0:T(8,128)S(1)} slice(f32[512,1024]{1,0:T(8,128)} %shard_map.82), slice={[256:512], [0:1024]} | slice | bytes 2097152 | tf_op jit(solution)/shard_map/slice | solution.py:150
  66.1 1.5 %collective-permute-start = (f32[256,1024]{1,0:T(8,128)S(1)}, f32[256,1024]{1,0:T(8,128)S(1)}, u32[]{:S(2)}, u32[]{:S(2)}) collective-permute-start(f32[256,1024]{1,0:T(8,128)S(1)} %slice.29), channel_id=1, source_target_pairs={{0,4},{4,0},{8,12},{12,8},{16,20},{20,16},{24,28},{28,24},{32,36},... | collective-permute-start | bytes 3145736 | tf_op jit(solution)/shard_map/ppermute | solution.py:150
  67.6 2.3 %collective-permute-done = f32[256,1024]{1,0:T(8,128)S(1)} collective-permute-done((f32[256,1024]{1,0:T(8,128)S(1)}, f32[256,1024]{1,0:T(8,128)S(1)}, u32[]{:S(2)}, u32[]{:S(2)}) %collective-permute-start) | collective-permute-done | bytes 1048608 | tf_op jit(solution)/shard_map/ppermute | solution.py:150
  69.9 0.0 copy-done
  69.9 0.2 slice_add_fusion
  70.0 1.9 %reshape.183 = f32[128,2,2,512]{3,2,1,0:T(2,128)} reshape(f32[256,1024]{1,0:T(8,128)S(1)} %slice_add_fusion) | data formatting | bytes 2097152 | tf_op jit(solution)/shard_map/reshape | solution.py:153
  71.9 10.4 %all-to-all-start = ((f32[128,2,2,512]{3,2,1,0:T(2,128)}), f32[128,2,2,512]{3,2,1,0:T(2,128)S(1)}, u32[]{:S(2)}, u32[]{:S(2)}) async-start(f32[128,2,2,512]{3,2,1,0:T(2,128)} %reshape.183), calls=%async_computation | async-start | bytes 2097152 | tf_op jit(solution)/shard_map/all_to_all | solution.py:152
  82.4 1.0 fusion.20
  83.3 1.1 sine_multiply_fusion
  84.4 0.1 maximum_maximum_fusion
  84.5 0.0 copy-done.2
  84.5 0.3 fusion.31
  84.9 17.2 %all-to-all-done = f32[128,2,2,512]{3,2,1,0:T(2,128)S(1)} async-done(((f32[128,2,2,512]{3,2,1,0:T(2,128)}), f32[128,2,2,512]{3,2,1,0:T(2,128)S(1)}, u32[]{:S(2)}, u32[]{:S(2)}) %all-to-all-start) | async-done | bytes 1048608 | tf_op jit(solution)/shard_map/all_to_all | solution.py:152
  102.1 0.4 reduce_sum.9
  102.5 0.1 multiply_add_fusion
  102.6 1.2 fusion.8
  103.7 0.1 copy.12
  103.9 0.9 broadcast_in_dim.2
  104.8 3.6 %all-to-all-start.1 = ((f32[128,4,2,128]{3,2,1,0:T(2,128)}), f32[128,4,2,128]{3,2,1,0:T(2,128)S(1)}, u32[]{:S(2)}, u32[]{:S(2)}) async-start(f32[128,4,2,128]{3,2,1,0:T(2,128)} %bitcast.11), calls=%async_computation.1 | async-start | bytes 1048576 | tf_op jit(solution)/shard_map/all_to_all | solution.py:180
  108.4 0.0 copy-start.1
  108.5 0.6 constant_dynamic-slice_fusion
  109.7 0.3 cosine_multiply_fusion.2
  110.1 12.7 %all-to-all-done.1 = f32[128,4,2,128]{3,2,1,0:T(2,128)S(1)} async-done(((f32[128,4,2,128]{3,2,1,0:T(2,128)}), f32[128,4,2,128]{3,2,1,0:T(2,128)S(1)}, u32[]{:S(2)}, u32[]{:S(2)}) %all-to-all-start.1) | async-done | bytes 524320 | tf_op jit(solution)/shard_map/all_to_all | solution.py:180
  122.7 0.4 fusion.58
  123.2 0.6 fusion
  123.8 0.6 broadcast_multiply_fusion
  (12 shorter events, 0.1 us)
Async XLA Ops:
  64.6 5.3 %copy-start = (f32[512,1024]{1,0:T(8,128)S(1)}, f32[512,1024]{1,0:T(8,128)}, u32[]{:S(2)}) copy-start(f32[512,1024]{1,0:T(8,128)} %shard_map.82) | copy-start | bytes 6291460
  66.1 3.8 %collective-permute-start = (f32[256,1024]{1,0:T(8,128)S(1)}, f32[256,1024]{1,0:T(8,128)S(1)}, u32[]{:S(2)}, u32[]{:S(2)}) collective-permute-start(f32[256,1024]{1,0:T(8,128)S(1)} %slice.29), channel_id=1, source_target_pairs={{0,4},{4,0},{8,12},{12,8},{16,20},{20,16},{24,28},{28,24},{32,36},... | collective-permute-start | bytes 3145736 | tf_op jit(solution)/shard_map/ppermute | solution.py:150
  71.9 12.6 %copy-start.2 = (s32[32,2]{0,1:T(2,128)S(1)}, s32[32,2]{0,1:T(2,128)}, u32[]{:S(2)}) copy-start(s32[32,2]{0,1:T(2,128)} %param.14) | copy-start | bytes 772
  71.9 30.2 %all-to-all-start = ((f32[128,2,2,512]{3,2,1,0:T(2,128)}), f32[128,2,2,512]{3,2,1,0:T(2,128)S(1)}, u32[]{:S(2)}, u32[]{:S(2)}) async-start(f32[128,2,2,512]{3,2,1,0:T(2,128)} %reshape.183), calls=%async_computation | async-start | bytes 2097152 | tf_op jit(solution)/shard_map/all_to_all | solution.py:152
  104.8 17.9 %all-to-all-start.1 = ((f32[128,4,2,128]{3,2,1,0:T(2,128)}), f32[128,4,2,128]{3,2,1,0:T(2,128)S(1)}, u32[]{:S(2)}, u32[]{:S(2)}) async-start(f32[128,4,2,128]{3,2,1,0:T(2,128)} %bitcast.11), calls=%async_computation.1 | async-start | bytes 1048576 | tf_op jit(solution)/shard_map/all_to_all | solution.py:180
  108.4 15.3 %copy-start.1 = (f32[1,32,128]{2,1,0:T(8,128)S(1)}, f32[1,32,128]{2,1,0:T(8,128)}, u32[]{:S(2)}) copy-start(f32[1,32,128]{2,1,0:T(8,128)} %param.15) | copy-start | bytes 49156

commit v7 on v6

--- a/solution.py
+++ b/solution.py
@@ -11,6 +11,7 @@
 PATCH = 32
 FS = 128
 VIS = 1024
+VIS_PART = 512
 SG_PER = 16
 
 
@@ -27,7 +28,7 @@
 def patch_kernel(place_ref, coords_ref, values_ref, phase_ref, out_ref):
     step = coords_ref.shape[0]
     cells = lax.broadcasted_iota(jnp.int32, (PATCH, 1), 0).astype(jnp.float32)
-    slot = lax.broadcasted_iota(jnp.int32, (PATCH, 128), 1) // PATCH
+    pad = jnp.zeros((PATCH, 128 - PATCH), jnp.float32)
     half = out_ref.shape[1] // 2
     per_group = 128 // PATCH
 
@@ -36,19 +37,24 @@
         out_ref[...] = jnp.zeros_like(out_ref)
 
     def one_block(i, carry):
-        x = coords_ref[i, 0:1, :]
-        y = coords_ref[i, 1:2, :]
-        rows_kernel = jnp.exp2(((x - cells) ** 2) * gauss_scale)
-        cols_kernel = jnp.exp2(((y - cells) ** 2) * gauss_scale)
-        weighted = jnp.concatenate(
-            [cols_kernel * values_ref[i, 0:1, :], cols_kernel * values_ref[i, 1:2, :]], axis=0
-        )
-        both = lax.dot_general(
-            split_bf16(rows_kernel),
-            split_bf16(weighted),
-            (((1,), (1,)), ((), ())),
-            preferred_element_type=jnp.float32,
-        )
+        both = None
+        for part in range(VIS // VIS_PART):
+            lanes = pl.ds(part * VIS_PART, VIS_PART)
+            x = coords_ref[i, 0:1, lanes]
+            y = coords_ref[i, 1:2, lanes]
+            rows_kernel = jnp.exp2(((x - cells) ** 2) * gauss_scale)
+            cols_kernel = jnp.exp2(((y - cells) ** 2) * gauss_scale)
+            weighted = jnp.concatenate(
+                [cols_kernel * values_ref[i, 0:1, lanes], cols_kernel * values_ref[i, 1:2, lanes]],
+                axis=0,
+            )
+            term = lax.dot_general(
+                split_bf16(rows_kernel),
+                split_bf16(weighted),
+                (((1,), (1,)), ((), ())),
+                preferred_element_type=jnp.float32,
+            )
+            both = term if both is None else both + term
         width = 2 * PATCH
         plain = (both[:PATCH, :width] + both[:PATCH, width:]) + (
             both[PATCH:, :width] + both[PATCH:, width:]
@@ -66,11 +72,11 @@
         row_tile = tile // (SG // PATCH)
         col_tile = tile % (SG // PATCH)
         rows = pl.ds(pl.multiple_of(row_tile * PATCH, PATCH), PATCH)
-        keep = slot == col_tile % per_group
+        shift = (col_tile % per_group) * PATCH
         for part, values in enumerate(phased):
             start = pl.multiple_of(part * half + (col_tile // per_group) * 128, 128)
-            spread = jnp.concatenate([values] * per_group, axis=1)
-            out_ref[rows, pl.ds(start, 128)] += jnp.where(keep, spread, 0.0)
+            padded = jnp.concatenate([values, pad], axis=1)
+            out_ref[rows, pl.ds(start, 128)] += pltpu.roll(padded, shift, 1)
         return carry
 
     lax.fori_loop(0, step, one_block, 0)

time: 125 us -> 130 us (1.040)
  Pallas kernels: 61 us -> 66.7 us
    pallas_call x1, Pallas kernels: 61 us -> 66.7 us  [make_phased_grid(): pl.pallas_call(patch_kernel, grid_spec=pltpu.PrefetchScalarGridSpec(num_s...]
where the time goes in v7:
time: 130 us
  Pallas kernels  66.7 us (51%)
  waiting for transfers between devices  32.2 us (25%)
  starting transfers between devices  15.6 us (12%)
  other arithmetic  6.93 us (5%)
  local copies, waits for them, and re-layouts  5.52 us (4%)
  matrix products  1.77 us (1%)
  between operations  1.5 us (1%)
    pallas_call x1, Pallas kernels, make_phased_grid(): pl.pallas_call(patch_kernel, grid_spec=pltpu.PrefetchScalarGridSpec(num_s...  66.7 us
    all_to_all x1, waiting for transfers between devices, body(): lax.all_to_all(chip_half.reshape(devices, half_chunk, 2, SG), ('tm', 'sub...  17.2 us
    all_to_all x1, waiting for transfers between devices, body(): lax.all_to_all(windows, ('tm', 'sub'), split_axis=0, concat_axis=0, tiled...  12.7 us
    all_to_all x1, starting transfers between devices, body(): lax.all_to_all(chip_half.reshape(devices, half_chunk, 2, SG), ('tm', 'sub...  10.4 us
    all_to_all x1, starting transfers between devices, body(): lax.all_to_all(windows, ('tm', 'sub'), split_axis=0, concat_axis=0, tiled...  3.63 us
  transfers between devices with their start and end apart: 3, of which 3 were waited for; matrix products, arithmetic and copies ran while one was open for 3% of the time, Pallas kernels for 0%

profile of v7, /device:TPU:1, one launch (start us, length us, event | category | flops | bytes accessed | tf_op | source)
XLA Modules:
  0.0 130.2 jit_solution(16857409107679358176)
XLA Ops:
  0.0 0.7 fusion.33
  0.7 0.1 copy.11
  1.4 0.2 cosine_multiply_fusion.1
  1.7 0.7 pad_maximum_fusion.phase_ref
  2.4 1.2 fusion.50.place_ref
  3.6 66.7 %shard_map.82 = f32[512,1024]{1,0:T(8,128)} custom-call(s32[128]{0:T(128)} %fusion.50.place_ref, f32[128,2,1024]{2,1,0:T(2,128)} %coords_ref.1, f32[128,2,1024]{2,1,0:T(2,128)} %values_ref.1, f32[128,64]{1,0:T(8,128)} %pad_maximum_fusion.phase_ref), custom_call_target="tpu_custom_call" | custom-call | flops 4294967296 | bytes 4194304 | tf_op jit(solution)/shard_map/pallas_call | solution.py:93
  70.3 1.5 %slice.29 = f32[256,1024]{1,0:T(8,128)S(1)} slice(f32[512,1024]{1,0:T(8,128)} %shard_map.82), slice={[256:512], [0:1024]} | slice | bytes 2097152 | tf_op jit(solution)/shard_map/slice | solution.py:156
  71.8 1.5 %collective-permute-start = (f32[256,1024]{1,0:T(8,128)S(1)}, f32[256,1024]{1,0:T(8,128)S(1)}, u32[]{:S(2)}, u32[]{:S(2)}) collective-permute-start(f32[256,1024]{1,0:T(8,128)S(1)} %slice.29), channel_id=1, source_target_pairs={{0,4},{4,0},{8,12},{12,8},{16,20},{20,16},{24,28},{28,24},{32,36},... | collective-permute-start | bytes 3145736 | tf_op jit(solution)/shard_map/ppermute | solution.py:156
  73.3 2.3 %collective-permute-done = f32[256,1024]{1,0:T(8,128)S(1)} collective-permute-done((f32[256,1024]{1,0:T(8,128)S(1)}, f32[256,1024]{1,0:T(8,128)S(1)}, u32[]{:S(2)}, u32[]{:S(2)}) %collective-permute-start) | collective-permute-done | bytes 1048608 | tf_op jit(solution)/shard_map/ppermute | solution.py:156
  75.6 0.0 copy-done
  75.6 0.2 slice_add_fusion
  75.8 1.9 %reshape.183 = f32[128,2,2,512]{3,2,1,0:T(2,128)} reshape(f32[256,1024]{1,0:T(8,128)S(1)} %slice_add_fusion) | data formatting | bytes 2097152 | tf_op jit(solution)/shard_map/reshape | solution.py:159
  77.7 10.4 %all-to-all-start = ((f32[128,2,2,512]{3,2,1,0:T(2,128)}), f32[128,2,2,512]{3,2,1,0:T(2,128)S(1)}, u32[]{:S(2)}, u32[]{:S(2)}) async-start(f32[128,2,2,512]{3,2,1,0:T(2,128)} %reshape.183), calls=%async_computation | async-start | bytes 2097152 | tf_op jit(solution)/shard_map/all_to_all | solution.py:158
  88.1 1.0 fusion.20
  89.1 1.1 sine_multiply_fusion
  90.1 0.1 maximum_maximum_fusion
  90.3 0.0 copy-done.2
  90.3 0.3 fusion.31
  90.6 17.2 %all-to-all-done = f32[128,2,2,512]{3,2,1,0:T(2,128)S(1)} async-done(((f32[128,2,2,512]{3,2,1,0:T(2,128)}), f32[128,2,2,512]{3,2,1,0:T(2,128)S(1)}, u32[]{:S(2)}, u32[]{:S(2)}) %all-to-all-start) | async-done | bytes 1048608 | tf_op jit(solution)/shard_map/all_to_all | solution.py:158
  107.9 0.4 reduce_sum.9
  108.2 0.1 multiply_add_fusion
  108.3 1.2 fusion.8
  109.5 0.1 copy.12
  109.6 0.9 broadcast_in_dim.2
  110.5 3.6 %all-to-all-start.1 = ((f32[128,4,2,128]{3,2,1,0:T(2,128)}), f32[128,4,2,128]{3,2,1,0:T(2,128)S(1)}, u32[]{:S(2)}, u32[]{:S(2)}) async-start(f32[128,4,2,128]{3,2,1,0:T(2,128)} %bitcast.11), calls=%async_computation.1 | async-start | bytes 1048576 | tf_op jit(solution)/shard_map/all_to_all | solution.py:186
  114.2 0.0 copy-start.1
  114.2 0.6 constant_dynamic-slice_fusion
  115.5 0.3 cosine_multiply_fusion.2
  115.8 12.7 %all-to-all-done.1 = f32[128,4,2,128]{3,2,1,0:T(2,128)S(1)} async-done(((f32[128,4,2,128]{3,2,1,0:T(2,128)}), f32[128,4,2,128]{3,2,1,0:T(2,128)S(1)}, u32[]{:S(2)}, u32[]{:S(2)}) %all-to-all-start.1) | async-done | bytes 524320 | tf_op jit(solution)/shard_map/all_to_all | solution.py:186
  128.5 0.4 fusion.58
  128.9 0.6 fusion
  129.5 0.6 broadcast_multiply_fusion
  (12 shorter events, 0.1 us)
Async XLA Ops:
  70.3 5.3 %copy-start = (f32[512,1024]{1,0:T(8,128)S(1)}, f32[512,1024]{1,0:T(8,128)}, u32[]{:S(2)}) copy-start(f32[512,1024]{1,0:T(8,128)} %shard_map.82) | copy-start | bytes 6291460
  71.8 3.8 %collective-permute-start = (f32[256,1024]{1,0:T(8,128)S(1)}, f32[256,1024]{1,0:T(8,128)S(1)}, u32[]{:S(2)}, u32[]{:S(2)}) collective-permute-start(f32[256,1024]{1,0:T(8,128)S(1)} %slice.29), channel_id=1, source_target_pairs={{0,4},{4,0},{8,12},{12,8},{16,20},{20,16},{24,28},{28,24},{32,36},... | collective-permute-start | bytes 3145736 | tf_op jit(solution)/shard_map/ppermute | solution.py:156
  77.6 12.6 %copy-start.2 = (s32[32,2]{0,1:T(2,128)S(1)}, s32[32,2]{0,1:T(2,128)}, u32[]{:S(2)}) copy-start(s32[32,2]{0,1:T(2,128)} %param.14) | copy-start | bytes 772
  77.7 30.2 %all-to-all-start = ((f32[128,2,2,512]{3,2,1,0:T(2,128)}), f32[128,2,2,512]{3,2,1,0:T(2,128)S(1)}, u32[]{:S(2)}, u32[]{:S(2)}) async-start(f32[128,2,2,512]{3,2,1,0:T(2,128)} %reshape.183), calls=%async_computation | async-start | bytes 2097152 | tf_op jit(solution)/shard_map/all_to_all | solution.py:158
  110.5 17.9 %all-to-all-start.1 = ((f32[128,4,2,128]{3,2,1,0:T(2,128)}), f32[128,4,2,128]{3,2,1,0:T(2,128)S(1)}, u32[]{:S(2)}, u32[]{:S(2)}) async-start(f32[128,4,2,128]{3,2,1,0:T(2,128)} %bitcast.11), calls=%async_computation.1 | async-start | bytes 1048576 | tf_op jit(solution)/shard_map/all_to_all | solution.py:186
  114.2 15.3 %copy-start.1 = (f32[1,32,128]{2,1,0:T(8,128)S(1)}, f32[1,32,128]{2,1,0:T(8,128)}, u32[]{:S(2)}) copy-start(f32[1,32,128]{2,1,0:T(8,128)} %param.15) | copy-start | bytes 49156

commit v8 on v6

--- a/solution.py
+++ b/solution.py
@@ -27,7 +27,7 @@
 def patch_kernel(place_ref, coords_ref, values_ref, phase_ref, out_ref):
     step = coords_ref.shape[0]
     cells = lax.broadcasted_iota(jnp.int32, (PATCH, 1), 0).astype(jnp.float32)
-    slot = lax.broadcasted_iota(jnp.int32, (PATCH, 128), 1) // PATCH
+    pad = jnp.zeros((PATCH, 128 - PATCH), jnp.float32)
     half = out_ref.shape[1] // 2
     per_group = 128 // PATCH
 
@@ -66,11 +66,11 @@
         row_tile = tile // (SG // PATCH)
         col_tile = tile % (SG // PATCH)
         rows = pl.ds(pl.multiple_of(row_tile * PATCH, PATCH), PATCH)
-        keep = slot == col_tile % per_group
+        shift = (col_tile % per_group) * PATCH
         for part, values in enumerate(phased):
             start = pl.multiple_of(part * half + (col_tile // per_group) * 128, 128)
-            spread = jnp.concatenate([values] * per_group, axis=1)
-            out_ref[rows, pl.ds(start, 128)] += jnp.where(keep, spread, 0.0)
+            padded = jnp.concatenate([values, pad], axis=1)
+            out_ref[rows, pl.ds(start, 128)] += pltpu.roll(padded, shift, 1)
         return carry
 
     lax.fori_loop(0, step, one_block, 0)

time: 125 us -> 131 us (1.048)
  Pallas kernels: 61 us -> 66.8 us
    pallas_call x1, Pallas kernels: 61 us -> 66.8 us  [make_phased_grid(): pl.pallas_call(patch_kernel, grid_spec=pltpu.PrefetchScalarGridSpec(num_s...]
where the time goes in v8:
time: 131 us; the launch traced here: 130 us
  Pallas kernels  66.8 us (51%)
  waiting for transfers between devices  32.2 us (25%)
  starting transfers between devices  15.6 us (12%)
  other arithmetic  6.93 us (5%)
  local copies, waits for them, and re-layouts  5.52 us (4%)
  matrix products  1.76 us (1%)
  between operations  1.5 us (1%)
    pallas_call x1, Pallas kernels, make_phased_grid(): pl.pallas_call(patch_kernel, grid_spec=pltpu.PrefetchScalarGridSpec(num_s...  66.8 us
    all_to_all x1, waiting for transfers between devices, body(): lax.all_to_all(chip_half.reshape(devices, half_chunk, 2, SG), ('tm', 'sub...  17.2 us
    all_to_all x1, waiting for transfers between devices, body(): lax.all_to_all(windows, ('tm', 'sub'), split_axis=0, concat_axis=0, tiled...  12.7 us
    all_to_all x1, starting transfers between devices, body(): lax.all_to_all(chip_half.reshape(devices, half_chunk, 2, SG), ('tm', 'sub...  10.4 us
    all_to_all x1, starting transfers between devices, body(): lax.all_to_all(windows, ('tm', 'sub'), split_axis=0, concat_axis=0, tiled...  3.64 us
  transfers between devices with their start and end apart: 3, of which 3 were waited for; matrix products, arithmetic and copies ran while one was open for 3% of the time, Pallas kernels for 0%

profile of v8, /device:TPU:1, one launch (start us, length us, event | category | flops | bytes accessed | tf_op | source)
XLA Modules:
  0.0 130.3 jit_solution(15866429508290832525)
XLA Ops:
  0.0 0.7 fusion.33
  0.7 0.1 copy.11
  1.4 0.2 cosine_multiply_fusion.1
  1.7 0.7 pad_maximum_fusion.phase_ref
  2.4 1.2 fusion.50.place_ref
  3.6 66.8 %shard_map.82 = f32[512,1024]{1,0:T(8,128)} custom-call(s32[128]{0:T(128)} %fusion.50.place_ref, f32[128,2,1024]{2,1,0:T(2,128)} %coords_ref.1, f32[128,2,1024]{2,1,0:T(2,128)} %values_ref.1, f32[128,64]{1,0:T(8,128)} %pad_maximum_fusion.phase_ref), custom_call_target="tpu_custom_call" | custom-call | flops 4294967296 | bytes 4194304 | tf_op jit(solution)/shard_map/pallas_call | solution.py:87
  70.4 1.5 %slice.29 = f32[256,1024]{1,0:T(8,128)S(1)} slice(f32[512,1024]{1,0:T(8,128)} %shard_map.82), slice={[256:512], [0:1024]} | slice | bytes 2097152 | tf_op jit(solution)/shard_map/slice | solution.py:150
  71.9 1.5 %collective-permute-start = (f32[256,1024]{1,0:T(8,128)S(1)}, f32[256,1024]{1,0:T(8,128)S(1)}, u32[]{:S(2)}, u32[]{:S(2)}) collective-permute-start(f32[256,1024]{1,0:T(8,128)S(1)} %slice.29), channel_id=1, source_target_pairs={{0,4},{4,0},{8,12},{12,8},{16,20},{20,16},{24,28},{28,24},{32,36},... | collective-permute-start | bytes 3145736 | tf_op jit(solution)/shard_map/ppermute | solution.py:150
  73.4 2.3 %collective-permute-done = f32[256,1024]{1,0:T(8,128)S(1)} collective-permute-done((f32[256,1024]{1,0:T(8,128)S(1)}, f32[256,1024]{1,0:T(8,128)S(1)}, u32[]{:S(2)}, u32[]{:S(2)}) %collective-permute-start) | collective-permute-done | bytes 1048608 | tf_op jit(solution)/shard_map/ppermute | solution.py:150
  75.7 0.0 copy-done
  75.7 0.2 slice_add_fusion
  75.9 1.9 %reshape.183 = f32[128,2,2,512]{3,2,1,0:T(2,128)} reshape(f32[256,1024]{1,0:T(8,128)S(1)} %slice_add_fusion) | data formatting | bytes 2097152 | tf_op jit(solution)/shard_map/reshape | solution.py:153
  77.8 10.4 %all-to-all-start = ((f32[128,2,2,512]{3,2,1,0:T(2,128)}), f32[128,2,2,512]{3,2,1,0:T(2,128)S(1)}, u32[]{:S(2)}, u32[]{:S(2)}) async-start(f32[128,2,2,512]{3,2,1,0:T(2,128)} %reshape.183), calls=%async_computation | async-start | bytes 2097152 | tf_op jit(solution)/shard_map/all_to_all | solution.py:152
  88.2 1.0 fusion.20
  89.2 1.1 sine_multiply_fusion
  90.3 0.1 maximum_maximum_fusion
  90.4 0.3 fusion.31
  90.8 17.2 %all-to-all-done = f32[128,2,2,512]{3,2,1,0:T(2,128)S(1)} async-done(((f32[128,2,2,512]{3,2,1,0:T(2,128)}), f32[128,2,2,512]{3,2,1,0:T(2,128)S(1)}, u32[]{:S(2)}, u32[]{:S(2)}) %all-to-all-start) | async-done | bytes 1048608 | tf_op jit(solution)/shard_map/all_to_all | solution.py:152
  108.0 0.4 reduce_sum.9
  108.3 0.1 multiply_add_fusion
  108.4 1.2 fusion.8
  109.6 0.1 copy.12
  109.7 0.9 broadcast_in_dim.2
  110.7 3.6 %all-to-all-start.1 = ((f32[128,4,2,128]{3,2,1,0:T(2,128)}), f32[128,4,2,128]{3,2,1,0:T(2,128)S(1)}, u32[]{:S(2)}, u32[]{:S(2)}) async-start(f32[128,4,2,128]{3,2,1,0:T(2,128)} %bitcast.11), calls=%async_computation.1 | async-start | bytes 1048576 | tf_op jit(solution)/shard_map/all_to_all | solution.py:180
  114.3 0.0 copy-start.1
  114.3 0.6 constant_dynamic-slice_fusion
  115.6 0.3 cosine_multiply_fusion.2
  115.9 12.7 %all-to-all-done.1 = f32[128,4,2,128]{3,2,1,0:T(2,128)S(1)} async-done(((f32[128,4,2,128]{3,2,1,0:T(2,128)}), f32[128,4,2,128]{3,2,1,0:T(2,128)S(1)}, u32[]{:S(2)}, u32[]{:S(2)}) %all-to-all-start.1) | async-done | bytes 524320 | tf_op jit(solution)/shard_map/all_to_all | solution.py:180
  128.6 0.4 fusion.58
  129.0 0.6 fusion
  129.6 0.0 copy-done.1
  129.7 0.6 broadcast_multiply_fusion
  (12 shorter events, 0.1 us)
Async XLA Ops:
  70.4 5.3 %copy-start = (f32[512,1024]{1,0:T(8,128)S(1)}, f32[512,1024]{1,0:T(8,128)}, u32[]{:S(2)}) copy-start(f32[512,1024]{1,0:T(8,128)} %shard_map.82) | copy-start | bytes 6291460
  71.9 3.8 %collective-permute-start = (f32[256,1024]{1,0:T(8,128)S(1)}, f32[256,1024]{1,0:T(8,128)S(1)}, u32[]{:S(2)}, u32[]{:S(2)}) collective-permute-start(f32[256,1024]{1,0:T(8,128)S(1)} %slice.29), channel_id=1, source_target_pairs={{0,4},{4,0},{8,12},{12,8},{16,20},{20,16},{24,28},{28,24},{32,36},... | collective-permute-start | bytes 3145736 | tf_op jit(solution)/shard_map/ppermute | solution.py:150
  77.8 12.6 %copy-start.2 = (s32[32,2]{0,1:T(2,128)S(1)}, s32[32,2]{0,1:T(2,128)}, u32[]{:S(2)}) copy-start(s32[32,2]{0,1:T(2,128)} %param.14) | copy-start | bytes 772
  77.8 30.2 %all-to-all-start = ((f32[128,2,2,512]{3,2,1,0:T(2,128)}), f32[128,2,2,512]{3,2,1,0:T(2,128)S(1)}, u32[]{:S(2)}, u32[]{:S(2)}) async-start(f32[128,2,2,512]{3,2,1,0:T(2,128)} %reshape.183), calls=%async_computation | async-start | bytes 2097152 | tf_op jit(solution)/shard_map/all_to_all | solution.py:152
  110.7 17.9 %all-to-all-start.1 = ((f32[128,4,2,128]{3,2,1,0:T(2,128)}), f32[128,4,2,128]{3,2,1,0:T(2,128)S(1)}, u32[]{:S(2)}, u32[]{:S(2)}) async-start(f32[128,4,2,128]{3,2,1,0:T(2,128)} %bitcast.11), calls=%async_computation.1 | async-start | bytes 1048576 | tf_op jit(solution)/shard_map/all_to_all | solution.py:180
  114.3 15.3 %copy-start.1 = (f32[1,32,128]{2,1,0:T(8,128)S(1)}, f32[1,32,128]{2,1,0:T(8,128)}, u32[]{:S(2)}) copy-start(f32[1,32,128]{2,1,0:T(8,128)} %param.15) | copy-start | bytes 49156

commit v9 on v8

--- a/solution.py
+++ b/solution.py
@@ -26,10 +26,9 @@
 
 def patch_kernel(place_ref, coords_ref, values_ref, phase_ref, out_ref):
     step = coords_ref.shape[0]
+    width = 2 * PATCH
     cells = lax.broadcasted_iota(jnp.int32, (PATCH, 1), 0).astype(jnp.float32)
-    pad = jnp.zeros((PATCH, 128 - PATCH), jnp.float32)
-    half = out_ref.shape[1] // 2
-    per_group = 128 // PATCH
+    lane_half = lax.broadcasted_iota(jnp.int32, (PATCH, 2 * width), 1) // width
 
     @pl.when(pl.program_id(0) == 0)
     def _():
@@ -49,28 +48,19 @@
             (((1,), (1,)), ((), ())),
             preferred_element_type=jnp.float32,
         )
-        width = 2 * PATCH
-        plain = (both[:PATCH, :width] + both[:PATCH, width:]) + (
-            both[PATCH:, :width] + both[PATCH:, width:]
-        )
-        real_part = plain[:, :PATCH]
-        imag_part = plain[:, PATCH:]
+        both = both + pltpu.roll(both, width, 1)
+        plain = both[:PATCH] + both[PATCH:]
+        swapped = pltpu.roll(plain, PATCH, 1)
         phase = phase_ref[pl.ds(i, 1), :]
-        cos_b = phase[:, :PATCH]
-        sin_b = phase[:, PATCH:]
-        phased = (
-            real_part * cos_b + imag_part * sin_b,
-            imag_part * cos_b - real_part * sin_b,
-        )
+        phased = plain * phase[:, : 2 * width] + swapped * phase[:, 2 * width :]
         tile = place_ref[pl.program_id(0) * step + i]
         row_tile = tile // (SG // PATCH)
         col_tile = tile % (SG // PATCH)
         rows = pl.ds(pl.multiple_of(row_tile * PATCH, PATCH), PATCH)
-        shift = (col_tile % per_group) * PATCH
-        for part, values in enumerate(phased):
-            start = pl.multiple_of(part * half + (col_tile // per_group) * 128, 128)
-            padded = jnp.concatenate([values, pad], axis=1)
-            out_ref[rows, pl.ds(start, 128)] += pltpu.roll(padded, shift, 1)
+        start = pl.multiple_of((col_tile // 2) * 2 * width, 2 * width)
+        out_ref[rows, pl.ds(start, 2 * width)] += jnp.where(
+            lane_half == col_tile % 2, phased, 0.0
+        )
         return carry
 
     lax.fori_loop(0, step, one_block, 0)
@@ -82,7 +72,11 @@
     phase = (jnp.arange(PATCH, dtype=jnp.int32)[None, :] * local[:, None]) % SG_PER
     angle = phase.astype(jnp.float32) * (2.0 * math.pi / SG_PER)
     keep = live.astype(jnp.float32)[:, None]
-    phases = jnp.concatenate([jnp.cos(angle) * keep, jnp.sin(angle) * keep], axis=1)
+    cos_b = jnp.cos(angle) * keep
+    sin_b = jnp.sin(angle) * keep
+    phases = jnp.concatenate(
+        [cos_b, cos_b, cos_b, cos_b, sin_b, -sin_b, sin_b, -sin_b], axis=1
+    )
     spec = pl.BlockSpec((step, 2, VIS), lambda i, place: (i, 0, 0))
     return pl.pallas_call(
         patch_kernel,
@@ -92,7 +86,7 @@
             in_specs=[
                 spec,
                 spec,
-                pl.BlockSpec((step, 2 * PATCH), lambda i, place: (i, 0)),
+                pl.BlockSpec((step, 8 * PATCH), lambda i, place: (i, 0)),
             ],
             out_specs=pl.BlockSpec((SG, 2 * SG), lambda i, place: (0, 0)),
         ),
@@ -158,7 +152,10 @@
     )
     grid_rows = jnp.sum(
         arrived.reshape(n_tm // 2, 2, n_sub, half_chunk, 2, SG), axis=(0, 2)
-    ).reshape(chunk, 2 * SG)
+    )
+    grid_rows = (
+        grid_rows.reshape(chunk, col_tiles, 2, PATCH).transpose(0, 2, 1, 3).reshape(chunk, 2 * SG)
+    )
     offsets = jnp.clip(facet_offsets, 0, SG - FS)
     cs = jnp.arange(SG, dtype=jnp.int32)
     shift = ((offsets[:, 1][:, None] * cs[None, :]) % SG).astype(jnp.float32) * (

time: 131 us -> 114 us (0.87)
  Pallas kernels: 66.8 us -> 49.4 us
    pallas_call x1, Pallas kernels: 66.8 us -> 49.4 us  [make_phased_grid(): pl.pallas_call(patch_kernel, grid_spec=pltpu.PrefetchScalarGridSpec(num_s...]
where the time goes in v9:
time: 114 us; the launch traced here: 113 us
  Pallas kernels  49.4 us (43%)
  waiting for transfers between devices  32.2 us (28%)
  starting transfers between devices  15.6 us (14%)
  local copies, waits for them, and re-layouts  6.54 us (6%)
  other arithmetic  6.23 us (5%)
  matrix products  1.76 us (2%)
  between operations  1.51 us (1%)
    pallas_call x1, Pallas kernels, make_phased_grid(): pl.pallas_call(patch_kernel, grid_spec=pltpu.PrefetchScalarGridSpec(num_s...  49.4 us
    all_to_all x1, waiting for transfers between devices, body(): lax.all_to_all(chip_half.reshape(devices, half_chunk, 2, SG), ('tm', 'sub...  17.2 us
    all_to_all x1, waiting for transfers between devices, body(): lax.all_to_all(windows, ('tm', 'sub'), split_axis=0, concat_axis=0, tiled...  12.7 us
    all_to_all x1, starting transfers between devices, body(): lax.all_to_all(chip_half.reshape(devices, half_chunk, 2, SG), ('tm', 'sub...  10.4 us
    all_to_all x1, starting transfers between devices, body(): lax.all_to_all(windows, ('tm', 'sub'), split_axis=0, concat_axis=0, tiled...  3.64 us
    ppermute x1, waiting for transfers between devices, body(): chip_half = grid[:SG // 2] + lax.ppermute(grid[SG // 2:], 'tm', pair)  2.29 us
  transfers between devices with their start and end apart: 3, of which 3 were waited for; matrix products, arithmetic and copies ran while one was open for 3% of the time, Pallas kernels for 0%

profile of v9, /device:TPU:1, one launch (start us, length us, event | category | flops | bytes accessed | tf_op | source)
XLA Modules:
  0.0 113.2 jit_solution(14609368953351361708)
XLA Ops:
  0.0 0.7 fusion.33
  0.7 0.1 copy.16
  1.4 0.3 fusion.58
  1.7 1.2 %fusion.50.place_ref = s32[128]{0:T(128)} fusion(s32[128,1]{0,1:T(1,128)} %param.10, s32[128]{0:T(128)} %param.12, s32[]{:T(128)S(6)} %mul.277), kind=kLoop, calls=%fused_computation.98 | loop fusion | flops 5888 | bytes 1540 | tf_op jit(solution)/shard_map/add | solution.py:140
  2.9 0.8 concatenate.30.phase_ref
  3.7 49.4 %shard_map.82 = f32[512,1024]{1,0:T(8,128)} custom-call(s32[128]{0:T(128)} %fusion.50.place_ref, f32[128,2,1024]{2,1,0:T(2,128)} %coords_ref.1, f32[128,2,1024]{2,1,0:T(2,128)} %values_ref.1, f32[128,256]{1,0:T(8,128)} %concatenate.30.phase_ref), custom_call_target="tpu_custom_call" | custom-call | flops 4294967296 | bytes 4194304 | tf_op jit(solution)/shard_map/pallas_call | solution.py:81
  53.1 1.5 %slice.29 = f32[256,1024]{1,0:T(8,128)S(1)} slice(f32[512,1024]{1,0:T(8,128)} %shard_map.82), slice={[256:512], [0:1024]} | slice | bytes 2097152 | tf_op jit(solution)/shard_map/slice | solution.py:144
  54.6 1.5 %collective-permute-start = (f32[256,1024]{1,0:T(8,128)S(1)}, f32[256,1024]{1,0:T(8,128)S(1)}, u32[]{:S(2)}, u32[]{:S(2)}) collective-permute-start(f32[256,1024]{1,0:T(8,128)S(1)} %slice.29), channel_id=1, source_target_pairs={{0,4},{4,0},{8,12},{12,8},{16,20},{20,16},{24,28},{28,24},{32,36},... | collective-permute-start | bytes 3145736 | tf_op jit(solution)/shard_map/ppermute | solution.py:144
  56.1 2.3 %collective-permute-done = f32[256,1024]{1,0:T(8,128)S(1)} collective-permute-done((f32[256,1024]{1,0:T(8,128)S(1)}, f32[256,1024]{1,0:T(8,128)S(1)}, u32[]{:S(2)}, u32[]{:S(2)}) %collective-permute-start) | collective-permute-done | bytes 1048608 | tf_op jit(solution)/shard_map/ppermute | solution.py:144
  58.4 0.2 slice_add_fusion
  58.6 1.9 %reshape.186 = f32[128,2,2,512]{3,2,1,0:T(2,128)} reshape(f32[256,1024]{1,0:T(8,128)S(1)} %slice_add_fusion) | data formatting | bytes 2097152 | tf_op jit(solution)/shard_map/reshape | solution.py:147
  60.4 10.4 %all-to-all-start = ((f32[128,2,2,512]{3,2,1,0:T(2,128)}), f32[128,2,2,512]{3,2,1,0:T(2,128)S(1)}, u32[]{:S(2)}, u32[]{:S(2)}) async-start(f32[128,2,2,512]{3,2,1,0:T(2,128)} %reshape.186), calls=%async_computation | async-start | bytes 2097152 | tf_op jit(solution)/shard_map/all_to_all | solution.py:146
  70.9 1.0 fusion.20
  71.9 1.1 sine_multiply_fusion
  72.9 0.1 maximum_maximum_fusion
  73.1 0.3 fusion.31
  73.4 17.2 %all-to-all-done = f32[128,2,2,512]{3,2,1,0:T(2,128)S(1)} async-done(((f32[128,2,2,512]{3,2,1,0:T(2,128)}), f32[128,2,2,512]{3,2,1,0:T(2,128)S(1)}, u32[]{:S(2)}, u32[]{:S(2)}) %all-to-all-start) | async-done | bytes 1048608 | tf_op jit(solution)/shard_map/all_to_all | solution.py:146
  90.7 0.4 reduce_sum.9
  91.0 0.1 reshape.188
  91.1 0.1 reshape.189
  91.2 0.1 multiply_add_fusion
  91.3 1.2 %fusion.8 = f32[32,4,2,128]{3,0,2,1:T(8,128)S(1)} fusion(f32[2,128,1024,1]{2,1,0,3:T(8,128)S(1)} %bitcast.32, f32[32,1,4,512]{3,0,2,1:T(8,128)S(1)} %get-tuple-element.10, f32[32,1,4,512]{3,0,2,1:T(8,128)S(1)} %get-tuple-element.9), kind=kOutput, calls=%fused_computation.11 | convolution fusion | flops 402784256 | bytes 1703936 | tf_op jit(solution)/shard_map/dot_general | solution.py:171
  92.5 0.1 copy.18
  92.6 0.9 broadcast_in_dim.2
  93.6 3.6 %all-to-all-start.1 = ((f32[128,4,2,128]{3,2,1,0:T(2,128)}), f32[128,4,2,128]{3,2,1,0:T(2,128)S(1)}, u32[]{:S(2)}, u32[]{:S(2)}) async-start(f32[128,4,2,128]{3,2,1,0:T(2,128)} %bitcast.12), calls=%async_computation.1 | async-start | bytes 1048576 | tf_op jit(solution)/shard_map/all_to_all | solution.py:177
  97.2 0.0 copy-start.1
  97.2 0.6 constant_dynamic-slice_fusion
  98.5 0.3 cosine_multiply_fusion.2
  98.8 12.7 %all-to-all-done.1 = f32[128,4,2,128]{3,2,1,0:T(2,128)S(1)} async-done(((f32[128,4,2,128]{3,2,1,0:T(2,128)}), f32[128,4,2,128]{3,2,1,0:T(2,128)S(1)}, u32[]{:S(2)}, u32[]{:S(2)}) %all-to-all-start.1) | async-done | bytes 524320 | tf_op jit(solution)/shard_map/all_to_all | solution.py:177
  111.5 0.4 fusion.59
  111.9 0.6 fusion
  112.6 0.6 broadcast_multiply_fusion
  (14 shorter events, 0.1 us)
Async XLA Ops:
  53.1 5.3 %copy-start = (f32[512,1024]{1,0:T(8,128)S(1)}, f32[512,1024]{1,0:T(8,128)}, u32[]{:S(2)}) copy-start(f32[512,1024]{1,0:T(8,128)} %shard_map.82) | copy-start | bytes 6291460
  54.6 3.8 %collective-permute-start = (f32[256,1024]{1,0:T(8,128)S(1)}, f32[256,1024]{1,0:T(8,128)S(1)}, u32[]{:S(2)}, u32[]{:S(2)}) collective-permute-start(f32[256,1024]{1,0:T(8,128)S(1)} %slice.29), channel_id=1, source_target_pairs={{0,4},{4,0},{8,12},{12,8},{16,20},{20,16},{24,28},{28,24},{32,36},... | collective-permute-start | bytes 3145736 | tf_op jit(solution)/shard_map/ppermute | solution.py:144
  60.4 12.6 %copy-start.2 = (s32[32,2]{0,1:T(2,128)S(1)}, s32[32,2]{0,1:T(2,128)}, u32[]{:S(2)}) copy-start(s32[32,2]{0,1:T(2,128)} %param.14) | copy-start | bytes 772
  60.4 30.2 %all-to-all-start = ((f32[128,2,2,512]{3,2,1,0:T(2,128)}), f32[128,2,2,512]{3,2,1,0:T(2,128)S(1)}, u32[]{:S(2)}, u32[]{:S(2)}) async-start(f32[128,2,2,512]{3,2,1,0:T(2,128)} %reshape.186), calls=%async_computation | async-start | bytes 2097152 | tf_op jit(solution)/shard_map/all_to_all | solution.py:146
  93.6 17.9 %all-to-all-start.1 = ((f32[128,4,2,128]{3,2,1,0:T(2,128)}), f32[128,4,2,128]{3,2,1,0:T(2,128)S(1)}, u32[]{:S(2)}, u32[]{:S(2)}) async-start(f32[128,4,2,128]{3,2,1,0:T(2,128)} %bitcast.12), calls=%async_computation.1 | async-start | bytes 1048576 | tf_op jit(solution)/shard_map/all_to_all | solution.py:177
  97.2 15.3 %copy-start.1 = (f32[1,32,128]{2,1,0:T(8,128)S(1)}, f32[1,32,128]{2,1,0:T(8,128)}, u32[]{:S(2)}) copy-start(f32[1,32,128]{2,1,0:T(8,128)} %param.15) | copy-start | bytes 49156

commit v10 on v9

--- a/solution.py
+++ b/solution.py
@@ -68,7 +68,7 @@
 
 def make_phased_grid(vis_coords, vis_values, live, local, tile_id):
     count = vis_coords.shape[0]
-    step = 8
+    step = 32
     phase = (jnp.arange(PATCH, dtype=jnp.int32)[None, :] * local[:, None]) % SG_PER
     angle = phase.astype(jnp.float32) * (2.0 * math.pi / SG_PER)
     keep = live.astype(jnp.float32)[:, None]

time: 114 us -> 113 us (level)
  no operation moved by 1% of the time
where the time goes in v10:
time: 113 us
  Pallas kernels  49.4 us (44%)
  waiting for transfers between devices  32.2 us (28%)
  starting transfers between devices  15.6 us (14%)
  local copies, waits for them, and re-layouts  6.54 us (6%)
  other arithmetic  6.23 us (6%)
  matrix products  1.76 us (2%)
  between operations  1.51 us (1%)
    pallas_call x1, Pallas kernels, make_phased_grid(): pl.pallas_call(patch_kernel, grid_spec=pltpu.PrefetchScalarGridSpec(num_s...  49.4 us
    all_to_all x1, waiting for transfers between devices, body(): lax.all_to_all(chip_half.reshape(devices, half_chunk, 2, SG), ('tm', 'sub...  17.2 us
    all_to_all x1, waiting for transfers between devices, body(): lax.all_to_all(windows, ('tm', 'sub'), split_axis=0, concat_axis=0, tiled...  12.7 us
    all_to_all x1, starting transfers between devices, body(): lax.all_to_all(chip_half.reshape(devices, half_chunk, 2, SG), ('tm', 'sub...  10.4 us
    all_to_all x1, starting transfers between devices, body(): lax.all_to_all(windows, ('tm', 'sub'), split_axis=0, concat_axis=0, tiled...  3.64 us
    ppermute x1, waiting for transfers between devices, body(): chip_half = grid[:SG // 2] + lax.ppermute(grid[SG // 2:], 'tm', pair)  2.29 us
  transfers between devices with their start and end apart: 3, of which 3 were waited for; matrix products, arithmetic and copies ran while one was open for 3% of the time, Pallas kernels for 0%

profile of v10, /device:TPU:1, one launch (start us, length us, event | category | flops | bytes accessed | tf_op | source)
XLA Modules:
  0.0 113.2 jit_solution(6708019550622792318)
XLA Ops:
  0.0 0.7 fusion.33
  0.7 0.1 copy.16
  1.4 0.3 fusion.58
  1.7 1.2 %fusion.50.place_ref = s32[128]{0:T(128)} fusion(s32[128,1]{0,1:T(1,128)} %param.10, s32[128]{0:T(128)} %param.12, s32[]{:T(128)S(6)} %mul.277), kind=kLoop, calls=%fused_computation.98 | loop fusion | flops 5888 | bytes 1540 | tf_op jit(solution)/shard_map/add | solution.py:140
  2.9 0.8 concatenate.30.phase_ref
  3.7 49.4 %shard_map.82 = f32[512,1024]{1,0:T(8,128)} custom-call(s32[128]{0:T(128)} %fusion.50.place_ref, f32[128,2,1024]{2,1,0:T(2,128)} %coords_ref.1, f32[128,2,1024]{2,1,0:T(2,128)} %values_ref.1, f32[128,256]{1,0:T(8,128)} %concatenate.30.phase_ref), custom_call_target="tpu_custom_call" | custom-call | flops 4294967296 | bytes 4194304 | tf_op jit(solution)/shard_map/pallas_call | solution.py:81
  53.1 1.5 %slice.29 = f32[256,1024]{1,0:T(8,128)S(1)} slice(f32[512,1024]{1,0:T(8,128)} %shard_map.82), slice={[256:512], [0:1024]} | slice | bytes 2097152 | tf_op jit(solution)/shard_map/slice | solution.py:144
  54.6 1.5 %collective-permute-start = (f32[256,1024]{1,0:T(8,128)S(1)}, f32[256,1024]{1,0:T(8,128)S(1)}, u32[]{:S(2)}, u32[]{:S(2)}) collective-permute-start(f32[256,1024]{1,0:T(8,128)S(1)} %slice.29), channel_id=1, source_target_pairs={{0,4},{4,0},{8,12},{12,8},{16,20},{20,16},{24,28},{28,24},{32,36},... | collective-permute-start | bytes 3145736 | tf_op jit(solution)/shard_map/ppermute | solution.py:144
  56.1 2.3 %collective-permute-done = f32[256,1024]{1,0:T(8,128)S(1)} collective-permute-done((f32[256,1024]{1,0:T(8,128)S(1)}, f32[256,1024]{1,0:T(8,128)S(1)}, u32[]{:S(2)}, u32[]{:S(2)}) %collective-permute-start) | collective-permute-done | bytes 1048608 | tf_op jit(solution)/shard_map/ppermute | solution.py:144
  58.4 0.2 slice_add_fusion
  58.6 1.9 %reshape.186 = f32[128,2,2,512]{3,2,1,0:T(2,128)} reshape(f32[256,1024]{1,0:T(8,128)S(1)} %slice_add_fusion) | data formatting | bytes 2097152 | tf_op jit(solution)/shard_map/reshape | solution.py:147
  60.4 10.4 %all-to-all-start = ((f32[128,2,2,512]{3,2,1,0:T(2,128)}), f32[128,2,2,512]{3,2,1,0:T(2,128)S(1)}, u32[]{:S(2)}, u32[]{:S(2)}) async-start(f32[128,2,2,512]{3,2,1,0:T(2,128)} %reshape.186), calls=%async_computation | async-start | bytes 2097152 | tf_op jit(solution)/shard_map/all_to_all | solution.py:146
  70.9 1.0 fusion.20
  71.9 1.1 sine_multiply_fusion
  72.9 0.1 maximum_maximum_fusion
  73.1 0.3 fusion.31
  73.4 17.2 %all-to-all-done = f32[128,2,2,512]{3,2,1,0:T(2,128)S(1)} async-done(((f32[128,2,2,512]{3,2,1,0:T(2,128)}), f32[128,2,2,512]{3,2,1,0:T(2,128)S(1)}, u32[]{:S(2)}, u32[]{:S(2)}) %all-to-all-start) | async-done | bytes 1048608 | tf_op jit(solution)/shard_map/all_to_all | solution.py:146
  90.7 0.4 reduce_sum.9
  91.0 0.1 reshape.188
  91.1 0.1 reshape.189
  91.2 0.1 multiply_add_fusion
  91.3 1.2 %fusion.8 = f32[32,4,2,128]{3,0,2,1:T(8,128)S(1)} fusion(f32[2,128,1024,1]{2,1,0,3:T(8,128)S(1)} %bitcast.32, f32[32,1,4,512]{3,0,2,1:T(8,128)S(1)} %get-tuple-element.10, f32[32,1,4,512]{3,0,2,1:T(8,128)S(1)} %get-tuple-element.9), kind=kOutput, calls=%fused_computation.11 | convolution fusion | flops 402784256 | bytes 1703936 | tf_op jit(solution)/shard_map/dot_general | solution.py:171
  92.5 0.1 copy.18
  92.6 0.9 broadcast_in_dim.2
  93.6 3.6 %all-to-all-start.1 = ((f32[128,4,2,128]{3,2,1,0:T(2,128)}), f32[128,4,2,128]{3,2,1,0:T(2,128)S(1)}, u32[]{:S(2)}, u32[]{:S(2)}) async-start(f32[128,4,2,128]{3,2,1,0:T(2,128)} %bitcast.12), calls=%async_computation.1 | async-start | bytes 1048576 | tf_op jit(solution)/shard_map/all_to_all | solution.py:177
  97.2 0.0 copy-start.1
  97.2 0.6 constant_dynamic-slice_fusion
  98.5 0.3 cosine_multiply_fusion.2
  98.8 12.7 %all-to-all-done.1 = f32[128,4,2,128]{3,2,1,0:T(2,128)S(1)} async-done(((f32[128,4,2,128]{3,2,1,0:T(2,128)}), f32[128,4,2,128]{3,2,1,0:T(2,128)S(1)}, u32[]{:S(2)}, u32[]{:S(2)}) %all-to-all-start.1) | async-done | bytes 524320 | tf_op jit(solution)/shard_map/all_to_all | solution.py:177
  111.5 0.4 fusion.59
  111.9 0.6 fusion
  112.6 0.6 broadcast_multiply_fusion
  (14 shorter events, 0.1 us)
Async XLA Ops:
  53.1 5.3 %copy-start = (f32[512,1024]{1,0:T(8,128)S(1)}, f32[512,1024]{1,0:T(8,128)}, u32[]{:S(2)}) copy-start(f32[512,1024]{1,0:T(8,128)} %shard_map.82) | copy-start | bytes 6291460
  54.6 3.8 %collective-permute-start = (f32[256,1024]{1,0:T(8,128)S(1)}, f32[256,1024]{1,0:T(8,128)S(1)}, u32[]{:S(2)}, u32[]{:S(2)}) collective-permute-start(f32[256,1024]{1,0:T(8,128)S(1)} %slice.29), channel_id=1, source_target_pairs={{0,4},{4,0},{8,12},{12,8},{16,20},{20,16},{24,28},{28,24},{32,36},... | collective-permute-start | bytes 3145736 | tf_op jit(solution)/shard_map/ppermute | solution.py:144
  60.4 12.6 %copy-start.2 = (s32[32,2]{0,1:T(2,128)S(1)}, s32[32,2]{0,1:T(2,128)}, u32[]{:S(2)}) copy-start(s32[32,2]{0,1:T(2,128)} %param.14) | copy-start | bytes 772
  60.4 30.2 %all-to-all-start = ((f32[128,2,2,512]{3,2,1,0:T(2,128)}), f32[128,2,2,512]{3,2,1,0:T(2,128)S(1)}, u32[]{:S(2)}, u32[]{:S(2)}) async-start(f32[128,2,2,512]{3,2,1,0:T(2,128)} %reshape.186), calls=%async_computation | async-start | bytes 2097152 | tf_op jit(solution)/shard_map/all_to_all | solution.py:146
  93.6 17.9 %all-to-all-start.1 = ((f32[128,4,2,128]{3,2,1,0:T(2,128)}), f32[128,4,2,128]{3,2,1,0:T(2,128)S(1)}, u32[]{:S(2)}, u32[]{:S(2)}) async-start(f32[128,4,2,128]{3,2,1,0:T(2,128)} %bitcast.12), calls=%async_computation.1 | async-start | bytes 1048576 | tf_op jit(solution)/shard_map/all_to_all | solution.py:177
  97.2 15.3 %copy-start.1 = (f32[1,32,128]{2,1,0:T(8,128)S(1)}, f32[1,32,128]{2,1,0:T(8,128)}, u32[]{:S(2)}) copy-start(f32[1,32,128]{2,1,0:T(8,128)} %param.15) | copy-start | bytes 49156

commit v11 on v9

--- a/solution.py
+++ b/solution.py
@@ -63,7 +63,7 @@
         )
         return carry
 
-    lax.fori_loop(0, step, one_block, 0)
+    lax.fori_loop(0, step, one_block, 0, unroll=2)
 
 
 def make_phased_grid(vis_coords, vis_values, live, local, tile_id):

time: 114 us -> 96.9 us (0.85)
  Pallas kernels: 49.4 us -> 32.8 us
    pallas_call x1, Pallas kernels: 49.4 us -> 32.8 us  [make_phased_grid(): pl.pallas_call(patch_kernel, grid_spec=pltpu.PrefetchScalarGridSpec(num_s...]
  transfers between devices with their start and end apart: 3 -> 3, of which waited for: 3 -> 3; matrix products, arithmetic and copies ran while one was open for 3% -> 4% of each run, Pallas kernels for 0% -> 0%
where the time goes in v11:
time: 96.9 us; the launch traced here: 96.6 us
  Pallas kernels  32.8 us (34%)
  waiting for transfers between devices  32.2 us (33%)
  starting transfers between devices  15.6 us (16%)
  local copies, waits for them, and re-layouts  6.54 us (7%)
  other arithmetic  6.23 us (6%)
  matrix products  1.77 us (2%)
  between operations  1.51 us (2%)
    pallas_call x1, Pallas kernels, make_phased_grid(): pl.pallas_call(patch_kernel, grid_spec=pltpu.PrefetchScalarGridSpec(num_s...  32.8 us
    all_to_all x1, waiting for transfers between devices, body(): lax.all_to_all(chip_half.reshape(devices, half_chunk, 2, SG), ('tm', 'sub...  17.2 us
    all_to_all x1, waiting for transfers between devices, body(): lax.all_to_all(windows, ('tm', 'sub'), split_axis=0, concat_axis=0, tiled...  12.7 us
    all_to_all x1, starting transfers between devices, body(): lax.all_to_all(chip_half.reshape(devices, half_chunk, 2, SG), ('tm', 'sub...  10.4 us
    all_to_all x1, starting transfers between devices, body(): lax.all_to_all(windows, ('tm', 'sub'), split_axis=0, concat_axis=0, tiled...  3.64 us
    ppermute x1, waiting for transfers between devices, body(): chip_half = grid[:SG // 2] + lax.ppermute(grid[SG // 2:], 'tm', pair)  2.29 us
  transfers between devices with their start and end apart: 3, of which 3 were waited for; matrix products, arithmetic and copies ran while one was open for 4% of the time, Pallas kernels for 0%

profile of v11, /device:TPU:1, one launch (start us, length us, event | category | flops | bytes accessed | tf_op | source)
XLA Modules:
  0.0 96.6 jit_solution(15337725112396556712)
XLA Ops:
  0.0 0.7 fusion.33
  0.7 0.1 copy.16
  1.4 0.3 fusion.58
  1.7 1.2 %fusion.50.place_ref = s32[128]{0:T(128)} fusion(s32[128,1]{0,1:T(1,128)} %param.10, s32[128]{0:T(128)} %param.12, s32[]{:T(128)S(6)} %mul.277), kind=kLoop, calls=%fused_computation.98 | loop fusion | flops 5888 | bytes 1540 | tf_op jit(solution)/shard_map/add | solution.py:140
  2.9 0.8 concatenate.30.phase_ref
  3.7 32.8 %shard_map.82 = f32[512,1024]{1,0:T(8,128)} custom-call(s32[128]{0:T(128)} %fusion.50.place_ref, f32[128,2,1024]{2,1,0:T(2,128)} %coords_ref.1, f32[128,2,1024]{2,1,0:T(2,128)} %values_ref.1, f32[128,256]{1,0:T(8,128)} %concatenate.30.phase_ref), custom_call_target="tpu_custom_call" | custom-call | flops 4294967296 | bytes 4194304 | tf_op jit(solution)/shard_map/pallas_call | solution.py:81
  36.6 1.5 %slice.29 = f32[256,1024]{1,0:T(8,128)S(1)} slice(f32[512,1024]{1,0:T(8,128)} %shard_map.82), slice={[256:512], [0:1024]} | slice | bytes 2097152 | tf_op jit(solution)/shard_map/slice | solution.py:144
  38.0 1.5 %collective-permute-start = (f32[256,1024]{1,0:T(8,128)S(1)}, f32[256,1024]{1,0:T(8,128)S(1)}, u32[]{:S(2)}, u32[]{:S(2)}) collective-permute-start(f32[256,1024]{1,0:T(8,128)S(1)} %slice.29), channel_id=1, source_target_pairs={{0,4},{4,0},{8,12},{12,8},{16,20},{20,16},{24,28},{28,24},{32,36},... | collective-permute-start | bytes 3145736 | tf_op jit(solution)/shard_map/ppermute | solution.py:144
  39.5 2.3 %collective-permute-done = f32[256,1024]{1,0:T(8,128)S(1)} collective-permute-done((f32[256,1024]{1,0:T(8,128)S(1)}, f32[256,1024]{1,0:T(8,128)S(1)}, u32[]{:S(2)}, u32[]{:S(2)}) %collective-permute-start) | collective-permute-done | bytes 1048608 | tf_op jit(solution)/shard_map/ppermute | solution.py:144
  41.8 0.2 slice_add_fusion
  42.0 1.9 %reshape.186 = f32[128,2,2,512]{3,2,1,0:T(2,128)} reshape(f32[256,1024]{1,0:T(8,128)S(1)} %slice_add_fusion) | data formatting | bytes 2097152 | tf_op jit(solution)/shard_map/reshape | solution.py:147
  43.9 10.4 %all-to-all-start = ((f32[128,2,2,512]{3,2,1,0:T(2,128)}), f32[128,2,2,512]{3,2,1,0:T(2,128)S(1)}, u32[]{:S(2)}, u32[]{:S(2)}) async-start(f32[128,2,2,512]{3,2,1,0:T(2,128)} %reshape.186), calls=%async_computation | async-start | bytes 2097152 | tf_op jit(solution)/shard_map/all_to_all | solution.py:146
  54.3 1.0 %fusion.20 = f32[512,128]{0,1:T(8,128)S(1)} fusion(), kind=kLoop, calls=%fused_computation.33 | loop fusion | flops 1048576 | bytes 262144 | tf_op jit(solution)/shard_map/neg | solution.py:110
  55.3 1.1 %sine_multiply_fusion = (f32[512,128]{0,1:T(8,128)S(1)}, f32[512,128]{0,1:T(8,128)S(1)}) fusion(), kind=kLoop, calls=%fused_computation.20 | loop fusion | flops 1048576 | bytes 524288 | tf_op jit(solution)/shard_map/mul | solution.py:108
  56.4 0.1 maximum_maximum_fusion
  56.5 0.3 fusion.31
  56.9 17.2 %all-to-all-done = f32[128,2,2,512]{3,2,1,0:T(2,128)S(1)} async-done(((f32[128,2,2,512]{3,2,1,0:T(2,128)}), f32[128,2,2,512]{3,2,1,0:T(2,128)S(1)}, u32[]{:S(2)}, u32[]{:S(2)}) %all-to-all-start) | async-done | bytes 1048608 | tf_op jit(solution)/shard_map/all_to_all | solution.py:146
  74.1 0.4 reduce_sum.9
  74.4 0.1 reshape.188
  74.6 0.1 reshape.189
  74.7 0.1 multiply_add_fusion
  74.8 1.2 %fusion.8 = f32[32,4,2,128]{3,0,2,1:T(8,128)S(1)} fusion(f32[2,128,1024,1]{2,1,0,3:T(8,128)S(1)} %bitcast.32, f32[32,1,4,512]{3,0,2,1:T(8,128)S(1)} %get-tuple-element.10, f32[32,1,4,512]{3,0,2,1:T(8,128)S(1)} %get-tuple-element.9), kind=kOutput, calls=%fused_computation.11 | convolution fusion | flops 402784256 | bytes 1703936 | tf_op jit(solution)/shard_map/dot_general | solution.py:171
  75.9 0.1 copy.18
  76.1 0.9 broadcast_in_dim.2
  77.0 3.6 %all-to-all-start.1 = ((f32[128,4,2,128]{3,2,1,0:T(2,128)}), f32[128,4,2,128]{3,2,1,0:T(2,128)S(1)}, u32[]{:S(2)}, u32[]{:S(2)}) async-start(f32[128,4,2,128]{3,2,1,0:T(2,128)} %bitcast.12), calls=%async_computation.1 | async-start | bytes 1048576 | tf_op jit(solution)/shard_map/all_to_all | solution.py:177
  80.6 0.0 copy-start.1
  80.7 0.6 constant_dynamic-slice_fusion
  81.9 0.3 cosine_multiply_fusion.2
  82.3 12.7 %all-to-all-done.1 = f32[128,4,2,128]{3,2,1,0:T(2,128)S(1)} async-done(((f32[128,4,2,128]{3,2,1,0:T(2,128)}), f32[128,4,2,128]{3,2,1,0:T(2,128)S(1)}, u32[]{:S(2)}, u32[]{:S(2)}) %all-to-all-start.1) | async-done | bytes 524320 | tf_op jit(solution)/shard_map/all_to_all | solution.py:177
  94.9 0.4 fusion.59
  95.4 0.6 fusion
  96.0 0.6 broadcast_multiply_fusion
  (14 shorter events, 0.1 us)
Async XLA Ops:
  36.6 5.3 %copy-start = (f32[512,1024]{1,0:T(8,128)S(1)}, f32[512,1024]{1,0:T(8,128)}, u32[]{:S(2)}) copy-start(f32[512,1024]{1,0:T(8,128)} %shard_map.82) | copy-start | bytes 6291460
  38.0 3.8 %collective-permute-start = (f32[256,1024]{1,0:T(8,128)S(1)}, f32[256,1024]{1,0:T(8,128)S(1)}, u32[]{:S(2)}, u32[]{:S(2)}) collective-permute-start(f32[256,1024]{1,0:T(8,128)S(1)} %slice.29), channel_id=1, source_target_pairs={{0,4},{4,0},{8,12},{12,8},{16,20},{20,16},{24,28},{28,24},{32,36},... | collective-permute-start | bytes 3145736 | tf_op jit(solution)/shard_map/ppermute | solution.py:144
  43.9 12.6 %copy-start.2 = (s32[32,2]{0,1:T(2,128)S(1)}, s32[32,2]{0,1:T(2,128)}, u32[]{:S(2)}) copy-start(s32[32,2]{0,1:T(2,128)} %param.14) | copy-start | bytes 772
  43.9 30.2 %all-to-all-start = ((f32[128,2,2,512]{3,2,1,0:T(2,128)}), f32[128,2,2,512]{3,2,1,0:T(2,128)S(1)}, u32[]{:S(2)}, u32[]{:S(2)}) async-start(f32[128,2,2,512]{3,2,1,0:T(2,128)} %reshape.186), calls=%async_computation | async-start | bytes 2097152 | tf_op jit(solution)/shard_map/all_to_all | solution.py:146
  77.0 17.9 %all-to-all-start.1 = ((f32[128,4,2,128]{3,2,1,0:T(2,128)}), f32[128,4,2,128]{3,2,1,0:T(2,128)S(1)}, u32[]{:S(2)}, u32[]{:S(2)}) async-start(f32[128,4,2,128]{3,2,1,0:T(2,128)} %bitcast.12), calls=%async_computation.1 | async-start | bytes 1048576 | tf_op jit(solution)/shard_map/all_to_all | solution.py:177
  80.6 15.3 %copy-start.1 = (f32[1,32,128]{2,1,0:T(8,128)S(1)}, f32[1,32,128]{2,1,0:T(8,128)}, u32[]{:S(2)}) copy-start(f32[1,32,128]{2,1,0:T(8,128)} %param.15) | copy-start | bytes 49156

commit v12 on v11

--- a/solution.py
+++ b/solution.py
@@ -63,7 +63,7 @@
         )
         return carry
 
-    lax.fori_loop(0, step, one_block, 0, unroll=2)
+    lax.fori_loop(0, step, one_block, 0, unroll=4)
 
 
 def make_phased_grid(vis_coords, vis_values, live, local, tile_id):

time: 96.9 us -> 88.5 us (0.913)
  Pallas kernels: 32.8 us -> 24.3 us
    pallas_call x1, Pallas kernels: 32.8 us -> 24.3 us  [make_phased_grid(): pl.pallas_call(patch_kernel, grid_spec=pltpu.PrefetchScalarGridSpec(num_s...]
where the time goes in v12:
time: 88.5 us; the launch traced here: 88.1 us
  waiting for transfers between devices  32.2 us (36%)
  Pallas kernels  24.3 us (27%)
  starting transfers between devices  15.6 us (18%)
  local copies, waits for them, and re-layouts  6.54 us (7%)
  other arithmetic  6.23 us (7%)
  matrix products  1.77 us (2%)
  between operations  1.51 us (2%)
    pallas_call x1, Pallas kernels, make_phased_grid(): pl.pallas_call(patch_kernel, grid_spec=pltpu.PrefetchScalarGridSpec(num_s...  24.3 us
    all_to_all x1, waiting for transfers between devices, body(): lax.all_to_all(chip_half.reshape(devices, half_chunk, 2, SG), ('tm', 'sub...  17.2 us
    all_to_all x1, waiting for transfers between devices, body(): lax.all_to_all(windows, ('tm', 'sub'), split_axis=0, concat_axis=0, tiled...  12.7 us
    all_to_all x1, starting transfers between devices, body(): lax.all_to_all(chip_half.reshape(devices, half_chunk, 2, SG), ('tm', 'sub...  10.4 us
    all_to_all x1, starting transfers between devices, body(): lax.all_to_all(windows, ('tm', 'sub'), split_axis=0, concat_axis=0, tiled...  3.63 us
    ppermute x1, waiting for transfers between devices, body(): chip_half = grid[:SG // 2] + lax.ppermute(grid[SG // 2:], 'tm', pair)  2.29 us
    reshape x1, local copies, waits for them, and re-layouts, body(): chip_half.reshape(devices, half_chunk, 2, SG)  1.86 us
  transfers between devices with their start and end apart: 3, of which 3 were waited for; matrix products, arithmetic and copies ran while one was open for 4% of the time, Pallas kernels for 0%

profile of v12, /device:TPU:1, one launch (start us, length us, event | category | flops | bytes accessed | tf_op | source)
XLA Modules:
  0.0 88.1 jit_solution(11739059734017970083)
XLA Ops:
  0.0 0.7 fusion.33
  0.7 0.1 copy.16
  1.4 0.3 fusion.58
  1.7 1.2 %fusion.50.place_ref = s32[128]{0:T(128)} fusion(s32[128,1]{0,1:T(1,128)} %param.10, s32[128]{0:T(128)} %param.12, s32[]{:T(128)S(6)} %mul.277), kind=kLoop, calls=%fused_computation.98 | loop fusion | flops 5888 | bytes 1540 | tf_op jit(solution)/shard_map/add | solution.py:140
  2.9 0.8 concatenate.30.phase_ref
  3.7 24.3 %shard_map.82 = f32[512,1024]{1,0:T(8,128)} custom-call(s32[128]{0:T(128)} %fusion.50.place_ref, f32[128,2,1024]{2,1,0:T(2,128)} %coords_ref.1, f32[128,2,1024]{2,1,0:T(2,128)} %values_ref.1, f32[128,256]{1,0:T(8,128)} %concatenate.30.phase_ref), custom_call_target="tpu_custom_call" | custom-call | flops 4294967296 | bytes 4194304 | tf_op jit(solution)/shard_map/pallas_call | solution.py:81
  28.1 1.5 %slice.29 = f32[256,1024]{1,0:T(8,128)S(1)} slice(f32[512,1024]{1,0:T(8,128)} %shard_map.82), slice={[256:512], [0:1024]} | slice | bytes 2097152 | tf_op jit(solution)/shard_map/slice | solution.py:144
  29.6 1.5 %collective-permute-start = (f32[256,1024]{1,0:T(8,128)S(1)}, f32[256,1024]{1,0:T(8,128)S(1)}, u32[]{:S(2)}, u32[]{:S(2)}) collective-permute-start(f32[256,1024]{1,0:T(8,128)S(1)} %slice.29), channel_id=1, source_target_pairs={{0,4},{4,0},{8,12},{12,8},{16,20},{20,16},{24,28},{28,24},{32,36},... | collective-permute-start | bytes 3145736 | tf_op jit(solution)/shard_map/ppermute | solution.py:144
  31.1 2.3 %collective-permute-done = f32[256,1024]{1,0:T(8,128)S(1)} collective-permute-done((f32[256,1024]{1,0:T(8,128)S(1)}, f32[256,1024]{1,0:T(8,128)S(1)}, u32[]{:S(2)}, u32[]{:S(2)}) %collective-permute-start) | collective-permute-done | bytes 1048608 | tf_op jit(solution)/shard_map/ppermute | solution.py:144
  33.3 0.2 slice_add_fusion
  33.5 1.9 %reshape.186 = f32[128,2,2,512]{3,2,1,0:T(2,128)} reshape(f32[256,1024]{1,0:T(8,128)S(1)} %slice_add_fusion) | data formatting | bytes 2097152 | tf_op jit(solution)/shard_map/reshape | solution.py:147
  35.4 10.4 %all-to-all-start = ((f32[128,2,2,512]{3,2,1,0:T(2,128)}), f32[128,2,2,512]{3,2,1,0:T(2,128)S(1)}, u32[]{:S(2)}, u32[]{:S(2)}) async-start(f32[128,2,2,512]{3,2,1,0:T(2,128)} %reshape.186), calls=%async_computation | async-start | bytes 2097152 | tf_op jit(solution)/shard_map/all_to_all | solution.py:146
  45.8 1.0 %fusion.20 = f32[512,128]{0,1:T(8,128)S(1)} fusion(), kind=kLoop, calls=%fused_computation.33 | loop fusion | flops 1048576 | bytes 262144 | tf_op jit(solution)/shard_map/neg | solution.py:110
  46.8 1.1 %sine_multiply_fusion = (f32[512,128]{0,1:T(8,128)S(1)}, f32[512,128]{0,1:T(8,128)S(1)}) fusion(), kind=kLoop, calls=%fused_computation.20 | loop fusion | flops 1048576 | bytes 524288 | tf_op jit(solution)/shard_map/mul | solution.py:108
  47.9 0.1 maximum_maximum_fusion
  48.0 0.3 fusion.31
  48.4 17.2 %all-to-all-done = f32[128,2,2,512]{3,2,1,0:T(2,128)S(1)} async-done(((f32[128,2,2,512]{3,2,1,0:T(2,128)}), f32[128,2,2,512]{3,2,1,0:T(2,128)S(1)}, u32[]{:S(2)}, u32[]{:S(2)}) %all-to-all-start) | async-done | bytes 1048608 | tf_op jit(solution)/shard_map/all_to_all | solution.py:146
  65.6 0.4 reduce_sum.9
  66.0 0.1 reshape.188
  66.1 0.1 reshape.189
  66.2 0.1 multiply_add_fusion
  66.3 1.2 %fusion.8 = f32[32,4,2,128]{3,0,2,1:T(8,128)S(1)} fusion(f32[2,128,1024,1]{2,1,0,3:T(8,128)S(1)} %bitcast.32, f32[32,1,4,512]{3,0,2,1:T(8,128)S(1)} %get-tuple-element.10, f32[32,1,4,512]{3,0,2,1:T(8,128)S(1)} %get-tuple-element.9), kind=kOutput, calls=%fused_computation.11 | convolution fusion | flops 402784256 | bytes 1703936 | tf_op jit(solution)/shard_map/dot_general | solution.py:171
  67.5 0.1 copy.18
  67.6 0.9 %broadcast_in_dim.2 = f32[32,4,4,2,128]{4,3,2,1,0:T(2,128)} broadcast(f32[32,4,2,128]{3,2,1,0:T(2,128)S(1)} %copy.18), dimensions={0,2,3,4} | broadcast | bytes 655360 | tf_op jit(solution)/shard_map/broadcast_in_dim | solution.py:174
  68.5 3.6 %all-to-all-start.1 = ((f32[128,4,2,128]{3,2,1,0:T(2,128)}), f32[128,4,2,128]{3,2,1,0:T(2,128)S(1)}, u32[]{:S(2)}, u32[]{:S(2)}) async-start(f32[128,4,2,128]{3,2,1,0:T(2,128)} %bitcast.12), calls=%async_computation.1 | async-start | bytes 1048576 | tf_op jit(solution)/shard_map/all_to_all | solution.py:177
  72.2 0.0 copy-start.1
  72.2 0.6 constant_dynamic-slice_fusion
  73.4 0.3 cosine_multiply_fusion.2
  73.8 12.7 %all-to-all-done.1 = f32[128,4,2,128]{3,2,1,0:T(2,128)S(1)} async-done(((f32[128,4,2,128]{3,2,1,0:T(2,128)}), f32[128,4,2,128]{3,2,1,0:T(2,128)S(1)}, u32[]{:S(2)}, u32[]{:S(2)}) %all-to-all-start.1) | async-done | bytes 524320 | tf_op jit(solution)/shard_map/all_to_all | solution.py:177
  86.4 0.4 fusion.59
  86.9 0.6 fusion
  87.5 0.6 broadcast_multiply_fusion
  (14 shorter events, 0.1 us)
Async XLA Ops:
  28.1 5.3 %copy-start = (f32[512,1024]{1,0:T(8,128)S(1)}, f32[512,1024]{1,0:T(8,128)}, u32[]{:S(2)}) copy-start(f32[512,1024]{1,0:T(8,128)} %shard_map.82) | copy-start | bytes 6291460
  29.6 3.8 %collective-permute-start = (f32[256,1024]{1,0:T(8,128)S(1)}, f32[256,1024]{1,0:T(8,128)S(1)}, u32[]{:S(2)}, u32[]{:S(2)}) collective-permute-start(f32[256,1024]{1,0:T(8,128)S(1)} %slice.29), channel_id=1, source_target_pairs={{0,4},{4,0},{8,12},{12,8},{16,20},{20,16},{24,28},{28,24},{32,36},... | collective-permute-start | bytes 3145736 | tf_op jit(solution)/shard_map/ppermute | solution.py:144
  35.4 12.6 %copy-start.2 = (s32[32,2]{0,1:T(2,128)S(1)}, s32[32,2]{0,1:T(2,128)}, u32[]{:S(2)}) copy-start(s32[32,2]{0,1:T(2,128)} %param.14) | copy-start | bytes 772
  35.4 30.2 %all-to-all-start = ((f32[128,2,2,512]{3,2,1,0:T(2,128)}), f32[128,2,2,512]{3,2,1,0:T(2,128)S(1)}, u32[]{:S(2)}, u32[]{:S(2)}) async-start(f32[128,2,2,512]{3,2,1,0:T(2,128)} %reshape.186), calls=%async_computation | async-start | bytes 2097152 | tf_op jit(solution)/shard_map/all_to_all | solution.py:146
  68.5 17.9 %all-to-all-start.1 = ((f32[128,4,2,128]{3,2,1,0:T(2,128)}), f32[128,4,2,128]{3,2,1,0:T(2,128)S(1)}, u32[]{:S(2)}, u32[]{:S(2)}) async-start(f32[128,4,2,128]{3,2,1,0:T(2,128)} %bitcast.12), calls=%async_computation.1 | async-start | bytes 1048576 | tf_op jit(solution)/shard_map/all_to_all | solution.py:177
  72.2 15.3 %copy-start.1 = (f32[1,32,128]{2,1,0:T(8,128)S(1)}, f32[1,32,128]{2,1,0:T(8,128)}, u32[]{:S(2)}) copy-start(f32[1,32,128]{2,1,0:T(8,128)} %param.15) | copy-start | bytes 49156

commit v13 on v12

--- a/solution.py
+++ b/solution.py
@@ -63,7 +63,7 @@
         )
         return carry
 
-    lax.fori_loop(0, step, one_block, 0, unroll=4)
+    lax.fori_loop(0, step, one_block, 0, unroll=8)
 
 
 def make_phased_grid(vis_coords, vis_values, live, local, tile_id):

time: 88.5 us -> 84.4 us (0.954)
  Pallas kernels: 24.3 us -> 20.3 us
    pallas_call x1, Pallas kernels: 24.3 us -> 20.3 us  [make_phased_grid(): pl.pallas_call(patch_kernel, grid_spec=pltpu.PrefetchScalarGridSpec(num_s...]
where the time goes in v13:
time: 84.4 us; the launch traced here: 84.1 us
  waiting for transfers between devices  32.2 us (38%)
  Pallas kernels  20.3 us (24%)
  starting transfers between devices  15.6 us (18%)
  local copies, waits for them, and re-layouts  6.54 us (8%)
  other arithmetic  6.23 us (7%)
  matrix products  1.76 us (2%)
  between operations  1.51 us (2%)
    pallas_call x1, Pallas kernels, make_phased_grid(): pl.pallas_call(patch_kernel, grid_spec=pltpu.PrefetchScalarGridSpec(num_s...  20.3 us
    all_to_all x1, waiting for transfers between devices, body(): lax.all_to_all(chip_half.reshape(devices, half_chunk, 2, SG), ('tm', 'sub...  17.2 us
    all_to_all x1, waiting for transfers between devices, body(): lax.all_to_all(windows, ('tm', 'sub'), split_axis=0, concat_axis=0, tiled...  12.7 us
    all_to_all x1, starting transfers between devices, body(): lax.all_to_all(chip_half.reshape(devices, half_chunk, 2, SG), ('tm', 'sub...  10.4 us
    all_to_all x1, starting transfers between devices, body(): lax.all_to_all(windows, ('tm', 'sub'), split_axis=0, concat_axis=0, tiled...  3.64 us
    ppermute x1, waiting for transfers between devices, body(): chip_half = grid[:SG // 2] + lax.ppermute(grid[SG // 2:], 'tm', pair)  2.29 us
    reshape x1, local copies, waits for them, and re-layouts, body(): chip_half.reshape(devices, half_chunk, 2, SG)  1.86 us
  transfers between devices with their start and end apart: 3, of which 3 were waited for; matrix products, arithmetic and copies ran while one was open for 4% of the time, Pallas kernels for 0%

profile of v13, /device:TPU:1, one launch (start us, length us, event | category | flops | bytes accessed | tf_op | source)
XLA Modules:
  0.0 84.1 jit_solution(15349804756730793909)
XLA Ops:
  0.0 0.7 fusion.33
  0.7 0.1 copy.16
  1.4 0.3 fusion.58
  1.7 1.2 %fusion.50.place_ref = s32[128]{0:T(128)} fusion(s32[128,1]{0,1:T(1,128)} %param.10, s32[128]{0:T(128)} %param.12, s32[]{:T(128)S(6)} %mul.277), kind=kLoop, calls=%fused_computation.98 | loop fusion | flops 5888 | bytes 1540 | tf_op jit(solution)/shard_map/add | solution.py:140
  2.9 0.8 concatenate.30.phase_ref
  3.7 20.3 %shard_map.82 = f32[512,1024]{1,0:T(8,128)} custom-call(s32[128]{0:T(128)} %fusion.50.place_ref, f32[128,2,1024]{2,1,0:T(2,128)} %coords_ref.1, f32[128,2,1024]{2,1,0:T(2,128)} %values_ref.1, f32[128,256]{1,0:T(8,128)} %concatenate.30.phase_ref), custom_call_target="tpu_custom_call" | custom-call | flops 4294967296 | bytes 4194304 | tf_op jit(solution)/shard_map/pallas_call | solution.py:81
  24.0 1.5 %slice.29 = f32[256,1024]{1,0:T(8,128)S(1)} slice(f32[512,1024]{1,0:T(8,128)} %shard_map.82), slice={[256:512], [0:1024]} | slice | bytes 2097152 | tf_op jit(solution)/shard_map/slice | solution.py:144
  25.5 1.5 %collective-permute-start = (f32[256,1024]{1,0:T(8,128)S(1)}, f32[256,1024]{1,0:T(8,128)S(1)}, u32[]{:S(2)}, u32[]{:S(2)}) collective-permute-start(f32[256,1024]{1,0:T(8,128)S(1)} %slice.29), channel_id=1, source_target_pairs={{0,4},{4,0},{8,12},{12,8},{16,20},{20,16},{24,28},{28,24},{32,36},... | collective-permute-start | bytes 3145736 | tf_op jit(solution)/shard_map/ppermute | solution.py:144
  27.0 2.3 %collective-permute-done = f32[256,1024]{1,0:T(8,128)S(1)} collective-permute-done((f32[256,1024]{1,0:T(8,128)S(1)}, f32[256,1024]{1,0:T(8,128)S(1)}, u32[]{:S(2)}, u32[]{:S(2)}) %collective-permute-start) | collective-permute-done | bytes 1048608 | tf_op jit(solution)/shard_map/ppermute | solution.py:144
  29.3 0.2 slice_add_fusion
  29.5 1.9 %reshape.186 = f32[128,2,2,512]{3,2,1,0:T(2,128)} reshape(f32[256,1024]{1,0:T(8,128)S(1)} %slice_add_fusion) | data formatting | bytes 2097152 | tf_op jit(solution)/shard_map/reshape | solution.py:147
  31.3 10.4 %all-to-all-start = ((f32[128,2,2,512]{3,2,1,0:T(2,128)}), f32[128,2,2,512]{3,2,1,0:T(2,128)S(1)}, u32[]{:S(2)}, u32[]{:S(2)}) async-start(f32[128,2,2,512]{3,2,1,0:T(2,128)} %reshape.186), calls=%async_computation | async-start | bytes 2097152 | tf_op jit(solution)/shard_map/all_to_all | solution.py:146
  41.8 1.0 %fusion.20 = f32[512,128]{0,1:T(8,128)S(1)} fusion(), kind=kLoop, calls=%fused_computation.33 | loop fusion | flops 1048576 | bytes 262144 | tf_op jit(solution)/shard_map/neg | solution.py:110
  42.8 1.1 %sine_multiply_fusion = (f32[512,128]{0,1:T(8,128)S(1)}, f32[512,128]{0,1:T(8,128)S(1)}) fusion(), kind=kLoop, calls=%fused_computation.20 | loop fusion | flops 1048576 | bytes 524288 | tf_op jit(solution)/shard_map/mul | solution.py:108
  43.8 0.1 maximum_maximum_fusion
  44.0 0.3 fusion.31
  44.3 17.2 %all-to-all-done = f32[128,2,2,512]{3,2,1,0:T(2,128)S(1)} async-done(((f32[128,2,2,512]{3,2,1,0:T(2,128)}), f32[128,2,2,512]{3,2,1,0:T(2,128)S(1)}, u32[]{:S(2)}, u32[]{:S(2)}) %all-to-all-start) | async-done | bytes 1048608 | tf_op jit(solution)/shard_map/all_to_all | solution.py:146
  61.5 0.4 reduce_sum.9
  61.9 0.1 reshape.188
  62.0 0.1 reshape.189
  62.1 0.1 multiply_add_fusion
  62.2 1.2 %fusion.8 = f32[32,4,2,128]{3,0,2,1:T(8,128)S(1)} fusion(f32[2,128,1024,1]{2,1,0,3:T(8,128)S(1)} %bitcast.32, f32[32,1,4,512]{3,0,2,1:T(8,128)S(1)} %get-tuple-element.10, f32[32,1,4,512]{3,0,2,1:T(8,128)S(1)} %get-tuple-element.9), kind=kOutput, calls=%fused_computation.11 | convolution fusion | flops 402784256 | bytes 1703936 | tf_op jit(solution)/shard_map/dot_general | solution.py:171
  63.4 0.1 copy.18
  63.5 0.9 %broadcast_in_dim.2 = f32[32,4,4,2,128]{4,3,2,1,0:T(2,128)} broadcast(f32[32,4,2,128]{3,2,1,0:T(2,128)S(1)} %copy.18), dimensions={0,2,3,4} | broadcast | bytes 655360 | tf_op jit(solution)/shard_map/broadcast_in_dim | solution.py:174
  64.5 3.6 %all-to-all-start.1 = ((f32[128,4,2,128]{3,2,1,0:T(2,128)}), f32[128,4,2,128]{3,2,1,0:T(2,128)S(1)}, u32[]{:S(2)}, u32[]{:S(2)}) async-start(f32[128,4,2,128]{3,2,1,0:T(2,128)} %bitcast.12), calls=%async_computation.1 | async-start | bytes 1048576 | tf_op jit(solution)/shard_map/all_to_all | solution.py:177
  68.1 0.0 copy-start.1
  68.1 0.6 constant_dynamic-slice_fusion
  69.4 0.3 cosine_multiply_fusion.2
  69.7 12.7 %all-to-all-done.1 = f32[128,4,2,128]{3,2,1,0:T(2,128)S(1)} async-done(((f32[128,4,2,128]{3,2,1,0:T(2,128)}), f32[128,4,2,128]{3,2,1,0:T(2,128)S(1)}, u32[]{:S(2)}, u32[]{:S(2)}) %all-to-all-start.1) | async-done | bytes 524320 | tf_op jit(solution)/shard_map/all_to_all | solution.py:177
  82.4 0.4 fusion.59
  82.8 0.6 fusion
  83.5 0.6 broadcast_multiply_fusion
  (14 shorter events, 0.1 us)
Async XLA Ops:
  24.0 5.3 %copy-start = (f32[512,1024]{1,0:T(8,128)S(1)}, f32[512,1024]{1,0:T(8,128)}, u32[]{:S(2)}) copy-start(f32[512,1024]{1,0:T(8,128)} %shard_map.82) | copy-start | bytes 6291460
  25.5 3.8 %collective-permute-start = (f32[256,1024]{1,0:T(8,128)S(1)}, f32[256,1024]{1,0:T(8,128)S(1)}, u32[]{:S(2)}, u32[]{:S(2)}) collective-permute-start(f32[256,1024]{1,0:T(8,128)S(1)} %slice.29), channel_id=1, source_target_pairs={{0,4},{4,0},{8,12},{12,8},{16,20},{20,16},{24,28},{28,24},{32,36},... | collective-permute-start | bytes 3145736 | tf_op jit(solution)/shard_map/ppermute | solution.py:144
  31.3 12.6 %copy-start.2 = (s32[32,2]{0,1:T(2,128)S(1)}, s32[32,2]{0,1:T(2,128)}, u32[]{:S(2)}) copy-start(s32[32,2]{0,1:T(2,128)} %param.14) | copy-start | bytes 772
  31.3 30.2 %all-to-all-start = ((f32[128,2,2,512]{3,2,1,0:T(2,128)}), f32[128,2,2,512]{3,2,1,0:T(2,128)S(1)}, u32[]{:S(2)}, u32[]{:S(2)}) async-start(f32[128,2,2,512]{3,2,1,0:T(2,128)} %reshape.186), calls=%async_computation | async-start | bytes 2097152 | tf_op jit(solution)/shard_map/all_to_all | solution.py:146
  64.5 17.9 %all-to-all-start.1 = ((f32[128,4,2,128]{3,2,1,0:T(2,128)}), f32[128,4,2,128]{3,2,1,0:T(2,128)S(1)}, u32[]{:S(2)}, u32[]{:S(2)}) async-start(f32[128,4,2,128]{3,2,1,0:T(2,128)} %bitcast.12), calls=%async_computation.1 | async-start | bytes 1048576 | tf_op jit(solution)/shard_map/all_to_all | solution.py:177
  68.1 15.3 %copy-start.1 = (f32[1,32,128]{2,1,0:T(8,128)S(1)}, f32[1,32,128]{2,1,0:T(8,128)}, u32[]{:S(2)}) copy-start(f32[1,32,128]{2,1,0:T(8,128)} %param.15) | copy-start | bytes 49156

commit v14 on v13

--- a/solution.py
+++ b/solution.py
@@ -171,21 +171,16 @@
     windows = jnp.dot(shifted, window_table(), precision=lax.Precision.HIGHEST).reshape(
         n_tm, chunk, 2, FS
     )
-    windows = jnp.broadcast_to(
-        windows[:, None], (n_tm, n_sub, chunk, 2, FS)
-    ).reshape(devices, chunk, 2, FS)
-    gathered = lax.all_to_all(
-        windows, ("tm", "sub"), split_axis=0, concat_axis=0, tiled=True
-    ).reshape(SG, 2, FS)
+    gathered = lax.all_to_all(windows, "tm", split_axis=0, concat_axis=0, tiled=True)
+    gathered = gathered.reshape(n_tm * chunk, 2, FS)
 
     facet = lax.axis_index("tm")
     band = lax.axis_index("sub")
-    first_y = offsets[facet, 0] + band * facet_rows
-    ys = first_y + jnp.arange(facet_rows, dtype=jnp.int32)
-    order = jnp.arange(SG, dtype=jnp.int32)
+    ys = offsets[facet, 0] + jnp.arange(FS, dtype=jnp.int32)
+    order = jnp.arange(n_tm * chunk, dtype=jnp.int32)
     rs = (
         ((order // half_chunk) % 2) * (SG // 2)
-        + (order // chunk) * half_chunk
+        + ((order // chunk) * n_sub + band) * half_chunk
         + order % half_chunk
     )
     angle = ((ys[:, None] * rs[None, :]) % SG).astype(jnp.float32) * (2.0 * math.pi / SG)
@@ -200,9 +195,14 @@
         ],
         0,
     )
-    summed = jnp.dot(left, right, precision=lax.Precision.HIGHEST).reshape(
-        1, facet_rows, 2, FS
-    )
+    partial = jnp.dot(left, right, precision=lax.Precision.HIGHEST).reshape(
+        n_sub, facet_rows, 2, FS
+    )
+    summed = jnp.sum(
+        lax.all_to_all(partial, "sub", split_axis=0, concat_axis=0, tiled=True)
+        .reshape(n_sub, facet_rows, 2, FS),
+        axis=0,
+    )[None]
     return summed * correction[:, :, None, :]
 
 

time: 84.4 us -> 84.8 us (level)
  blocking collectives: 0 us -> 7.21 us
  waiting for transfers between devices: 32.2 us -> 25.6 us
    all_to_all x0 -> x1, blocking collectives: none -> 7.21 us  [body(): lax.all_to_all(partial, 'sub', split_axis=0, concat_axis=0, tiled=True)]
    all_to_all x1, waiting for transfers between devices: 12.7 us -> 7.36 us  [body(): lax.all_to_all(windows, 'tm', split_axis=0, concat_axis=0, tiled=True)]
    all_to_all x1, waiting for transfers between devices: 17.2 us -> 16 us  [body(): lax.all_to_all(chip_half.reshape(devices, half_chunk, 2, SG), ('tm', 'sub...]
    broadcast_in_dim x1 -> x0, local copies, waits for them, and re-layouts: 0.94 us -> none  [body(): jnp.broadcast_to(windows[:, None], (n_tm, n_sub, chunk, 2, FS))]
  transfers between devices with their start and end apart: 3 -> 3, of which waited for: 3 -> 3; matrix products, arithmetic and copies ran while one was open for 4% -> 5% of each run, Pallas kernels for 0% -> 0%
where the time goes in v14:
time: 84.8 us; the launch traced here: 84.2 us
  waiting for transfers between devices  25.6 us (30%)
  Pallas kernels  20.3 us (24%)
  starting transfers between devices  15.9 us (19%)
  blocking collectives  7.21 us (9%)
  other arithmetic  6.91 us (8%)
  local copies, waits for them, and re-layouts  5.95 us (7%)
  matrix products  1.46 us (2%)
  between operations  0.87 us (1%)
    pallas_call x1, Pallas kernels, make_phased_grid(): pl.pallas_call(patch_kernel, grid_spec=pltpu.PrefetchScalarGridSpec(num_s...  20.3 us
    all_to_all x1, waiting for transfers between devices, body(): lax.all_to_all(chip_half.reshape(devices, half_chunk, 2, SG), ('tm', 'sub...  16 us
    all_to_all x1, starting transfers between devices, body(): lax.all_to_all(chip_half.reshape(devices, half_chunk, 2, SG), ('tm', 'sub...  10.5 us
    all_to_all x1, waiting for transfers between devices, body(): lax.all_to_all(windows, 'tm', split_axis=0, concat_axis=0, tiled=True)  7.36 us
    all_to_all x1, blocking collectives, body(): lax.all_to_all(partial, 'sub', split_axis=0, concat_axis=0, tiled=True)  7.21 us
    all_to_all x1, starting transfers between devices, body(): lax.all_to_all(windows, 'tm', split_axis=0, concat_axis=0, tiled=True)  3.91 us
    ppermute x1, waiting for transfers between devices, body(): chip_half = grid[:SG // 2] + lax.ppermute(grid[SG // 2:], 'tm', pair)  2.29 us
    reshape x1, local copies, waits for them, and re-layouts, body(): chip_half.reshape(devices, half_chunk, 2, SG)  1.86 us
  transfers between devices with their start and end apart: 3, of which 3 were waited for; matrix products, arithmetic and copies ran while one was open for 5% of the time, Pallas kernels for 0%

profile of v14, /device:TPU:1, one launch (start us, length us, event | category | flops | bytes accessed | tf_op | source)
XLA Modules:
  0.0 84.2 jit_solution(3371862557928571240)
XLA Ops:
  0.0 0.7 fusion.33
  0.7 0.1 copy.16
  1.4 0.3 fusion.53
  1.7 1.2 %fusion.38.place_ref = s32[128]{0:T(128)} fusion(s32[128,1]{0,1:T(1,128)} %param.10, s32[128]{0:T(128)} %param.12, s32[]{:T(128)S(6)} %mul.263), kind=kLoop, calls=%fused_computation.89 | loop fusion | flops 5888 | bytes 1540 | tf_op jit(solution)/shard_map/add | solution.py:140
  2.9 0.8 concatenate.30.phase_ref
  3.7 20.3 %shard_map.82 = f32[512,1024]{1,0:T(8,128)} custom-call(s32[128]{0:T(128)} %fusion.38.place_ref, f32[128,2,1024]{2,1,0:T(2,128)} %coords_ref.1, f32[128,2,1024]{2,1,0:T(2,128)} %values_ref.1, f32[128,256]{1,0:T(8,128)} %concatenate.30.phase_ref), custom_call_target="tpu_custom_call" | custom-call | flops 4294967296 | bytes 4194304 | tf_op jit(solution)/shard_map/pallas_call | solution.py:81
  24.0 1.5 %slice.29 = f32[256,1024]{1,0:T(8,128)S(1)} slice(f32[512,1024]{1,0:T(8,128)} %shard_map.82), slice={[256:512], [0:1024]} | slice | bytes 2097152 | tf_op jit(solution)/shard_map/slice | solution.py:144
  25.5 1.5 %collective-permute-start = (f32[256,1024]{1,0:T(8,128)S(1)}, f32[256,1024]{1,0:T(8,128)S(1)}, u32[]{:S(2)}, u32[]{:S(2)}) collective-permute-start(f32[256,1024]{1,0:T(8,128)S(1)} %slice.29), channel_id=1, source_target_pairs={{0,4},{4,0},{8,12},{12,8},{16,20},{20,16},{24,28},{28,24},{32,36},... | collective-permute-start | bytes 3145736 | tf_op jit(solution)/shard_map/ppermute | solution.py:144
  27.0 2.3 %collective-permute-done = f32[256,1024]{1,0:T(8,128)S(1)} collective-permute-done((f32[256,1024]{1,0:T(8,128)S(1)}, f32[256,1024]{1,0:T(8,128)S(1)}, u32[]{:S(2)}, u32[]{:S(2)}) %collective-permute-start) | collective-permute-done | bytes 1048608 | tf_op jit(solution)/shard_map/ppermute | solution.py:144
  29.3 0.2 slice_add_fusion
  29.5 1.9 %reshape.151 = f32[128,2,2,512]{3,2,1,0:T(2,128)} reshape(f32[256,1024]{1,0:T(8,128)S(1)} %slice_add_fusion) | data formatting | bytes 2097152 | tf_op jit(solution)/shard_map/reshape | solution.py:147
  31.4 10.5 %all-to-all-start = ((f32[128,2,2,512]{3,2,1,0:T(2,128)}), f32[128,2,2,512]{3,2,1,0:T(2,128)S(1)}, u32[]{:S(2)}, u32[]{:S(2)}) async-start(f32[128,2,2,512]{3,2,1,0:T(2,128)} %reshape.151), calls=%async_computation | async-start | bytes 2097152 | tf_op jit(solution)/shard_map/all_to_all | solution.py:146
  41.8 0.6 constant_dynamic-slice_fusion
  42.4 0.7 fusion.37
  43.1 1.0 %fusion.20 = f32[512,128]{0,1:T(8,128)S(1)} fusion(), kind=kLoop, calls=%fused_computation.33 | loop fusion | flops 1048576 | bytes 262144 | tf_op jit(solution)/shard_map/neg | solution.py:110
  44.1 1.1 %sine_multiply_fusion = (f32[512,128]{0,1:T(8,128)S(1)}, f32[512,128]{0,1:T(8,128)S(1)}) fusion(), kind=kLoop, calls=%fused_computation.20 | loop fusion | flops 1048576 | bytes 524288 | tf_op jit(solution)/shard_map/mul | solution.py:108
  45.1 0.1 maximum_maximum_fusion
  45.3 0.3 fusion.31
  45.6 16.0 %all-to-all-done = f32[128,2,2,512]{3,2,1,0:T(2,128)S(1)} async-done(((f32[128,2,2,512]{3,2,1,0:T(2,128)}), f32[128,2,2,512]{3,2,1,0:T(2,128)S(1)}, u32[]{:S(2)}, u32[]{:S(2)}) %all-to-all-start) | async-done | bytes 1048608 | tf_op jit(solution)/shard_map/all_to_all | solution.py:146
  61.6 0.4 reduce_sum.20
  61.9 0.1 reshape.153
  62.1 0.1 reshape.154
  62.2 0.1 multiply_add_fusion
  62.3 1.2 %fusion = f32[32,4,2,128]{3,0,2,1:T(8,128)S(1)} fusion(f32[2,128,1024,1]{2,1,0,3:T(8,128)S(1)} %bitcast.35, f32[32,4,512]{2,0,1:T(8,128)S(1)} %get-tuple-element.8, f32[32,4,512]{2,0,1:T(8,128)S(1)} %get-tuple-element.7), kind=kOutput, calls=%fused_computation.3 | convolution fusion | flops 402784256 | bytes 1703936 | tf_op jit(solution)/shard_map/dot_general | solution.py:171
  63.4 0.7 copy.18
  64.2 3.9 %all-to-all-start.1 = ((f32[32,4,2,128]{3,2,1,0:T(2,128)}), f32[32,4,2,128]{3,2,1,0:T(2,128)S(1)}, u32[]{:S(2)}, u32[]{:S(2)}) async-start(f32[32,4,2,128]{3,2,1,0:T(2,128)} %copy.18), calls=%async_computation.1 | async-start | bytes 262144 | tf_op jit(solution)/shard_map/all_to_all | solution.py:174
  68.1 0.3 cosine_multiply_fusion.2
  68.5 7.4 %all-to-all-done.1 = f32[32,4,2,128]{3,2,1,0:T(2,128)S(1)} async-done(((f32[32,4,2,128]{3,2,1,0:T(2,128)}), f32[32,4,2,128]{3,2,1,0:T(2,128)S(1)}, u32[]{:S(2)}, u32[]{:S(2)}) %all-to-all-start.1) | async-done | bytes 131104 | tf_op jit(solution)/shard_map/all_to_all | solution.py:174
  75.9 0.3 fusion.6
  76.2 0.1 reshape.156
  76.2 7.2 %all_to_all.15 = f32[4,32,2,128]{3,2,1,0:T(2,128)S(1)} all-to-all(f32[4,32,2,128]{3,2,1,0:T(2,128)S(1)} %reshape.156), channel_id=1, replica_groups=mesh['tm'=32,'sub'=4] {'sub'}, dimensions={0} | all-to-all | bytes 262144 | tf_op jit(solution)/shard_map/all_to_all | solution.py:202
  83.5 0.6 bitcast_multiply_fusion
  (15 shorter events, 0.1 us)
Async XLA Ops:
  24.0 5.3 %copy-start = (f32[512,1024]{1,0:T(8,128)S(1)}, f32[512,1024]{1,0:T(8,128)}, u32[]{:S(2)}) copy-start(f32[512,1024]{1,0:T(8,128)} %shard_map.82) | copy-start | bytes 6291460
  25.5 3.8 %collective-permute-start = (f32[256,1024]{1,0:T(8,128)S(1)}, f32[256,1024]{1,0:T(8,128)S(1)}, u32[]{:S(2)}, u32[]{:S(2)}) collective-permute-start(f32[256,1024]{1,0:T(8,128)S(1)} %slice.29), channel_id=1, source_target_pairs={{0,4},{4,0},{8,12},{12,8},{16,20},{20,16},{24,28},{28,24},{32,36},... | collective-permute-start | bytes 3145736 | tf_op jit(solution)/shard_map/ppermute | solution.py:144
  29.5 12.3 %copy-start.2 = (s32[32,2]{0,1:T(2,128)S(1)}, s32[32,2]{0,1:T(2,128)}, u32[]{:S(2)}) copy-start(s32[32,2]{0,1:T(2,128)} %param.14) | copy-start | bytes 772
  31.4 30.2 %all-to-all-start = ((f32[128,2,2,512]{3,2,1,0:T(2,128)}), f32[128,2,2,512]{3,2,1,0:T(2,128)S(1)}, u32[]{:S(2)}, u32[]{:S(2)}) async-start(f32[128,2,2,512]{3,2,1,0:T(2,128)} %reshape.151), calls=%async_computation | async-start | bytes 2097152 | tf_op jit(solution)/shard_map/all_to_all | solution.py:146
  62.2 21.3 %copy-start.1 = (f32[1,32,128]{2,1,0:T(8,128)S(1)}, f32[1,32,128]{2,1,0:T(8,128)}, u32[]{:S(2)}) copy-start(f32[1,32,128]{2,1,0:T(8,128)} %param.15) | copy-start | bytes 49156
  64.2 11.6 %all-to-all-start.1 = ((f32[32,4,2,128]{3,2,1,0:T(2,128)}), f32[32,4,2,128]{3,2,1,0:T(2,128)S(1)}, u32[]{:S(2)}, u32[]{:S(2)}) async-start(f32[32,4,2,128]{3,2,1,0:T(2,128)} %copy.18), calls=%async_computation.1 | async-start | bytes 262144 | tf_op jit(solution)/shard_map/all_to_all | solution.py:174

commit v15 on v13

--- a/solution.py
+++ b/solution.py
@@ -63,12 +63,12 @@
         )
         return carry
 
-    lax.fori_loop(0, step, one_block, 0, unroll=8)
+    lax.fori_loop(0, step, one_block, 0, unroll=16)
 
 
 def make_phased_grid(vis_coords, vis_values, live, local, tile_id):
     count = vis_coords.shape[0]
-    step = 8
+    step = 16
     phase = (jnp.arange(PATCH, dtype=jnp.int32)[None, :] * local[:, None]) % SG_PER
     angle = phase.astype(jnp.float32) * (2.0 * math.pi / SG_PER)
     keep = live.astype(jnp.float32)[:, None]

time: 84.4 us -> 82.4 us (0.976)
  Pallas kernels: 20.3 us -> 18.3 us
    pallas_call x1, Pallas kernels: 20.3 us -> 18.3 us  [make_phased_grid(): pl.pallas_call(patch_kernel, grid_spec=pltpu.PrefetchScalarGridSpec(num_s...]
where the time goes in v15:
time: 82.4 us; the launch traced here: 82.1 us
  waiting for transfers between devices  32.2 us (39%)
  Pallas kernels  18.3 us (22%)
  starting transfers between devices  15.6 us (19%)
  local copies, waits for them, and re-layouts  6.54 us (8%)
  other arithmetic  6.23 us (8%)
  matrix products  1.77 us (2%)
  between operations  1.51 us (2%)
    pallas_call x1, Pallas kernels, make_phased_grid(): pl.pallas_call(patch_kernel, grid_spec=pltpu.PrefetchScalarGridSpec(num_s...  18.3 us
    all_to_all x1, waiting for transfers between devices, body(): lax.all_to_all(chip_half.reshape(devices, half_chunk, 2, SG), ('tm', 'sub...  17.2 us
    all_to_all x1, waiting for transfers between devices, body(): lax.all_to_all(windows, ('tm', 'sub'), split_axis=0, concat_axis=0, tiled...  12.7 us
    all_to_all x1, starting transfers between devices, body(): lax.all_to_all(chip_half.reshape(devices, half_chunk, 2, SG), ('tm', 'sub...  10.4 us
    all_to_all x1, starting transfers between devices, body(): lax.all_to_all(windows, ('tm', 'sub'), split_axis=0, concat_axis=0, tiled...  3.63 us
    ppermute x1, waiting for transfers between devices, body(): chip_half = grid[:SG // 2] + lax.ppermute(grid[SG // 2:], 'tm', pair)  2.29 us
    reshape x1, local copies, waits for them, and re-layouts, body(): chip_half.reshape(devices, half_chunk, 2, SG)  1.86 us
  transfers between devices with their start and end apart: 3, of which 3 were waited for; matrix products, arithmetic and copies ran while one was open for 4% of the time, Pallas kernels for 0%

profile of v15, /device:TPU:1, one launch (start us, length us, event | category | flops | bytes accessed | tf_op | source)
XLA Modules:
  0.0 82.1 jit_solution(5903018651098644912)
XLA Ops:
  0.0 0.7 fusion.33
  0.7 0.1 copy.16
  1.4 0.3 fusion.58
  1.7 1.2 %fusion.50.place_ref = s32[128]{0:T(128)} fusion(s32[128,1]{0,1:T(1,128)} %param.10, s32[128]{0:T(128)} %param.12, s32[]{:T(128)S(6)} %mul.277), kind=kLoop, calls=%fused_computation.98 | loop fusion | flops 5888 | bytes 1540 | tf_op jit(solution)/shard_map/add | solution.py:140
  2.9 0.8 concatenate.30.phase_ref
  3.7 18.3 %shard_map.82 = f32[512,1024]{1,0:T(8,128)} custom-call(s32[128]{0:T(128)} %fusion.50.place_ref, f32[128,2,1024]{2,1,0:T(2,128)} %coords_ref.1, f32[128,2,1024]{2,1,0:T(2,128)} %values_ref.1, f32[128,256]{1,0:T(8,128)} %concatenate.30.phase_ref), custom_call_target="tpu_custom_call" | custom-call | flops 4294967296 | bytes 4194304 | tf_op jit(solution)/shard_map/pallas_call | solution.py:81
  22.0 1.5 %slice.29 = f32[256,1024]{1,0:T(8,128)S(1)} slice(f32[512,1024]{1,0:T(8,128)} %shard_map.82), slice={[256:512], [0:1024]} | slice | bytes 2097152 | tf_op jit(solution)/shard_map/slice | solution.py:144
  23.5 1.5 %collective-permute-start = (f32[256,1024]{1,0:T(8,128)S(1)}, f32[256,1024]{1,0:T(8,128)S(1)}, u32[]{:S(2)}, u32[]{:S(2)}) collective-permute-start(f32[256,1024]{1,0:T(8,128)S(1)} %slice.29), channel_id=1, source_target_pairs={{0,4},{4,0},{8,12},{12,8},{16,20},{20,16},{24,28},{28,24},{32,36},... | collective-permute-start | bytes 3145736 | tf_op jit(solution)/shard_map/ppermute | solution.py:144
  25.0 2.3 %collective-permute-done = f32[256,1024]{1,0:T(8,128)S(1)} collective-permute-done((f32[256,1024]{1,0:T(8,128)S(1)}, f32[256,1024]{1,0:T(8,128)S(1)}, u32[]{:S(2)}, u32[]{:S(2)}) %collective-permute-start) | collective-permute-done | bytes 1048608 | tf_op jit(solution)/shard_map/ppermute | solution.py:144
  27.3 0.2 slice_add_fusion
  27.5 1.9 %reshape.186 = f32[128,2,2,512]{3,2,1,0:T(2,128)} reshape(f32[256,1024]{1,0:T(8,128)S(1)} %slice_add_fusion) | data formatting | bytes 2097152 | tf_op jit(solution)/shard_map/reshape | solution.py:147
  29.4 10.4 %all-to-all-start = ((f32[128,2,2,512]{3,2,1,0:T(2,128)}), f32[128,2,2,512]{3,2,1,0:T(2,128)S(1)}, u32[]{:S(2)}, u32[]{:S(2)}) async-start(f32[128,2,2,512]{3,2,1,0:T(2,128)} %reshape.186), calls=%async_computation | async-start | bytes 2097152 | tf_op jit(solution)/shard_map/all_to_all | solution.py:146
  39.8 1.0 %fusion.20 = f32[512,128]{0,1:T(8,128)S(1)} fusion(), kind=kLoop, calls=%fused_computation.33 | loop fusion | flops 1048576 | bytes 262144 | tf_op jit(solution)/shard_map/neg | solution.py:110
  40.8 1.1 %sine_multiply_fusion = (f32[512,128]{0,1:T(8,128)S(1)}, f32[512,128]{0,1:T(8,128)S(1)}) fusion(), kind=kLoop, calls=%fused_computation.20 | loop fusion | flops 1048576 | bytes 524288 | tf_op jit(solution)/shard_map/mul | solution.py:108
  41.9 0.1 maximum_maximum_fusion
  42.0 0.3 fusion.31
  42.4 17.2 %all-to-all-done = f32[128,2,2,512]{3,2,1,0:T(2,128)S(1)} async-done(((f32[128,2,2,512]{3,2,1,0:T(2,128)}), f32[128,2,2,512]{3,2,1,0:T(2,128)S(1)}, u32[]{:S(2)}, u32[]{:S(2)}) %all-to-all-start) | async-done | bytes 1048608 | tf_op jit(solution)/shard_map/all_to_all | solution.py:146
  59.6 0.4 reduce_sum.9
  59.9 0.1 reshape.188
  60.1 0.1 reshape.189
  60.2 0.1 multiply_add_fusion
  60.2 1.2 %fusion.8 = f32[32,4,2,128]{3,0,2,1:T(8,128)S(1)} fusion(f32[2,128,1024,1]{2,1,0,3:T(8,128)S(1)} %bitcast.32, f32[32,1,4,512]{3,0,2,1:T(8,128)S(1)} %get-tuple-element.10, f32[32,1,4,512]{3,0,2,1:T(8,128)S(1)} %get-tuple-element.9), kind=kOutput, calls=%fused_computation.11 | convolution fusion | flops 402784256 | bytes 1703936 | tf_op jit(solution)/shard_map/dot_general | solution.py:171
  61.4 0.1 copy.18
  61.5 0.9 %broadcast_in_dim.2 = f32[32,4,4,2,128]{4,3,2,1,0:T(2,128)} broadcast(f32[32,4,2,128]{3,2,1,0:T(2,128)S(1)} %copy.18), dimensions={0,2,3,4} | broadcast | bytes 655360 | tf_op jit(solution)/shard_map/broadcast_in_dim | solution.py:174
  62.5 3.6 %all-to-all-start.1 = ((f32[128,4,2,128]{3,2,1,0:T(2,128)}), f32[128,4,2,128]{3,2,1,0:T(2,128)S(1)}, u32[]{:S(2)}, u32[]{:S(2)}) async-start(f32[128,4,2,128]{3,2,1,0:T(2,128)} %bitcast.12), calls=%async_computation.1 | async-start | bytes 1048576 | tf_op jit(solution)/shard_map/all_to_all | solution.py:177
  66.1 0.0 copy-start.1
  66.1 0.6 constant_dynamic-slice_fusion
  67.4 0.3 cosine_multiply_fusion.2
  67.8 12.7 %all-to-all-done.1 = f32[128,4,2,128]{3,2,1,0:T(2,128)S(1)} async-done(((f32[128,4,2,128]{3,2,1,0:T(2,128)}), f32[128,4,2,128]{3,2,1,0:T(2,128)S(1)}, u32[]{:S(2)}, u32[]{:S(2)}) %all-to-all-start.1) | async-done | bytes 524320 | tf_op jit(solution)/shard_map/all_to_all | solution.py:177
  80.4 0.4 fusion.59
  80.8 0.6 fusion
  81.5 0.6 broadcast_multiply_fusion
  (14 shorter events, 0.1 us)
Async XLA Ops:
  22.0 5.3 %copy-start = (f32[512,1024]{1,0:T(8,128)S(1)}, f32[512,1024]{1,0:T(8,128)}, u32[]{:S(2)}) copy-start(f32[512,1024]{1,0:T(8,128)} %shard_map.82) | copy-start | bytes 6291460
  23.5 3.8 %collective-permute-start = (f32[256,1024]{1,0:T(8,128)S(1)}, f32[256,1024]{1,0:T(8,128)S(1)}, u32[]{:S(2)}, u32[]{:S(2)}) collective-permute-start(f32[256,1024]{1,0:T(8,128)S(1)} %slice.29), channel_id=1, source_target_pairs={{0,4},{4,0},{8,12},{12,8},{16,20},{20,16},{24,28},{28,24},{32,36},... | collective-permute-start | bytes 3145736 | tf_op jit(solution)/shard_map/ppermute | solution.py:144
  29.4 12.6 %copy-start.2 = (s32[32,2]{0,1:T(2,128)S(1)}, s32[32,2]{0,1:T(2,128)}, u32[]{:S(2)}) copy-start(s32[32,2]{0,1:T(2,128)} %param.14) | copy-start | bytes 772
  29.4 30.2 %all-to-all-start = ((f32[128,2,2,512]{3,2,1,0:T(2,128)}), f32[128,2,2,512]{3,2,1,0:T(2,128)S(1)}, u32[]{:S(2)}, u32[]{:S(2)}) async-start(f32[128,2,2,512]{3,2,1,0:T(2,128)} %reshape.186), calls=%async_computation | async-start | bytes 2097152 | tf_op jit(solution)/shard_map/all_to_all | solution.py:146
  62.5 17.9 %all-to-all-start.1 = ((f32[128,4,2,128]{3,2,1,0:T(2,128)}), f32[128,4,2,128]{3,2,1,0:T(2,128)S(1)}, u32[]{:S(2)}, u32[]{:S(2)}) async-start(f32[128,4,2,128]{3,2,1,0:T(2,128)} %bitcast.12), calls=%async_computation.1 | async-start | bytes 1048576 | tf_op jit(solution)/shard_map/all_to_all | solution.py:177
  66.1 15.3 %copy-start.1 = (f32[1,32,128]{2,1,0:T(8,128)S(1)}, f32[1,32,128]{2,1,0:T(8,128)}, u32[]{:S(2)}) copy-start(f32[1,32,128]{2,1,0:T(8,128)} %param.15) | copy-start | bytes 49156

commit v16 on v10

--- a/solution.py
+++ b/solution.py
@@ -63,7 +63,7 @@
         )
         return carry
 
-    lax.fori_loop(0, step, one_block, 0)
+    lax.fori_loop(0, step, one_block, 0, unroll=32)
 
 
 def make_phased_grid(vis_coords, vis_values, live, local, tile_id):

time: 113 us -> 81.4 us (0.72)
  Pallas kernels: 49.4 us -> 17.4 us
    pallas_call x1, Pallas kernels: 49.4 us -> 17.4 us  [make_phased_grid(): pl.pallas_call(patch_kernel, grid_spec=pltpu.PrefetchScalarGridSpec(num_s...]
  transfers between devices with their start and end apart: 3 -> 3, of which waited for: 3 -> 3; matrix products, arithmetic and copies ran while one was open for 3% -> 4% of each run, Pallas kernels for 0% -> 0%
where the time goes in v16:
time: 81.4 us; the launch traced here: 81.1 us
  waiting for transfers between devices  32.2 us (40%)
  Pallas kernels  17.4 us (21%)
  starting transfers between devices  15.6 us (19%)
  local copies, waits for them, and re-layouts  6.54 us (8%)
  other arithmetic  6.23 us (8%)
  matrix products  1.77 us (2%)
  between operations  1.51 us (2%)
    pallas_call x1, Pallas kernels, make_phased_grid(): pl.pallas_call(patch_kernel, grid_spec=pltpu.PrefetchScalarGridSpec(num_s...  17.4 us
    all_to_all x1, waiting for transfers between devices, body(): lax.all_to_all(chip_half.reshape(devices, half_chunk, 2, SG), ('tm', 'sub...  17.2 us
    all_to_all x1, waiting for transfers between devices, body(): lax.all_to_all(windows, ('tm', 'sub'), split_axis=0, concat_axis=0, tiled...  12.7 us
    all_to_all x1, starting transfers between devices, body(): lax.all_to_all(chip_half.reshape(devices, half_chunk, 2, SG), ('tm', 'sub...  10.5 us
    all_to_all x1, starting transfers between devices, body(): lax.all_to_all(windows, ('tm', 'sub'), split_axis=0, concat_axis=0, tiled...  3.63 us
    ppermute x1, waiting for transfers between devices, body(): chip_half = grid[:SG // 2] + lax.ppermute(grid[SG // 2:], 'tm', pair)  2.29 us
    reshape x1, local copies, waits for them, and re-layouts, body(): chip_half.reshape(devices, half_chunk, 2, SG)  1.86 us
  transfers between devices with their start and end apart: 3, of which 3 were waited for; matrix products, arithmetic and copies ran while one was open for 4% of the time, Pallas kernels for 0%

profile of v16, /device:TPU:1, one launch (start us, length us, event | category | flops | bytes accessed | tf_op | source)
XLA Modules:
  0.0 81.1 jit_solution(18042706154523564039)
XLA Ops:
  0.0 0.7 fusion.33
  0.7 0.1 copy.16
  1.4 0.3 fusion.58
  1.7 1.2 %fusion.50.place_ref = s32[128]{0:T(128)} fusion(s32[128,1]{0,1:T(1,128)} %param.10, s32[128]{0:T(128)} %param.12, s32[]{:T(128)S(6)} %mul.277), kind=kLoop, calls=%fused_computation.98 | loop fusion | flops 5888 | bytes 1540 | tf_op jit(solution)/shard_map/add | solution.py:140
  2.9 0.8 concatenate.30.phase_ref
  3.7 17.4 %shard_map.82 = f32[512,1024]{1,0:T(8,128)} custom-call(s32[128]{0:T(128)} %fusion.50.place_ref, f32[128,2,1024]{2,1,0:T(2,128)} %coords_ref.1, f32[128,2,1024]{2,1,0:T(2,128)} %values_ref.1, f32[128,256]{1,0:T(8,128)} %concatenate.30.phase_ref), custom_call_target="tpu_custom_call" | custom-call | flops 4294967296 | bytes 4194304 | tf_op jit(solution)/shard_map/pallas_call | solution.py:81
  21.1 1.5 %slice.29 = f32[256,1024]{1,0:T(8,128)S(1)} slice(f32[512,1024]{1,0:T(8,128)} %shard_map.82), slice={[256:512], [0:1024]} | slice | bytes 2097152 | tf_op jit(solution)/shard_map/slice | solution.py:144
  22.6 1.5 %collective-permute-start = (f32[256,1024]{1,0:T(8,128)S(1)}, f32[256,1024]{1,0:T(8,128)S(1)}, u32[]{:S(2)}, u32[]{:S(2)}) collective-permute-start(f32[256,1024]{1,0:T(8,128)S(1)} %slice.29), channel_id=1, source_target_pairs={{0,4},{4,0},{8,12},{12,8},{16,20},{20,16},{24,28},{28,24},{32,36},... | collective-permute-start | bytes 3145736 | tf_op jit(solution)/shard_map/ppermute | solution.py:144
  24.1 2.3 %collective-permute-done = f32[256,1024]{1,0:T(8,128)S(1)} collective-permute-done((f32[256,1024]{1,0:T(8,128)S(1)}, f32[256,1024]{1,0:T(8,128)S(1)}, u32[]{:S(2)}, u32[]{:S(2)}) %collective-permute-start) | collective-permute-done | bytes 1048608 | tf_op jit(solution)/shard_map/ppermute | solution.py:144
  26.3 0.2 slice_add_fusion
  26.5 1.9 %reshape.186 = f32[128,2,2,512]{3,2,1,0:T(2,128)} reshape(f32[256,1024]{1,0:T(8,128)S(1)} %slice_add_fusion) | data formatting | bytes 2097152 | tf_op jit(solution)/shard_map/reshape | solution.py:147
  28.4 10.5 %all-to-all-start = ((f32[128,2,2,512]{3,2,1,0:T(2,128)}), f32[128,2,2,512]{3,2,1,0:T(2,128)S(1)}, u32[]{:S(2)}, u32[]{:S(2)}) async-start(f32[128,2,2,512]{3,2,1,0:T(2,128)} %reshape.186), calls=%async_computation | async-start | bytes 2097152 | tf_op jit(solution)/shard_map/all_to_all | solution.py:146
  38.9 1.0 %fusion.20 = f32[512,128]{0,1:T(8,128)S(1)} fusion(), kind=kLoop, calls=%fused_computation.33 | loop fusion | flops 1048576 | bytes 262144 | tf_op jit(solution)/shard_map/neg | solution.py:110
  39.8 1.1 %sine_multiply_fusion = (f32[512,128]{0,1:T(8,128)S(1)}, f32[512,128]{0,1:T(8,128)S(1)}) fusion(), kind=kLoop, calls=%fused_computation.20 | loop fusion | flops 1048576 | bytes 524288 | tf_op jit(solution)/shard_map/mul | solution.py:108
  40.9 0.1 maximum_maximum_fusion
  41.0 0.3 fusion.31
  41.4 17.2 %all-to-all-done = f32[128,2,2,512]{3,2,1,0:T(2,128)S(1)} async-done(((f32[128,2,2,512]{3,2,1,0:T(2,128)}), f32[128,2,2,512]{3,2,1,0:T(2,128)S(1)}, u32[]{:S(2)}, u32[]{:S(2)}) %all-to-all-start) | async-done | bytes 1048608 | tf_op jit(solution)/shard_map/all_to_all | solution.py:146
  58.6 0.4 reduce_sum.9
  59.0 0.1 reshape.188
  59.1 0.1 reshape.189
  59.2 0.1 multiply_add_fusion
  59.3 1.2 %fusion.8 = f32[32,4,2,128]{3,0,2,1:T(8,128)S(1)} fusion(f32[2,128,1024,1]{2,1,0,3:T(8,128)S(1)} %bitcast.32, f32[32,1,4,512]{3,0,2,1:T(8,128)S(1)} %get-tuple-element.10, f32[32,1,4,512]{3,0,2,1:T(8,128)S(1)} %get-tuple-element.9), kind=kOutput, calls=%fused_computation.11 | convolution fusion | flops 402784256 | bytes 1703936 | tf_op jit(solution)/shard_map/dot_general | solution.py:171
  60.5 0.1 copy.18
  60.6 0.9 %broadcast_in_dim.2 = f32[32,4,4,2,128]{4,3,2,1,0:T(2,128)} broadcast(f32[32,4,2,128]{3,2,1,0:T(2,128)S(1)} %copy.18), dimensions={0,2,3,4} | broadcast | bytes 655360 | tf_op jit(solution)/shard_map/broadcast_in_dim | solution.py:174
  61.5 3.6 %all-to-all-start.1 = ((f32[128,4,2,128]{3,2,1,0:T(2,128)}), f32[128,4,2,128]{3,2,1,0:T(2,128)S(1)}, u32[]{:S(2)}, u32[]{:S(2)}) async-start(f32[128,4,2,128]{3,2,1,0:T(2,128)} %bitcast.12), calls=%async_computation.1 | async-start | bytes 1048576 | tf_op jit(solution)/shard_map/all_to_all | solution.py:177
  65.2 0.0 copy-start.1
  65.2 0.6 constant_dynamic-slice_fusion
  66.4 0.3 cosine_multiply_fusion.2
  66.8 12.7 %all-to-all-done.1 = f32[128,4,2,128]{3,2,1,0:T(2,128)S(1)} async-done(((f32[128,4,2,128]{3,2,1,0:T(2,128)}), f32[128,4,2,128]{3,2,1,0:T(2,128)S(1)}, u32[]{:S(2)}, u32[]{:S(2)}) %all-to-all-start.1) | async-done | bytes 524320 | tf_op jit(solution)/shard_map/all_to_all | solution.py:177
  79.4 0.4 fusion.59
  79.9 0.6 fusion
  80.5 0.6 broadcast_multiply_fusion
  (14 shorter events, 0.1 us)
Async XLA Ops:
  21.1 5.3 %copy-start = (f32[512,1024]{1,0:T(8,128)S(1)}, f32[512,1024]{1,0:T(8,128)}, u32[]{:S(2)}) copy-start(f32[512,1024]{1,0:T(8,128)} %shard_map.82) | copy-start | bytes 6291460
  22.6 3.8 %collective-permute-start = (f32[256,1024]{1,0:T(8,128)S(1)}, f32[256,1024]{1,0:T(8,128)S(1)}, u32[]{:S(2)}, u32[]{:S(2)}) collective-permute-start(f32[256,1024]{1,0:T(8,128)S(1)} %slice.29), channel_id=1, source_target_pairs={{0,4},{4,0},{8,12},{12,8},{16,20},{20,16},{24,28},{28,24},{32,36},... | collective-permute-start | bytes 3145736 | tf_op jit(solution)/shard_map/ppermute | solution.py:144
  28.4 12.6 %copy-start.2 = (s32[32,2]{0,1:T(2,128)S(1)}, s32[32,2]{0,1:T(2,128)}, u32[]{:S(2)}) copy-start(s32[32,2]{0,1:T(2,128)} %param.14) | copy-start | bytes 772
  28.4 30.2 %all-to-all-start = ((f32[128,2,2,512]{3,2,1,0:T(2,128)}), f32[128,2,2,512]{3,2,1,0:T(2,128)S(1)}, u32[]{:S(2)}, u32[]{:S(2)}) async-start(f32[128,2,2,512]{3,2,1,0:T(2,128)} %reshape.186), calls=%async_computation | async-start | bytes 2097152 | tf_op jit(solution)/shard_map/all_to_all | solution.py:146
  61.5 17.9 %all-to-all-start.1 = ((f32[128,4,2,128]{3,2,1,0:T(2,128)}), f32[128,4,2,128]{3,2,1,0:T(2,128)S(1)}, u32[]{:S(2)}, u32[]{:S(2)}) async-start(f32[128,4,2,128]{3,2,1,0:T(2,128)} %bitcast.12), calls=%async_computation.1 | async-start | bytes 1048576 | tf_op jit(solution)/shard_map/all_to_all | solution.py:177
  65.2 15.3 %copy-start.1 = (f32[1,32,128]{2,1,0:T(8,128)S(1)}, f32[1,32,128]{2,1,0:T(8,128)}, u32[]{:S(2)}) copy-start(f32[1,32,128]{2,1,0:T(8,128)} %param.15) | copy-start | bytes 49156

commit v17 on v16

--- a/solution.py
+++ b/solution.py
@@ -63,12 +63,12 @@
         )
         return carry
 
-    lax.fori_loop(0, step, one_block, 0, unroll=32)
+    lax.fori_loop(0, step, one_block, 0, unroll=64)
 
 
 def make_phased_grid(vis_coords, vis_values, live, local, tile_id):
     count = vis_coords.shape[0]
-    step = 32
+    step = 64
     phase = (jnp.arange(PATCH, dtype=jnp.int32)[None, :] * local[:, None]) % SG_PER
     angle = phase.astype(jnp.float32) * (2.0 * math.pi / SG_PER)
     keep = live.astype(jnp.float32)[:, None]

time: 81.4 us -> 81.1 us (level)
  no operation moved by 1% of the time
where the time goes in v17:
time: 81.1 us; the launch traced here: 80.8 us
  waiting for transfers between devices  32.2 us (40%)
  Pallas kernels  17 us (21%)
  starting transfers between devices  15.6 us (19%)
  local copies, waits for them, and re-layouts  6.54 us (8%)
  other arithmetic  6.23 us (8%)
  matrix products  1.77 us (2%)
  between operations  1.51 us (2%)
    all_to_all x1, waiting for transfers between devices, body(): lax.all_to_all(chip_half.reshape(devices, half_chunk, 2, SG), ('tm', 'sub...  17.2 us
    pallas_call x1, Pallas kernels, make_phased_grid(): pl.pallas_call(patch_kernel, grid_spec=pltpu.PrefetchScalarGridSpec(num_s...  17 us
    all_to_all x1, waiting for transfers between devices, body(): lax.all_to_all(windows, ('tm', 'sub'), split_axis=0, concat_axis=0, tiled...  12.7 us
    all_to_all x1, starting transfers between devices, body(): lax.all_to_all(chip_half.reshape(devices, half_chunk, 2, SG), ('tm', 'sub...  10.5 us
    all_to_all x1, starting transfers between devices, body(): lax.all_to_all(windows, ('tm', 'sub'), split_axis=0, concat_axis=0, tiled...  3.63 us
    ppermute x1, waiting for transfers between devices, body(): chip_half = grid[:SG // 2] + lax.ppermute(grid[SG // 2:], 'tm', pair)  2.29 us
    reshape x1, local copies, waits for them, and re-layouts, body(): chip_half.reshape(devices, half_chunk, 2, SG)  1.86 us
  transfers between devices with their start and end apart: 3, of which 3 were waited for; matrix products, arithmetic and copies ran while one was open for 4% of the time, Pallas kernels for 0%

profile of v17, /device:TPU:1, one launch (start us, length us, event | category | flops | bytes accessed | tf_op | source)
XLA Modules:
  0.0 80.8 jit_solution(7056513871770539770)
XLA Ops:
  0.0 0.7 fusion.33
  0.7 0.1 copy.16
  1.4 0.3 fusion.58
  1.7 1.2 %fusion.50.place_ref = s32[128]{0:T(128)} fusion(s32[128,1]{0,1:T(1,128)} %param.10, s32[128]{0:T(128)} %param.12, s32[]{:T(128)S(6)} %mul.277), kind=kLoop, calls=%fused_computation.98 | loop fusion | flops 5888 | bytes 1540 | tf_op jit(solution)/shard_map/add | solution.py:140
  2.9 0.8 %concatenate.30.phase_ref = f32[128,256]{1,0:T(8,128)} concatenate(f32[128,32]{1,0:T(8,128)S(1)} %get-tuple-element.11, f32[128,32]{1,0:T(8,128)S(1)} %get-tuple-element.11, f32[128,32]{1,0:T(8,128)S(1)} %get-tuple-element.11, f32[128,32]{1,0:T(8,128)S(1)} %get-tuple-element.11, f32[128,32]{1,0:T(8,128)S(1)} %get-tuple-element.6, f32[128,32]{1,0:T(8,128)S(1)} %get-tuple-element.5, ...), dimensions={1} | concatenate | bytes 262144 | tf_op jit(solution)/shard_map/concatenate | solution.py:77
  3.7 17.0 %shard_map.82 = f32[512,1024]{1,0:T(8,128)} custom-call(s32[128]{0:T(128)} %fusion.50.place_ref, f32[128,2,1024]{2,1,0:T(2,128)} %coords_ref.1, f32[128,2,1024]{2,1,0:T(2,128)} %values_ref.1, f32[128,256]{1,0:T(8,128)} %concatenate.30.phase_ref), custom_call_target="tpu_custom_call" | custom-call | flops 4294967296 | bytes 4194304 | tf_op jit(solution)/shard_map/pallas_call | solution.py:81
  20.7 1.5 %slice.29 = f32[256,1024]{1,0:T(8,128)S(1)} slice(f32[512,1024]{1,0:T(8,128)} %shard_map.82), slice={[256:512], [0:1024]} | slice | bytes 2097152 | tf_op jit(solution)/shard_map/slice | solution.py:144
  22.2 1.5 %collective-permute-start = (f32[256,1024]{1,0:T(8,128)S(1)}, f32[256,1024]{1,0:T(8,128)S(1)}, u32[]{:S(2)}, u32[]{:S(2)}) collective-permute-start(f32[256,1024]{1,0:T(8,128)S(1)} %slice.29), channel_id=1, source_target_pairs={{0,4},{4,0},{8,12},{12,8},{16,20},{20,16},{24,28},{28,24},{32,36},... | collective-permute-start | bytes 3145736 | tf_op jit(solution)/shard_map/ppermute | solution.py:144
  23.7 2.3 %collective-permute-done = f32[256,1024]{1,0:T(8,128)S(1)} collective-permute-done((f32[256,1024]{1,0:T(8,128)S(1)}, f32[256,1024]{1,0:T(8,128)S(1)}, u32[]{:S(2)}, u32[]{:S(2)}) %collective-permute-start) | collective-permute-done | bytes 1048608 | tf_op jit(solution)/shard_map/ppermute | solution.py:144
  26.0 0.2 slice_add_fusion
  26.2 1.9 %reshape.186 = f32[128,2,2,512]{3,2,1,0:T(2,128)} reshape(f32[256,1024]{1,0:T(8,128)S(1)} %slice_add_fusion) | data formatting | bytes 2097152 | tf_op jit(solution)/shard_map/reshape | solution.py:147
  28.1 10.5 %all-to-all-start = ((f32[128,2,2,512]{3,2,1,0:T(2,128)}), f32[128,2,2,512]{3,2,1,0:T(2,128)S(1)}, u32[]{:S(2)}, u32[]{:S(2)}) async-start(f32[128,2,2,512]{3,2,1,0:T(2,128)} %reshape.186), calls=%async_computation | async-start | bytes 2097152 | tf_op jit(solution)/shard_map/all_to_all | solution.py:146
  38.5 1.0 %fusion.20 = f32[512,128]{0,1:T(8,128)S(1)} fusion(), kind=kLoop, calls=%fused_computation.33 | loop fusion | flops 1048576 | bytes 262144 | tf_op jit(solution)/shard_map/neg | solution.py:110
  39.5 1.1 %sine_multiply_fusion = (f32[512,128]{0,1:T(8,128)S(1)}, f32[512,128]{0,1:T(8,128)S(1)}) fusion(), kind=kLoop, calls=%fused_computation.20 | loop fusion | flops 1048576 | bytes 524288 | tf_op jit(solution)/shard_map/mul | solution.py:108
  40.6 0.1 maximum_maximum_fusion
  40.7 0.3 fusion.31
  41.1 17.2 %all-to-all-done = f32[128,2,2,512]{3,2,1,0:T(2,128)S(1)} async-done(((f32[128,2,2,512]{3,2,1,0:T(2,128)}), f32[128,2,2,512]{3,2,1,0:T(2,128)S(1)}, u32[]{:S(2)}, u32[]{:S(2)}) %all-to-all-start) | async-done | bytes 1048608 | tf_op jit(solution)/shard_map/all_to_all | solution.py:146
  58.3 0.4 reduce_sum.9
  58.6 0.1 reshape.188
  58.8 0.1 reshape.189
  58.9 0.1 multiply_add_fusion
  59.0 1.2 %fusion.8 = f32[32,4,2,128]{3,0,2,1:T(8,128)S(1)} fusion(f32[2,128,1024,1]{2,1,0,3:T(8,128)S(1)} %bitcast.32, f32[32,1,4,512]{3,0,2,1:T(8,128)S(1)} %get-tuple-element.10, f32[32,1,4,512]{3,0,2,1:T(8,128)S(1)} %get-tuple-element.9), kind=kOutput, calls=%fused_computation.11 | convolution fusion | flops 402784256 | bytes 1703936 | tf_op jit(solution)/shard_map/dot_general | solution.py:171
  60.1 0.1 copy.18
  60.3 0.9 %broadcast_in_dim.2 = f32[32,4,4,2,128]{4,3,2,1,0:T(2,128)} broadcast(f32[32,4,2,128]{3,2,1,0:T(2,128)S(1)} %copy.18), dimensions={0,2,3,4} | broadcast | bytes 655360 | tf_op jit(solution)/shard_map/broadcast_in_dim | solution.py:174
  61.2 3.6 %all-to-all-start.1 = ((f32[128,4,2,128]{3,2,1,0:T(2,128)}), f32[128,4,2,128]{3,2,1,0:T(2,128)S(1)}, u32[]{:S(2)}, u32[]{:S(2)}) async-start(f32[128,4,2,128]{3,2,1,0:T(2,128)} %bitcast.12), calls=%async_computation.1 | async-start | bytes 1048576 | tf_op jit(solution)/shard_map/all_to_all | solution.py:177
  64.8 0.0 copy-start.1
  64.8 0.6 constant_dynamic-slice_fusion
  66.1 0.3 cosine_multiply_fusion.2
  66.5 12.7 %all-to-all-done.1 = f32[128,4,2,128]{3,2,1,0:T(2,128)S(1)} async-done(((f32[128,4,2,128]{3,2,1,0:T(2,128)}), f32[128,4,2,128]{3,2,1,0:T(2,128)S(1)}, u32[]{:S(2)}, u32[]{:S(2)}) %all-to-all-start.1) | async-done | bytes 524320 | tf_op jit(solution)/shard_map/all_to_all | solution.py:177
  79.1 0.4 fusion.59
  79.5 0.6 fusion
  80.2 0.6 broadcast_multiply_fusion
  (14 shorter events, 0.1 us)
Async XLA Ops:
  20.7 5.3 %copy-start = (f32[512,1024]{1,0:T(8,128)S(1)}, f32[512,1024]{1,0:T(8,128)}, u32[]{:S(2)}) copy-start(f32[512,1024]{1,0:T(8,128)} %shard_map.82) | copy-start | bytes 6291460
  22.2 3.8 %collective-permute-start = (f32[256,1024]{1,0:T(8,128)S(1)}, f32[256,1024]{1,0:T(8,128)S(1)}, u32[]{:S(2)}, u32[]{:S(2)}) collective-permute-start(f32[256,1024]{1,0:T(8,128)S(1)} %slice.29), channel_id=1, source_target_pairs={{0,4},{4,0},{8,12},{12,8},{16,20},{20,16},{24,28},{28,24},{32,36},... | collective-permute-start | bytes 3145736 | tf_op jit(solution)/shard_map/ppermute | solution.py:144
  28.1 12.6 %copy-start.2 = (s32[32,2]{0,1:T(2,128)S(1)}, s32[32,2]{0,1:T(2,128)}, u32[]{:S(2)}) copy-start(s32[32,2]{0,1:T(2,128)} %param.14) | copy-start | bytes 772
  28.1 30.2 %all-to-all-start = ((f32[128,2,2,512]{3,2,1,0:T(2,128)}), f32[128,2,2,512]{3,2,1,0:T(2,128)S(1)}, u32[]{:S(2)}, u32[]{:S(2)}) async-start(f32[128,2,2,512]{3,2,1,0:T(2,128)} %reshape.186), calls=%async_computation | async-start | bytes 2097152 | tf_op jit(solution)/shard_map/all_to_all | solution.py:146
  61.2 17.9 %all-to-all-start.1 = ((f32[128,4,2,128]{3,2,1,0:T(2,128)}), f32[128,4,2,128]{3,2,1,0:T(2,128)S(1)}, u32[]{:S(2)}, u32[]{:S(2)}) async-start(f32[128,4,2,128]{3,2,1,0:T(2,128)} %bitcast.12), calls=%async_computation.1 | async-start | bytes 1048576 | tf_op jit(solution)/shard_map/all_to_all | solution.py:177
  64.8 15.3 %copy-start.1 = (f32[1,32,128]{2,1,0:T(8,128)S(1)}, f32[1,32,128]{2,1,0:T(8,128)}, u32[]{:S(2)}) copy-start(f32[1,32,128]{2,1,0:T(8,128)} %param.15) | copy-start | bytes 49156

commit v18 on v16

--- a/solution.py
+++ b/solution.py
@@ -1,6 +1,8 @@
+import functools
 import math
 
 import jax
+import numpy as np
 import jax.numpy as jnp
 from jax import lax
 from jax.experimental import pallas as pl
@@ -24,7 +26,7 @@
     return jnp.concatenate([high, low], axis=0)
 
 
-def patch_kernel(place_ref, coords_ref, values_ref, phase_ref, out_ref):
+def patch_kernel(n_sub, dest_ref, tile_ref, local_ref, count_ref, coords_ref, values_ref, phase_ref, out_ref):
     step = coords_ref.shape[0]
     width = 2 * PATCH
     cells = lax.broadcasted_iota(jnp.int32, (PATCH, 1), 0).astype(jnp.float32)
@@ -51,11 +53,14 @@
         both = both + pltpu.roll(both, width, 1)
         plain = both[:PATCH] + both[PATCH:]
         swapped = pltpu.roll(plain, PATCH, 1)
-        phase = phase_ref[pl.ds(i, 1), :]
+        block = pl.program_id(0) * step + i
+        phase = phase_ref[pl.ds(local_ref[block], 1), :]
+        phase = jnp.where(block < count_ref[0], phase, 0.0)
         phased = plain * phase[:, : 2 * width] + swapped * phase[:, 2 * width :]
-        tile = place_ref[pl.program_id(0) * step + i]
-        row_tile = tile // (SG // PATCH)
-        col_tile = tile % (SG // PATCH)
+        col_tiles = SG // PATCH
+        row_tile = (dest_ref[block] % n_sub) * (col_tiles // n_sub) + tile_ref[block] // col_tiles
+        row_tile = (row_tile + (lax.axis_index("tm") % 2) * (col_tiles // 2)) % col_tiles
+        col_tile = tile_ref[block] % col_tiles
         rows = pl.ds(pl.multiple_of(row_tile * PATCH, PATCH), PATCH)
         start = pl.multiple_of((col_tile // 2) * 2 * width, 2 * width)
         out_ref[rows, pl.ds(start, 2 * width)] += jnp.where(
@@ -66,29 +71,31 @@
     lax.fori_loop(0, step, one_block, 0, unroll=32)
 
 
-def make_phased_grid(vis_coords, vis_values, live, local, tile_id):
+def phase_table():
+    b = np.arange(PATCH)
+    rows = []
+    for local in range(SG_PER):
+        angle = ((b * local) % SG_PER) * (2.0 * math.pi / SG_PER)
+        cos_b, sin_b = np.cos(angle), np.sin(angle)
+        rows.append(np.concatenate([cos_b, cos_b, cos_b, cos_b, sin_b, -sin_b, sin_b, -sin_b]))
+    return jnp.asarray(np.stack(rows).astype(np.float32))
+
+
+def make_phased_grid(n_sub, vis_coords, vis_values, block_dest, block_tile, block_local, block_counts):
     count = vis_coords.shape[0]
     step = 32
-    phase = (jnp.arange(PATCH, dtype=jnp.int32)[None, :] * local[:, None]) % SG_PER
-    angle = phase.astype(jnp.float32) * (2.0 * math.pi / SG_PER)
-    keep = live.astype(jnp.float32)[:, None]
-    cos_b = jnp.cos(angle) * keep
-    sin_b = jnp.sin(angle) * keep
-    phases = jnp.concatenate(
-        [cos_b, cos_b, cos_b, cos_b, sin_b, -sin_b, sin_b, -sin_b], axis=1
-    )
-    spec = pl.BlockSpec((step, 2, VIS), lambda i, place: (i, 0, 0))
+    spec = pl.BlockSpec((step, 2, VIS), lambda i, *refs: (i, 0, 0))
     return pl.pallas_call(
-        patch_kernel,
+        functools.partial(patch_kernel, n_sub),
         grid_spec=pltpu.PrefetchScalarGridSpec(
-            num_scalar_prefetch=1,
+            num_scalar_prefetch=4,
             grid=(count // step,),
             in_specs=[
                 spec,
                 spec,
-                pl.BlockSpec((step, 8 * PATCH), lambda i, place: (i, 0)),
+                pl.BlockSpec((SG_PER, 8 * PATCH), lambda i, *refs: (0, 0)),
             ],
-            out_specs=pl.BlockSpec((SG, 2 * SG), lambda i, place: (0, 0)),
+            out_specs=pl.BlockSpec((SG, 2 * SG), lambda i, *refs: (0, 0)),
         ),
         out_shape=jax.ShapeDtypeStruct((SG, 2 * SG), jnp.float32),
         cost_estimate=pl.CostEstimate(
@@ -96,7 +103,7 @@
             transcendentals=count * 2 * PATCH * VIS,
             bytes_accessed=count * 4 * VIS * 4 + SG * SG * 8,
         ),
-    )(tile_id, vis_coords, vis_values, phases)
+    )(block_dest[:, 0], block_tile, block_local, block_counts, vis_coords, vis_values, phase_table())
 
 
 def window_table():
@@ -132,13 +139,10 @@
     chunk = SG // devices
     facet_rows = FS // n_sub
 
-    live = jnp.arange(blocks, dtype=jnp.int32) < block_counts[0]
-    target = block_dest[:, 0]
-    row_tile = (target % n_sub) * band_tiles + block_tile // col_tiles
-    core = lax.axis_index("tm") % 2
-    row_tile = (row_tile + core * (col_tiles // 2)) % col_tiles
-    tile_id = row_tile * col_tiles + block_tile % col_tiles
-    grid = make_phased_grid(vis_coords, vis_values, live, block_local, tile_id)
+    grid = make_phased_grid(
+        n_sub,
+        vis_coords, vis_values, block_dest, block_tile, block_local, block_counts
+    )
 
     pair = [(i, i ^ 1) for i in range(n_tm)]
     chip_half = grid[: SG // 2] + lax.ppermute(grid[SG // 2 :], "tm", pair)

time: 81.4 us -> 78.3 us (0.962)
  other arithmetic: 6.23 us -> 4.09 us
  local copies, waits for them, and re-layouts: 6.54 us -> 5.61 us
    add x1 -> x0, other arithmetic: 1.21 us -> none  [body(): tile_id = row_tile * col_tiles + block_tile % col_tiles]
where the time goes in v18:
time: 78.3 us; the launch traced here: 78.1 us
  waiting for transfers between devices  32.2 us (41%)
  Pallas kernels  17.4 us (22%)
  starting transfers between devices  15.6 us (20%)
  local copies, waits for them, and re-layouts  5.61 us (7%)
  other arithmetic  4.09 us (5%)
  matrix products  1.77 us (2%)
  between operations  1.49 us (2%)
    pallas_call x1, Pallas kernels, make_phased_grid(): pl.pallas_call(functools.partial(patch_kernel, n_sub), grid_spec=pltpu.Pr...  17.4 us
    all_to_all x1, waiting for transfers between devices, body(): lax.all_to_all(chip_half.reshape(devices, half_chunk, 2, SG), ('tm', 'sub...  17.2 us
    all_to_all x1, waiting for transfers between devices, body(): lax.all_to_all(windows, ('tm', 'sub'), split_axis=0, concat_axis=0, tiled...  12.7 us
    all_to_all x1, starting transfers between devices, body(): lax.all_to_all(chip_half.reshape(devices, half_chunk, 2, SG), ('tm', 'sub...  10.5 us
    all_to_all x1, starting transfers between devices, body(): lax.all_to_all(windows, ('tm', 'sub'), split_axis=0, concat_axis=0, tiled...  3.63 us
    ppermute x1, waiting for transfers between devices, body(): chip_half = grid[:SG // 2] + lax.ppermute(grid[SG // 2:], 'tm', pair)  2.29 us
    reshape x1, local copies, waits for them, and re-layouts, body(): chip_half.reshape(devices, half_chunk, 2, SG)  1.86 us
  transfers between devices with their start and end apart: 3, of which 3 were waited for; matrix products, arithmetic and copies ran while one was open for 4% of the time, Pallas kernels for 0%

profile of v18, /device:TPU:1, one launch (start us, length us, event | category | flops | bytes accessed | tf_op | source)
XLA Modules:
  0.0 78.1 jit_solution(9021596553344384621)
XLA Ops:
  0.7 17.4 %shard_map.91 = f32[512,1024]{1,0:T(8,128)} custom-call(s32[128]{0:T(128)} %bitcast.35, s32[128]{0:T(128)} %tile_ref.1, s32[128]{0:T(128)} %local_ref.1, s32[1]{0:T(128)S(6)} %copy.19.count_ref, f32[128,2,1024]{2,1,0:T(2,128)} %coords_ref.1, f32[128,2,1024]{2,1,0:T(2,128)} %values_ref.1, f32[16,256]{1,0:T(8,128)} %constant.100.clone.phase_ref), custom_call_target="tpu_custom_call" | custom-call | flops 4294967296 | bytes 4194304 | tf_op jit(solution)/shard_map/pallas_call | solution.py:88
  18.0 0.0 copy-start
  18.0 1.5 %slice.29 = f32[256,1024]{1,0:T(8,128)S(1)} slice(f32[512,1024]{1,0:T(8,128)} %shard_map.91), slice={[256:512], [0:1024]} | slice | bytes 2097152 | tf_op jit(solution)/shard_map/slice | solution.py:148
  19.5 1.5 %collective-permute-start = (f32[256,1024]{1,0:T(8,128)S(1)}, f32[256,1024]{1,0:T(8,128)S(1)}, u32[]{:S(2)}, u32[]{:S(2)}) collective-permute-start(f32[256,1024]{1,0:T(8,128)S(1)} %slice.29), channel_id=1, source_target_pairs={{0,4},{4,0},{8,12},{12,8},{16,20},{20,16},{24,28},{28,24},{32,36},... | collective-permute-start | bytes 3145736 | tf_op jit(solution)/shard_map/ppermute | solution.py:148
  21.0 2.3 %collective-permute-done = f32[256,1024]{1,0:T(8,128)S(1)} collective-permute-done((f32[256,1024]{1,0:T(8,128)S(1)}, f32[256,1024]{1,0:T(8,128)S(1)}, u32[]{:S(2)}, u32[]{:S(2)}) %collective-permute-start) | collective-permute-done | bytes 1048608 | tf_op jit(solution)/shard_map/ppermute | solution.py:148
  23.3 0.0 copy-done
  23.3 0.2 slice_add_fusion
  23.5 1.9 %reshape.180 = f32[128,2,2,512]{3,2,1,0:T(2,128)} reshape(f32[256,1024]{1,0:T(8,128)S(1)} %slice_add_fusion) | data formatting | bytes 2097152 | tf_op jit(solution)/shard_map/reshape | solution.py:151
  25.3 0.0 copy-start.2
  25.3 10.5 %all-to-all-start = ((f32[128,2,2,512]{3,2,1,0:T(2,128)}), f32[128,2,2,512]{3,2,1,0:T(2,128)S(1)}, u32[]{:S(2)}, u32[]{:S(2)}) async-start(f32[128,2,2,512]{3,2,1,0:T(2,128)} %reshape.180), calls=%async_computation | async-start | bytes 2097152 | tf_op jit(solution)/shard_map/all_to_all | solution.py:150
  35.8 1.0 %fusion.20 = f32[512,128]{0,1:T(8,128)S(1)} fusion(), kind=kLoop, calls=%fused_computation.33 | loop fusion | flops 1048576 | bytes 262144 | tf_op jit(solution)/shard_map/neg | solution.py:117
  36.8 1.1 %sine_multiply_fusion = (f32[512,128]{0,1:T(8,128)S(1)}, f32[512,128]{0,1:T(8,128)S(1)}) fusion(), kind=kLoop, calls=%fused_computation.20 | loop fusion | flops 1048576 | bytes 524288 | tf_op jit(solution)/shard_map/mul | solution.py:115
  37.8 0.1 maximum_maximum_fusion
  37.9 0.0 copy-done.2
  38.0 0.3 fusion.31
  38.3 17.2 %all-to-all-done = f32[128,2,2,512]{3,2,1,0:T(2,128)S(1)} async-done(((f32[128,2,2,512]{3,2,1,0:T(2,128)}), f32[128,2,2,512]{3,2,1,0:T(2,128)S(1)}, u32[]{:S(2)}, u32[]{:S(2)}) %all-to-all-start) | async-done | bytes 1048608 | tf_op jit(solution)/shard_map/all_to_all | solution.py:150
  55.5 0.4 reduce_sum.9
  55.9 0.1 reshape.182
  56.0 0.1 reshape.183
  56.1 0.1 multiply_add_fusion
  56.2 1.2 %fusion.8 = f32[32,4,2,128]{3,0,2,1:T(8,128)S(1)} fusion(f32[2,128,1024,1]{2,1,0,3:T(8,128)S(1)} %bitcast.27, f32[32,1,4,512]{3,0,2,1:T(8,128)S(1)} %get-tuple-element.8, f32[32,1,4,512]{3,0,2,1:T(8,128)S(1)} %get-tuple-element.7), kind=kOutput, calls=%fused_computation.11 | convolution fusion | flops 402784256 | bytes 1703936 | tf_op jit(solution)/shard_map/dot_general | solution.py:175
  57.4 0.1 copy.15
  57.5 0.9 %broadcast_in_dim.2 = f32[32,4,4,2,128]{4,3,2,1,0:T(2,128)} broadcast(f32[32,4,2,128]{3,2,1,0:T(2,128)S(1)} %copy.15), dimensions={0,2,3,4} | broadcast | bytes 655360 | tf_op jit(solution)/shard_map/broadcast_in_dim | solution.py:178
  58.4 3.6 %all-to-all-start.1 = ((f32[128,4,2,128]{3,2,1,0:T(2,128)}), f32[128,4,2,128]{3,2,1,0:T(2,128)S(1)}, u32[]{:S(2)}, u32[]{:S(2)}) async-start(f32[128,4,2,128]{3,2,1,0:T(2,128)} %bitcast.11), calls=%async_computation.1 | async-start | bytes 1048576 | tf_op jit(solution)/shard_map/all_to_all | solution.py:181
  62.1 0.0 copy-start.1
  62.1 0.6 constant_dynamic-slice_fusion
  63.4 0.3 cosine_multiply_fusion.1
  63.7 12.7 %all-to-all-done.1 = f32[128,4,2,128]{3,2,1,0:T(2,128)S(1)} async-done(((f32[128,4,2,128]{3,2,1,0:T(2,128)}), f32[128,4,2,128]{3,2,1,0:T(2,128)S(1)}, u32[]{:S(2)}, u32[]{:S(2)}) %all-to-all-start.1) | async-done | bytes 524320 | tf_op jit(solution)/shard_map/all_to_all | solution.py:181
  76.4 0.4 fusion.47
  76.8 0.6 fusion
  77.4 0.0 copy-done.1
  77.4 0.6 broadcast_multiply_fusion
  (8 shorter events, 0.1 us)
Async XLA Ops:
  18.0 5.3 %copy-start = (f32[512,1024]{1,0:T(8,128)S(1)}, f32[512,1024]{1,0:T(8,128)}, u32[]{:S(2)}) copy-start(f32[512,1024]{1,0:T(8,128)} %shard_map.91) | copy-start | bytes 6291460
  19.5 3.8 %collective-permute-start = (f32[256,1024]{1,0:T(8,128)S(1)}, f32[256,1024]{1,0:T(8,128)S(1)}, u32[]{:S(2)}, u32[]{:S(2)}) collective-permute-start(f32[256,1024]{1,0:T(8,128)S(1)} %slice.29), channel_id=1, source_target_pairs={{0,4},{4,0},{8,12},{12,8},{16,20},{20,16},{24,28},{28,24},{32,36},... | collective-permute-start | bytes 3145736 | tf_op jit(solution)/shard_map/ppermute | solution.py:148
  25.3 12.6 %copy-start.2 = (s32[32,2]{0,1:T(2,128)S(1)}, s32[32,2]{0,1:T(2,128)}, u32[]{:S(2)}) copy-start(s32[32,2]{0,1:T(2,128)} %param.15) | copy-start | bytes 772
  25.3 30.2 %all-to-all-start = ((f32[128,2,2,512]{3,2,1,0:T(2,128)}), f32[128,2,2,512]{3,2,1,0:T(2,128)S(1)}, u32[]{:S(2)}, u32[]{:S(2)}) async-start(f32[128,2,2,512]{3,2,1,0:T(2,128)} %reshape.180), calls=%async_computation | async-start | bytes 2097152 | tf_op jit(solution)/shard_map/all_to_all | solution.py:150
  58.4 17.9 %all-to-all-start.1 = ((f32[128,4,2,128]{3,2,1,0:T(2,128)}), f32[128,4,2,128]{3,2,1,0:T(2,128)S(1)}, u32[]{:S(2)}, u32[]{:S(2)}) async-start(f32[128,4,2,128]{3,2,1,0:T(2,128)} %bitcast.11), calls=%async_computation.1 | async-start | bytes 1048576 | tf_op jit(solution)/shard_map/all_to_all | solution.py:181
  62.1 15.3 %copy-start.1 = (f32[1,32,128]{2,1,0:T(8,128)S(1)}, f32[1,32,128]{2,1,0:T(8,128)}, u32[]{:S(2)}) copy-start(f32[1,32,128]{2,1,0:T(8,128)} %param.16) | copy-start | bytes 49156
